TPU v7x, 32 devices: a whole 2x2x4 slice. The times are simulated.
32 devices in a mesh: layer: 4 (over y, x), tok: 8 (over z, core).
Axes of the slice: x: 2, y: 2, z: 4, core: 2. Of those that a mesh axis runs over, the one named last changes fastest.
Arguments:
- residual: bfloat16 [4, 1024, 3584], P('layer', 'tok'), may hold values from -6 to 6
- targets: bfloat16 [4, 1024, 3584], P('layer', 'tok'), may hold values from -6 to 6
- block_ids: int32 [4, 1024, 2], P(None, 'tok'), may hold values from 0 to 127, all different within a row; in each aligned block of 128 rows (0 to 127, 128 to 255, ..., all dimensions but the last counted through in order) at most 4 rows name the same one
- encoder_weight: bfloat16 [4, 3584, 16384], P('layer', None, 'tok'), may hold values from -0.09375 to 0.09375
- encoder_bias: float32 [4, 16384], P('layer', 'tok'), may hold values from -3 to 3
- decoder_weight: bfloat16 [4, 4, 16384, 3584], P('layer', None, 'tok'), may hold values from -0.25 to 0.25
- decoder_bias: float32 [4, 3584], P('layer'), may hold values from -3 to 3
Outputs:
- reconstruction: bfloat16 [4, 1024, 3584], P('layer', 'tok')
- error: float32 [4, 1024], P('layer', 'tok')
Inputs may be any that keep to these rules, and one draw needn't show every extreme that they name: `block_ids`: A token's 2 blocks in a layer are distinct. In each layer, the 128 rows of one device (aligned blocks of tokens) name no block more than 4 times, and some block exactly 4 times.
All inputs are finite; a program needn't handle non-finite values.
Results may differ from a plain program's by a relative error of at most 0.0053.
Values may be sent and summed in bfloat16 or wider, within the bound.
No kernel may reach another device: no remote copies, remote signals or barrier semaphores. Data moves between devices by JAX's collectives and lax.ppermute only.
A program may use at most 192 MiB of HBM per device.

v0:
```python
import jax
import jax.numpy as jnp
from jax import lax
from jax.sharding import PartitionSpec as P

BLOCK = 128


def slot_positions(ids, blocks, capacity):
    flat_ids = ids.reshape(-1)
    onehot = (flat_ids[:, None] == jnp.arange(blocks, dtype=jnp.int32)[None, :]).astype(jnp.int32)
    before = jnp.cumsum(onehot, axis=0) - onehot
    rank_in = jnp.sum(before * onehot, axis=1)
    return flat_ids * capacity + rank_in


def body(residual, targets, block_ids, encoder_weight, encoder_bias, decoder_weight, decoder_bias):
    layer_index = lax.axis_index("layer")
    layers = lax.axis_size("layer")
    tok_count = lax.axis_size("tok")
    tok_rows = residual.shape[1]
    width = residual.shape[2]
    topk = block_ids.shape[2]
    per_owner = encoder_weight.shape[2] // BLOCK
    blocks = per_owner * tok_count
    capacity = max(2, 2 * tok_rows * topk // blocks)
    slot_count = blocks * capacity
    positions = jax.vmap(lambda ids: slot_positions(ids, blocks, capacity))(block_ids)
    own_positions = lax.dynamic_index_in_dim(positions, layer_index, 0, keepdims=False)
    source_row = (
        jnp.full((slot_count,), tok_rows, jnp.int32)
        .at[own_positions]
        .set(jnp.arange(tok_rows * topk, dtype=jnp.int32) // topk)
    )
    padded = jnp.concatenate([residual[0], jnp.zeros((1, width), residual.dtype)], axis=0)
    outgoing = padded[source_row].reshape(tok_count, per_owner * capacity, width)
    arrived = lax.all_to_all(outgoing, "tok", split_axis=0, concat_axis=0, tiled=True)
    arrived = arrived.reshape(tok_count, per_owner, capacity, width)
    enc_blocks = encoder_weight[0].reshape(width, per_owner, BLOCK)
    pre = jnp.einsum("sbcd,dbe->sbce", arrived, enc_blocks, preferred_element_type=jnp.float32)
    pre = pre + encoder_bias[0].reshape(per_owner, BLOCK)[None, :, None, :]
    codes = (
        jnp.maximum(pre, 0.0)
        .astype(jnp.bfloat16)
        .reshape(1, tok_count, per_owner * capacity, BLOCK)
    )
    all_codes = lax.all_gather(codes, "layer", axis=0, tiled=True)
    sources = jnp.arange(layers, dtype=jnp.int32)
    valid = sources <= layer_index
    weights = decoder_weight[0]
    keep_slot = valid.astype(jnp.float32)
    slot_sets = sources.shape[0]
    chosen_codes = (
        jnp.take(all_codes, sources, axis=0) * valid.astype(jnp.bfloat16)[:, None, None, None]
    )
    terms = (
        jnp.einsum(
            "snbce,sbed->snbcd",
            chosen_codes.reshape(slot_sets, tok_count, per_owner, capacity, BLOCK),
            weights.reshape(slot_sets, per_owner, BLOCK, width),
            preferred_element_type=jnp.float32,
        )
        .astype(jnp.bfloat16)
        .reshape(slot_sets, tok_count, per_owner * capacity, width)
    )
    returned = lax.all_to_all(terms, "tok", split_axis=1, concat_axis=1, tiled=True).reshape(
        slot_sets, slot_count, width
    )
    source_positions = jnp.take(positions, sources, axis=0)
    picked = jax.vmap(lambda rows, where_at: rows[where_at])(returned, source_positions)
    parts = jnp.sum(picked.astype(jnp.float32).reshape(slot_sets, tok_rows, topk, width), axis=2)
    own_sum = jnp.sum(parts * keep_slot[:, None, None], axis=0)
    recon32 = decoder_bias[0][None, :] + own_sum
    difference = recon32 - targets[0].astype(jnp.float32)
    error = jnp.mean(difference * difference, axis=1)
    return (recon32.astype(jnp.bfloat16)[None], error[None])


def solution(mesh):
    in_specs = (
        P("layer", "tok", None),
        P("layer", "tok", None),
        P(None, "tok", None),
        P("layer", None, "tok"),
        P("layer", "tok"),
        P("layer", None, "tok", None),
        P("layer", None),
    )
    out_specs = (P("layer", "tok", None), P("layer", "tok"))
    return jax.shard_map(body, mesh=mesh, in_specs=in_specs, out_specs=out_specs, check_vma=False)
```

profile of v0, /device:TPU:0, one launch (start us, length us, event | category | flops | bytes accessed | tf_op | source)
XLA Modules:
  0.0 584.5 jit_solution(2805510803366540468)
XLA Ops:
  0.6 0.8 copy.34
  1.5 1.0 copy.38
  2.5 0.9 fusion.14
  3.4 0.2 broadcast_add_fusion
  3.7 0.1 copy.35
  3.8 0.4 fusion.16
  4.2 1.4 scatter_custom_fusion
  5.6 1.2 concatenate.3
  6.9 4.2 gather_fusion
  11.1 6.3 %all-to-all-start = ((bf16[8,64,3584]{2,1,0:T(8,128)(2,1)}), bf16[8,64,3584]{2,1,0:T(8,128)(2,1)}, u32[]{:S(2)}, u32[]{:S(2)}) async-start(bf16[8,64,3584]{2,1,0:T(8,128)(2,1)} %bitcast.60), calls=%async_computation | async-start | bytes 7340032 | tf_op jit(solution)/shard_map/all_to_all | solution.py:37
  17.4 14.5 %copy.50 = bf16[448,8,16,128]{3,2,1,0:T(8,128)(2,1)} copy(bf16[448,8,16,128]{3,1,2,0:T(8,128)(2,1)} %bitcast.61) | data formatting | bytes 29360128
  31.9 68.3 %all-to-all-done = bf16[8,64,3584]{2,1,0:T(8,128)(2,1)} async-done(((bf16[8,64,3584]{2,1,0:T(8,128)(2,1)}), bf16[8,64,3584]{2,1,0:T(8,128)(2,1)}, u32[]{:S(2)}, u32[]{:S(2)}) %all-to-all-start) | async-done | bytes 3670048 | tf_op jit(solution)/shard_map/all_to_all | solution.py:37
  100.3 4.1 copy.40
  104.3 0.0 copy-done.2
  104.3 13.2 %fusion.11 = bf16[16,8,4,128]{3,1,2,0:T(8,128)(2,1)S(1)} fusion(bf16[8,16,4,3584]{3,0,2,1:T(8,128)(2,1)S(1)} %bitcast.63, bf16[3584,16,128,1]{2,1,0,3:T(8,128)(2,1)} %bitcast.62, f32[16,128]{1,0:T(8,128)S(1)} %bitcast.70), kind=kOutput, calls=%fused_computation.16 | convolution fusion | flops 469958656 | bytes 18489344 | tf_op jit(solution)/shard_map/sbcd,dbe->sbce/dot_general | solution.py:40
  117.6 10.2 %all_gather.3 = bf16[4,8,64,128]{3,2,1,0:T(8,128)(2,1)S(1)} all-gather(bf16[1,8,64,128]{3,2,1,0:T(8,128)(2,1)S(1)} %copy.42), channel_id=1, replica_groups=mesh['layer'=4,'tok'=8] {'layer'}, dimensions={0}, use_global_device_ids=true | all-gather | bytes 655360 | tf_op jit(solution)/shard_map/all_gather | solution.py:47
  127.8 0.6 gather_fusion.1
  128.5 25.9 %convolution_convert_fusion = bf16[4,16,8,4,3584]{4,2,3,1,0:T(8,128)(2,1)} fusion(bf16[4,16,128,3584,1]{3,2,4,1,0:T(8,128)(2,1)} %bitcast.59, bf16[4,8,16,4,128]{4,3,2,1,0:T(4,128)(2,1)S(1)} %bitcast.64, pred[4]{0:T(512)(128)(4,1)S(1)} %get-tuple-element.3, bf16[4]{0:T(256)(128)(2,1)S(1)} %get-tuple-element.2), kind=kOutput, calls=%fused_computation.7 | convolution fusion | flops 1886912512 | bytes 73924624 | tf_op jit(solution)/shard_map/snbce,sbed->snbcd/dot_general | solution.py:57
  154.4 15.6 %copy.44 = bf16[4,8,64,3584]{3,2,0,1:T(8,128)(2,1)} copy(bf16[4,8,64,3584]{3,1,2,0:T(8,128)(2,1)} %bitcast.58) | data formatting | bytes 29360128 | tf_op jit(solution)/shard_map/reshape | solution.py:64
  170.0 5.7 all-to-all-start.1
  175.7 0.6 gather_fusion.2
  176.2 0.1 fusion.27
  176.3 0.0 copy-done.1
  176.4 318.0 %all-to-all-done.1 = bf16[4,8,64,3584]{3,2,0,1:T(8,128)(2,1)} async-done(((bf16[4,8,64,3584]{3,2,0,1:T(8,128)(2,1)}), bf16[4,8,64,3584]{3,2,0,1:T(8,128)(2,1)}, u32[]{:S(2)}, u32[]{:S(2)}) %all-to-all-start.1) | async-done | bytes 14680096 | tf_op jit(solution)/shard_map/all_to_all | solution.py:66
  494.4 13.4 %copy.45 = bf16[4,8,64,3584]{3,2,1,0:T(8,128)(2,1)} copy(bf16[4,8,64,3584]{3,2,0,1:T(8,128)(2,1)} %all-to-all-done.1) | data formatting | bytes 29360128 | tf_op jit(solution)/shard_map/all_to_all | solution.py:66
  507.8 32.0 %gather_fusion.3 = bf16[1024,3584]{1,0:T(8,128)(2,1)} fusion(bf16[4,512,3584]{2,1,0:T(8,128)(2,1)} %bitcast.56, s32[1024]{0:T(1024)S(1)} %bitcast.57), kind=kCustom, calls=%fused_computation.3 | custom fusion | bytes 14688256 | tf_op jit(solution)/shard_map/vmap()/gather | solution.py:70
  539.8 16.2 %reshape.172 = f32[4,128,2,3584]{3,2,1,0:T(2,128)} reshape(bf16[1024,3584]{1,0:T(8,128)(2,1)} %gather_fusion.3) | data formatting | bytes 22020096 | tf_op jit(solution)/shard_map/convert_element_type | solution.py:71
  556.0 22.3 %reduce_sum.39 = f32[4,128,3584]{2,1,0:T(8,128)} reduce(f32[4,128,2,3584]{3,2,1,0:T(2,128)} %reshape.172, f32[]{:T(128)} %constant.75.clone.1), dimensions={2}, to_apply=%region_4.5 | reduce | flops 1835008 | bytes 22020100 | tf_op jit(solution)/shard_map/reduce_sum | solution.py:71
  578.3 4.3 multiply_reduce_fusion
  582.6 1.0 fusion.4
  583.6 0.4 fusion.3
  584.0 0.5 multiply_bitcast_fusion
  (20 shorter events, 0.2 us)
Async XLA Ops:
  11.1 89.2 %all-to-all-start = ((bf16[8,64,3584]{2,1,0:T(8,128)(2,1)}), bf16[8,64,3584]{2,1,0:T(8,128)(2,1)}, u32[]{:S(2)}, u32[]{:S(2)}) async-start(bf16[8,64,3584]{2,1,0:T(8,128)(2,1)} %bitcast.60), calls=%async_computation | async-start | bytes 7340032 | tf_op jit(solution)/shard_map/all_to_all | solution.py:37
  31.9 72.4 %copy-start.2 = (f32[1,2048]{1,0:T(1,128)S(1)}, f32[1,2048]{1,0:T(1,128)}, u32[]{:S(2)}) copy-start(f32[1,2048]{1,0:T(1,128)} %param.11) | copy-start | bytes 24580
  170.0 6.3 %copy-start.1 = (f32[1,3584]{1,0:T(1,128)S(1)}, f32[1,3584]{1,0:T(1,128)}, u32[]{:S(2)}) copy-start(f32[1,3584]{1,0:T(1,128)} %param.13) | copy-start | bytes 43012
  170.0 324.4 %all-to-all-start.1 = ((bf16[4,8,64,3584]{3,2,0,1:T(8,128)(2,1)}), bf16[4,8,64,3584]{3,2,0,1:T(8,128)(2,1)}, u32[]{:S(2)}, u32[]{:S(2)}) async-start(bf16[4,8,64,3584]{3,2,0,1:T(8,128)(2,1)} %copy.44), calls=%async_computation.1 | async-start | bytes 29360128 | tf_op jit(solution)/shard_map/all_to_all | solution.py:66
  578.3 5.3 copy-start
where the time goes:
time: 586 us; the launch traced here: 585 us
  waiting for transfers between devices  386 us (66%)
  local copies, waits for them, and re-layouts  106 us (18%)
  matrix products  39.2 us (7%)
  other arithmetic  30.2 us (5%)
  starting transfers between devices  12 us (2%)
  blocking collectives  10.2 us (2%)
    all_to_all x1, waiting for transfers between devices, body(): lax.all_to_all(terms, 'tok', split_axis=1, concat_axis=1, tiled=True)  318 us
    all_to_all x1, waiting for transfers between devices, body(): lax.all_to_all(outgoing, 'tok', split_axis=0, concat_axis=0, tiled=True)  68.3 us
    gather x1, local copies, waits for them, and re-layouts, body(): rows[where_at]  32 us
    dot_general x1, matrix products, body(): jnp.einsum('snbce,sbed->snbcd', chosen_codes.reshape(slot_sets, tok_count...  25.9 us
    reduce_sum x1, other arithmetic, body(): jnp.sum(picked.astype(jnp.float32).reshape(slot_sets, tok_rows, topk, wid...  22.3 us
    convert_element_type x1, local copies, waits for them, and re-layouts, body(): picked.astype(jnp.float32).reshape(slot_sets, tok_rows, topk, width)  16.2 us
    reshape x1, local copies, waits for them, and re-layouts, body(): terms = jnp.einsum('snbce,sbed->snbcd', chosen_codes.reshape(slot_sets, t...  15.6 us
    unnamed x9, local copies, waits for them, and re-layouts  15.3 us
  transfers between devices with their start and end apart: 2, of which 2 were waited for; matrix products, arithmetic and copies ran while one was open for 3% of the time, Pallas kernels for 0%

commit v1 on v0

v1 whole, which is shorter than its diff:
```python
import jax
import jax.numpy as jnp
from jax import lax
from jax.sharding import PartitionSpec as P

BLOCK = 128


def owner_tables(ids_all, owner, per_owner, capacity, tokens):
    layers, _, topk = ids_all.shape
    local = ids_all.reshape(layers, tokens * topk) - owner * per_owner
    owned = (local >= 0) & (local < per_owner)
    onehot = (local[..., None] == jnp.arange(per_owner, dtype=jnp.int32)).astype(jnp.int32)
    rank = jnp.sum((jnp.cumsum(onehot, axis=1) - onehot) * onehot, axis=2)
    slot_count = per_owner * capacity
    slot = jnp.where(owned, local * capacity + rank, slot_count)
    token_of = jnp.arange(tokens * topk, dtype=jnp.int32) // topk
    empty = jnp.full((slot_count,), tokens, jnp.int32)
    return jax.vmap(lambda s: empty.at[s].set(token_of, mode="drop"))(slot)


def body(residual, targets, block_ids, encoder_weight, encoder_bias, decoder_weight, decoder_bias):
    layer_index = lax.axis_index("layer")
    tok_index = lax.axis_index("tok")
    layers = lax.axis_size("layer")
    tok_count = lax.axis_size("tok")
    tok_rows = residual.shape[1]
    width = residual.shape[2]
    topk = block_ids.shape[2]
    per_owner = encoder_weight.shape[2] // BLOCK
    blocks = per_owner * tok_count
    capacity = max(2, 2 * tok_rows * topk // blocks) * tok_count
    slot_count = per_owner * capacity
    tokens = tok_rows * tok_count

    ids_all = lax.all_gather(block_ids, "tok", axis=1, tiled=True)
    table = owner_tables(ids_all, tok_index, per_owner, capacity, tokens)

    res_all = lax.all_gather(residual[0], "tok", axis=0, tiled=True)
    own_table = lax.dynamic_index_in_dim(table, layer_index, 0, keepdims=False)
    rows = jnp.take(res_all, jnp.minimum(own_table, tokens - 1), axis=0)
    enc_blocks = encoder_weight[0].reshape(width, per_owner, BLOCK)
    pre = jnp.einsum(
        "bcd,dbe->bce",
        rows.reshape(per_owner, capacity, width),
        enc_blocks,
        preferred_element_type=jnp.float32,
    )
    pre = pre + encoder_bias[0].reshape(per_owner, 1, BLOCK)
    codes = jnp.maximum(pre, 0.0).astype(jnp.bfloat16)
    all_codes = lax.all_gather(codes, "layer", axis=0, tiled=False)

    terms = jnp.einsum(
        "sbce,sbed->sbcd",
        all_codes,
        decoder_weight[0].reshape(layers, per_owner, BLOCK, width),
        preferred_element_type=jnp.float32,
    ).astype(jnp.bfloat16)
    valid = jnp.arange(layers, dtype=jnp.int32) <= layer_index
    scatter = (table[:, :, None] == jnp.arange(tokens, dtype=jnp.int32)[None, None, :]) & valid[:, None, None]
    partial = jnp.einsum(
        "sct,scd->td",
        scatter.astype(jnp.bfloat16),
        terms.reshape(layers, slot_count, width),
        preferred_element_type=jnp.float32,
    )
    summed = lax.psum_scatter(partial.astype(jnp.bfloat16), "tok", scatter_dimension=0, tiled=True)
    recon32 = decoder_bias[0][None, :] + summed.astype(jnp.float32)
    difference = recon32 - targets[0].astype(jnp.float32)
    error = jnp.mean(difference * difference, axis=1)
    return (recon32.astype(jnp.bfloat16)[None], error[None])


def solution(mesh):
    in_specs = (
        P("layer", "tok", None),
        P("layer", "tok", None),
        P(None, "tok", None),
        P("layer", None, "tok"),
        P("layer", "tok"),
        P("layer", None, "tok", None),
        P("layer", None),
    )
    out_specs = (P("layer", "tok", None), P("layer", "tok"))
    return jax.shard_map(body, mesh=mesh, in_specs=in_specs, out_specs=out_specs, check_vma=False)
```

time: 586 us -> 265 us (0.45)
  waiting for transfers between devices: 386 us -> 77.1 us
  local copies, waits for them, and re-layouts: 106 us -> 63.7 us
  matrix products: 39.2 us -> 62.9 us
  blocking collectives: 10.2 us -> 24.2 us
  between operations: 0.81 us -> 14.3 us
  starting transfers between devices: 12 us -> 0.08 us
  other arithmetic: 30.2 us -> 22.6 us
    all_to_all x2 -> x0, waiting for transfers between devices: 386 us -> none  [the longest x1 318 us: body(): lax.all_to_all(terms, 'tok', split_axis=1, concat_axis=1, tiled=True)]
    reduce_scatter x0 -> x1, waiting for transfers between devices: none -> 76.4 us  [body(): lax.psum_scatter(partial.astype(jnp.bfloat16), 'tok', scatter_dimension=0...]
    unnamed x9 -> x16, local copies, waits for them, and re-layouts: 15.3 us -> 45.7 us
    reduce_sum x3 -> x1, other arithmetic: 27 us -> 0.17 us  [owner_tables(): rank = jnp.sum((jnp.cumsum(onehot, axis=1) - onehot) * onehot, axis=2)]
    gather x4 -> x1, local copies, waits for them, and re-layouts: 37.4 us -> 12 us  [body(): rows = jnp.take(res_all, jnp.minimum(own_table, tokens - 1), axis=0)]
    dot_general x2 -> x3, matrix products: 39.2 us -> 62.9 us  [the longest x1 26.1 us: body(): jnp.einsum('sbce,sbed->sbcd', all_codes, decoder_weight[0].reshape(layers...]
    another operation x3, other arithmetic: 1.08 us -> 19 us
    all_to_all x2 -> x0, local copies, waits for them, and re-layouts: 17.4 us -> none  [the longest x1 13.4 us: body(): lax.all_to_all(terms, 'tok', split_axis=1, concat_axis=1, tiled=True)]
  transfers between devices with their start and end apart: 2 -> 2, of which waited for: 2 -> 1; matrix products, arithmetic and copies ran while one was open for 3% -> 27% of each run, Pallas kernels for 0% -> 0%
where the time goes in v1:
time: 265 us
  waiting for transfers between devices  77.1 us (29%)
  local copies, waits for them, and re-layouts  63.7 us (24%)
  matrix products  62.9 us (24%)
  blocking collectives  24.2 us (9%)
  other arithmetic  22.6 us (9%)
  between operations  14.3 us (5%)
    reduce_scatter x1, waiting for transfers between devices, body(): lax.psum_scatter(partial.astype(jnp.bfloat16), 'tok', scatter_dimension=0...  76.4 us
    unnamed x16, local copies, waits for them, and re-layouts  45.7 us
    dot_general x1, matrix products, body(): jnp.einsum('sbce,sbed->sbcd', all_codes, decoder_weight[0].reshape(layers...  26.1 us
    dot_general x1, matrix products, body(): jnp.einsum('sct,scd->td', scatter.astype(jnp.bfloat16), terms.reshape(lay...  21.6 us
    another operation x3, other arithmetic  19 us
    dot_general x1, matrix products, body(): jnp.einsum('bcd,dbe->bce', rows.reshape(per_owner, capacity, width), enc_...  15.1 us
    all_gather x1, blocking collectives, body(): ids_all = lax.all_gather(block_ids, 'tok', axis=1, tiled=True)  13.8 us
    gather x1, local copies, waits for them, and re-layouts, body(): rows = jnp.take(res_all, jnp.minimum(own_table, tokens - 1), axis=0)  12 us
  transfers between devices with their start and end apart: 2, of which 1 were waited for; matrix products, arithmetic and copies ran while one was open for 27% of the time, Pallas kernels for 0%

profile of v1, /device:TPU:0, one launch (start us, length us, event | category | flops | bytes accessed | tf_op | source)
XLA Modules:
  0.0 264.9 jit_solution(11410956164858787547)
XLA Ops:
  7.2 0.0 all-gather.4.cloned.1.call-start
  7.2 0.7 all-gather.4.cloned.1.call-update
  7.9 0.0 reduce-scatter.2.cloned.1.call-start
  8.0 13.8 %all_gather.12 = s32[4,1024,2]{1,2,0:T(2,128)S(1)} all-gather(s32[4,128,2]{1,2,0:T(2,128)} %param.9), channel_id=1, replica_groups=mesh['layer'=4,'tok'=8] {'tok'}, dimensions={1}, use_global_device_ids=true | all-gather | bytes 36864 | tf_op jit(solution)/shard_map/all_gather | solution.py:36
  21.8 0.6 copy.20
  22.3 0.3 copy.23
  22.7 0.1 fusion.30
  22.7 18.1 %reduce-window.6 = s32[4,16,16,128]{3,2,1,0:T(8,128)S(1)} reduce-window(s32[4,16,16,128]{3,2,1,0:T(8,128)S(1)} %fusion.30, s32[]{:T(128)} %constant.55.clone.1), window={size=1x1x1x128 pad=0_0x0_0x0_0x127_0}, to_apply=%region_0.0 | reduce-window | flops 16646144 | bytes 1048580 | tf_op jit(solution)/shard_map/reduce-window
  40.9 1.3 slice_reduce_fusion
  42.2 0.7 reduce-window.9
  42.9 0.2 broadcast_add_fusion
  43.1 0.1 reduce_window_sum.16
  43.2 0.3 copy.21
  43.6 0.8 copy.18
  44.4 1.6 and.37
  46.0 0.6 copy.19
  46.6 0.3 copy.24
  46.9 0.2 fusion.29
  47.1 0.1 multiply_reduce_fusion
  47.2 0.1 and_reduce_fusion
  47.4 30.4 %scatter_custom_fusion = s32[2048]{0:T(1024)S(1)} fusion(s32[8192]{0:T(1024)S(1)} %bitcast.59, s32[8192]{0:T(1024)S(1)} %bitcast.60, s32[]{:T(128)} %constant.30.clone.1), kind=kCustom, calls=%fused_computation.52 | custom fusion | bytes 8196
  77.9 0.1 min.26
  78.0 14.5 %copy.28 = bf16[448,8,16,128]{3,2,1,0:T(8,128)(2,1)} copy(bf16[448,8,16,128]{3,1,2,0:T(8,128)(2,1)} %bitcast.51) | data formatting | bytes 29360128
  92.6 12.0 %gather_fusion = bf16[512,3584]{1,0:T(8,128)(2,1)} fusion(bf16[1024,3584]{1,0:T(8,128)(2,1)} %bitcast.48, s32[1024]{0:T(1024)S(1)} %pad_clamp_fusion), kind=kCustom, calls=%fused_computation | custom fusion | bytes 7342080 | tf_op jit(solution)/shard_map/jit(_take)/gather | solution.py:41
  104.6 15.1 %fusion.22 = bf16[16,32,128]{2,1,0:T(8,128)(2,1)S(1)} fusion(bf16[3584,16,128]{2,1,0:T(8,128)(2,1)} %bitcast.52, bf16[16,32,3584]{2,1,0:T(8,128)(2,1)} %bitcast.56, pred[16,32]{1,0:T(8,128)(4,1)S(1)} %compare_and_fusion.1, f32[16,128]{1,0:T(8,128)S(1)} %bitcast.62), kind=kOutput, calls=%fused_computation.20 | convolution fusion | flops 471793664 | bytes 18489856 | tf_op jit(solution)/shard_map/bcd,dbe->bce/dot_general | solution.py:43
  119.7 10.4 %all-gather.1 = bf16[64,32,128]{2,1,0:T(8,128)(2,1)S(1)} all-gather(bf16[16,32,128]{2,1,0:T(8,128)(2,1)S(1)} %fusion.22), channel_id=3, replica_groups=mesh['layer'=4,'tok'=8] {'layer'}, dimensions={0}, use_global_device_ids=true | all-gather | bytes 655360 | tf_op jit(solution)/shard_map/all_gather | solution.py:51
  130.1 26.1 %convolution_convert_fusion = bf16[4,16,32,3584]{3,2,1,0:T(8,128)(2,1)} fusion(bf16[4,16,32,128]{3,2,1,0:T(8,128)(2,1)S(1)} %bitcast.57, bf16[4,16,128,3584]{3,2,1,0:T(8,128)(2,1)} %bitcast.49), kind=kOutput, calls=%fused_computation.5 | convolution fusion | flops 1886388224 | bytes 73924608 | tf_op jit(solution)/shard_map/sbce,sbed->sbcd/dot_general | solution.py:53
  156.3 21.6 %bitcast_convert_fusion = bf16[1024,3584]{1,0:T(8,128)(2,1)} fusion(bf16[4,512,3584]{2,1,0:T(8,128)(2,1)} %bitcast.50, s32[4,512]{1,0:T(4,128)S(1)} %reshape.136, pred[4]{0:T(512)(128)(4,1)S(1)} %iota_compare_fusion.3), kind=kOutput, calls=%fused_computation.2 | convolution fusion | flops 15040249856 | bytes 22028292 | tf_op jit(solution)/shard_map/sct,scd->td/dot_general | solution.py:61
  177.9 0.7 copy-done.1
  178.6 76.4 %reduce-scatter.2.cloned.1.call-done = bf16[128,3584]{1,0:T(8,128)(2,1)} async-done(((bf16[1024,3584]{1,0:T(8,128)(2,1)}), bf16[128,3584]{1,0:T(8,128)(2,1)}) %reduce-scatter.2.cloned.1.call-update) | async-done | bytes 917520 | tf_op jit(solution)/shard_map/reduce_scatter | solution.py:67
  255.0 2.5 fusion.9
  257.5 0.5 multiply_bitcast_fusion
  (27 shorter events, 0.3 us)
Async XLA Ops:
  7.2 40.0 %copy-start.3 = (s32[2]{0:T(128)S(1)}, s32[2]{0:T(128)}, u32[]{:S(2)}) copy-start(s32[2]{0:T(128)} %constant.72) | copy-start | bytes 28
  7.2 40.1 %copy-start.2 = (s32[2]{0:T(128)S(1)}, s32[2]{0:T(128)}, u32[]{:S(2)}) copy-start(s32[2]{0:T(128)} %constant.75) | copy-start | bytes 28
  7.2 85.4 %all-gather.4.cloned.1.call-start = ((), (), s32[]{:S(2)}) async-start(), calls=%async_computation.2 | async-start | bytes 8257536 | tf_op jit(solution)/shard_map/all_gather | solution.py:39
  7.9 247.1 %reduce-scatter.2.cloned.1.call-start = ((), (), s32[]{:S(2)}) async-start(), calls=%async_computation.1 | async-start | bytes 8257536 | tf_op jit(solution)/shard_map/reduce_scatter | solution.py:67
  92.6 12.0 %copy-start.4 = (f32[1,2048]{1,0:T(1,128)S(1)}, f32[1,2048]{1,0:T(1,128)}, u32[]{:S(2)}) copy-start(f32[1,2048]{1,0:T(1,128)} %param.11) | copy-start | bytes 24580
  177.9 0.7 copy-start.1
  177.9 77.1 %copy-start = (bf16[1,128,3584]{2,1,0:T(8,128)(2,1)S(1)}, bf16[1,128,3584]{2,1,0:T(8,128)(2,1)}, u32[]{:S(2)}) copy-start(bf16[1,128,3584]{2,1,0:T(8,128)(2,1)} %param.8) | copy-start | bytes 2752516
Sparse Core Ops, SparseCore 0:
  9.7 76.0 all-gather.3
  178.0 76.9 reduce-scatter.1

commit v2 on v1

v2 whole, which is shorter than its diff:
```python
import math

import jax
import jax.numpy as jnp
from jax import lax
from jax.experimental import pallas as pl
from jax.sharding import PartitionSpec as P

BLOCK = 128


def encode_kernel(rows_ref, w_ref, b_ref, o_ref):
    group = rows_ref.shape[0]
    for i in range(group):
        cols = slice(i * BLOCK, (i + 1) * BLOCK)
        acc = jnp.dot(rows_ref[i], w_ref[:, cols], preferred_element_type=jnp.float32)
        acc = acc + b_ref[:, cols]
        o_ref[i] = jnp.maximum(acc, 0.0).astype(o_ref.dtype)


def encode(rows, weight, bias):
    per_owner, capacity, width = rows.shape
    group = math.gcd(per_owner, 4)
    return pl.pallas_call(
        encode_kernel,
        grid=(per_owner // group,),
        in_specs=[
            pl.BlockSpec((group, capacity, width), lambda g: (g, 0, 0)),
            pl.BlockSpec((width, group * BLOCK), lambda g: (0, g)),
            pl.BlockSpec((1, group * BLOCK), lambda g: (0, g)),
        ],
        out_specs=pl.BlockSpec((group, capacity, BLOCK), lambda g: (g, 0, 0)),
        out_shape=jax.ShapeDtypeStruct((per_owner, capacity, BLOCK), jnp.bfloat16),
    )(rows, weight, bias)


def pair_slots(ids, per_owner, cap):
    layers = ids.shape[0]
    flat = ids.reshape(layers, -1)
    n = flat.shape[1]
    earlier = jnp.arange(n, dtype=jnp.int32)[None, :] < jnp.arange(n, dtype=jnp.int32)[:, None]
    same = (flat[:, :, None] == flat[:, None, :]) & earlier[None]
    rank = jnp.sum(same.astype(jnp.int32), axis=2)
    return (flat * cap + rank).reshape(ids.shape)


def body(residual, targets, block_ids, encoder_weight, encoder_bias, decoder_weight, decoder_bias):
    layer_index = lax.axis_index("layer")
    tok_index = lax.axis_index("tok")
    layers = lax.axis_size("layer")
    tok_count = lax.axis_size("tok")
    tok_rows = residual.shape[1]
    width = residual.shape[2]
    topk = block_ids.shape[2]
    per_owner = encoder_weight.shape[2] // BLOCK
    blocks = per_owner * tok_count
    cap = max(2, 2 * tok_rows * topk // blocks)
    per_src = per_owner * cap
    tokens = tok_rows * tok_count

    codes_own = pair_slots(block_ids, per_owner, cap)
    codes_all = lax.all_gather(codes_own, "tok", axis=1, tiled=True)
    local = codes_all.reshape(layers, tok_count, tok_rows, topk) - tok_index * per_src
    hit = local[..., None] == jnp.arange(per_src, dtype=jnp.int32)
    pick = jnp.any(hit, axis=3)

    res_all = lax.all_gather(residual[0], "tok", axis=0, tiled=True).reshape(tok_count, tok_rows, width)
    own_pick = lax.dynamic_index_in_dim(pick, layer_index, 0, keepdims=False).astype(jnp.bfloat16)
    rows = jnp.einsum("stx,std->sxd", own_pick, res_all, preferred_element_type=jnp.float32).astype(jnp.bfloat16)
    rows = rows.reshape(tok_count, per_owner, cap, width).transpose(1, 0, 2, 3).reshape(per_owner, tok_count * cap, width)
    codes = encode(rows, encoder_weight[0], encoder_bias[0].reshape(1, -1))
    gathered = lax.all_gather(codes, "layer", axis=0, tiled=False)

    terms = jnp.einsum(
        "lbxe,lbed->lbxd",
        gathered,
        decoder_weight[0].reshape(layers, per_owner, BLOCK, width),
        preferred_element_type=jnp.float32,
    ).astype(jnp.bfloat16)
    terms = terms.reshape(layers, per_owner, tok_count, cap, width)
    valid = jnp.arange(layers, dtype=jnp.int32) <= layer_index
    combine = (pick & valid[:, None, None, None]).astype(jnp.bfloat16).reshape(layers, tok_count, tok_rows, per_owner, cap)
    partial = jnp.einsum("lstbr,lbsrd->std", combine, terms, preferred_element_type=jnp.float32)
    partial = partial.reshape(tokens, width).astype(jnp.bfloat16)
    summed = lax.psum_scatter(partial, "tok", scatter_dimension=0, tiled=True)
    recon32 = decoder_bias[0][None, :] + summed.astype(jnp.float32)
    difference = recon32 - targets[0].astype(jnp.float32)
    error = jnp.mean(difference * difference, axis=1)
    return (recon32.astype(jnp.bfloat16)[None], error[None])


def solution(mesh):
    in_specs = (
        P("layer", "tok", None),
        P("layer", "tok", None),
        P(None, "tok", None),
        P("layer", None, "tok"),
        P("layer", "tok"),
        P("layer", None, "tok", None),
        P("layer", None),
    )
    out_specs = (P("layer", "tok", None), P("layer", "tok"))
    return jax.shard_map(body, mesh=mesh, in_specs=in_specs, out_specs=out_specs, check_vma=False)
```

time: 265 us -> 286 us (1.079)
  waiting for transfers between devices: 77.1 us -> 138 us
  local copies, waits for them, and re-layouts: 63.7 us -> 44.9 us
  other arithmetic: 22.6 us -> 4.91 us
  matrix products: 62.9 us -> 49.5 us
  Pallas kernels: 0 us -> 8.06 us
    all_gather x1, waiting for transfers between devices: 0.02 us -> 60.2 us  [body(): lax.all_gather(residual[0], 'tok', axis=0, tiled=True)]
    unnamed x16 -> x5, local copies, waits for them, and re-layouts: 45.7 us -> 1.52 us
    reshape x0 -> x4, local copies, waits for them, and re-layouts: none -> 42.9 us  [the longest x1 23.6 us: body(): terms = terms.reshape(layers, per_owner, tok_count, cap, width)]
    another operation x3 -> x0, other arithmetic: 19 us -> none
    dot_general x3, matrix products: 62.9 us -> 49.5 us  [the longest x1 25.8 us: body(): jnp.einsum('lbxe,lbed->lbxd', gathered, decoder_weight[0].reshape(layers,...]
    gather x1 -> x0, local copies, waits for them, and re-layouts: 12 us -> none  [body(): rows = jnp.take(res_all, jnp.minimum(own_table, tokens - 1), axis=0)]
    pallas_call x0 -> x1, Pallas kernels: none -> 8.06 us  [encode(): pl.pallas_call(encode_kernel, grid=(per_owner // group,), in_specs=[pl.Bl...]
  transfers between devices with their start and end apart: 2 -> 2, of which waited for: 1 -> 2; matrix products, arithmetic and copies ran while one was open for 27% -> 1% of each run, Pallas kernels for 0% -> 0%
where the time goes in v2:
time: 286 us; the launch traced here: 285 us
  waiting for transfers between devices  138 us (48%)
  matrix products  49.5 us (17%)
  local copies, waits for them, and re-layouts  44.9 us (16%)
  blocking collectives  25.4 us (9%)
  between operations  14.1 us (5%)
  Pallas kernels  8.06 us (3%)
  other arithmetic  4.91 us (2%)
    reduce_scatter x1, waiting for transfers between devices, body(): summed = lax.psum_scatter(partial, 'tok', scatter_dimension=0, tiled=True)  76.8 us
    all_gather x1, waiting for transfers between devices, body(): lax.all_gather(residual[0], 'tok', axis=0, tiled=True)  60.2 us
    dot_general x1, matrix products, body(): jnp.einsum('lbxe,lbed->lbxd', gathered, decoder_weight[0].reshape(layers,...  25.8 us
    reshape x1, local copies, waits for them, and re-layouts, body(): terms = terms.reshape(layers, per_owner, tok_count, cap, width)  23.6 us
    reshape x3, local copies, waits for them, and re-layouts, body(): rows.reshape(tok_count, per_owner, cap, width).transpose(1, 0, 2, 3)  19.3 us
    dot_general x1, matrix products, body(): jnp.einsum('lstbr,lbsrd->std', combine, terms, preferred_element_type=jnp...  17.6 us
    all_gather x1, blocking collectives, body(): codes_all = lax.all_gather(codes_own, 'tok', axis=1, tiled=True)  14.4 us
    all_gather x1, blocking collectives, body(): gathered = lax.all_gather(codes, 'layer', axis=0, tiled=False)  11 us
  transfers between devices with their start and end apart: 2, of which 2 were waited for; matrix products, arithmetic and copies ran while one was open for 1% of the time, Pallas kernels for 0%

profile of v2, /device:TPU:0, one launch (start us, length us, event | category | flops | bytes accessed | tf_op | source)
XLA Modules:
  0.0 284.7 jit_solution(2051033257295605151)
XLA Ops:
  7.2 0.0 all-gather.4.cloned.1.call-start
  7.2 0.7 all-gather.4.cloned.1.call-update
  7.9 0.0 reduce-scatter.2.cloned.1.call-start
  7.9 0.8 copy.46
  8.8 0.1 copy.47
  8.9 0.4 convert_reduce_fusion
  9.3 0.1 copy.49
  9.5 0.1 copy.50
  9.5 0.7 fusion.12
  10.2 14.4 %all_gather.12 = s32[4,1024,2]{1,0,2:T(4,128)S(1)} all-gather(s32[4,128,2]{1,0,2:T(4,128)S(1)} %fusion.12), channel_id=1, replica_groups=mesh['layer'=4,'tok'=8] {'tok'}, dimensions={1}, use_global_device_ids=true | all-gather | bytes 36864 | tf_op jit(solution)/shard_map/all_gather | solution.py:62
  24.7 0.5 fusion.4
  25.2 0.2 copy.52
  25.4 0.2 broadcast_and_fusion
  25.6 60.2 %all-gather.4.cloned.1.call-done = bf16[1,1024,3584]{2,1,0:T(8,128)(2,1)} async-done(((bf16[1,128,3584]{2,1,0:T(8,128)(2,1)}), bf16[1,1024,3584]{2,1,0:T(8,128)(2,1)}) %all-gather.4.cloned.1.call-update) | async-done | bytes 7340048 | tf_op jit(solution)/shard_map/all_gather | solution.py:67
  85.8 6.1 %convolution_convert_fusion.1 = bf16[8,64,3584]{2,1,0:T(8,128)(2,1)} fusion(bf16[8,128,3584]{2,1,0:T(8,128)(2,1)} %bitcast.36, pred[4,8,128,64]{2,3,1,0:T(8,128)(4,1)S(1)} %fusion.4, s32[]{:T(128)S(6)} %select_n.4), kind=kOutput, calls=%fused_computation.4 | convolution fusion | flops 471597056 | bytes 11075588 | tf_op jit(solution)/shard_map/stx,std->sxd/dot_general | solution.py:69
  91.9 7.0 %reshape.61 = bf16[8,16,4,3584]{3,2,1,0:T(4,128)(2,1)} reshape(bf16[8,64,3584]{2,1,0:T(8,128)(2,1)} %convolution_convert_fusion.1) | data formatting | bytes 7340032 | tf_op jit(solution)/shard_map/reshape | solution.py:70
  98.9 5.6 %copy.67 = bf16[8,16,4,3584]{3,2,0,1:T(4,128)(2,1)} copy(bf16[8,16,4,3584]{3,2,1,0:T(4,128)(2,1)} %reshape.61) | data formatting | bytes 7340032 | tf_op jit(solution)/shard_map/reshape | solution.py:70
  104.5 6.7 %reshape.62.rows_ref = bf16[16,32,3584]{2,1,0:T(8,128)(2,1)} reshape(bf16[16,8,4,3584]{3,2,1,0:T(4,128)(2,1)} %bitcast.37) | data formatting | bytes 7340032 | tf_op jit(solution)/shard_map/reshape | solution.py:70
  111.2 8.1 %shard_map.86 = bf16[16,32,128]{2,1,0:T(8,128)(2,1)} custom-call(bf16[16,32,3584]{2,1,0:T(8,128)(2,1)} %reshape.62.rows_ref, bf16[3584,2048]{1,0:T(8,128)(2,1)} %bitcast.38, f32[1,2048]{1,0:T(1,128)} %b_ref.1), custom_call_target="tpu_custom_call" | custom-call | tf_op jit(solution)/shard_map/pallas_call | solution.py:24
  119.3 11.0 %all-gather.1 = bf16[64,32,128]{2,1,0:T(8,128)(2,1)S(1)} all-gather(bf16[16,32,128]{2,1,0:T(8,128)(2,1)} %shard_map.86), channel_id=3, replica_groups=mesh['layer'=4,'tok'=8] {'layer'}, dimensions={0}, use_global_device_ids=true | all-gather | bytes 655360 | tf_op jit(solution)/shard_map/all_gather | solution.py:72
  130.3 25.8 %convolution_convert_fusion = bf16[4,16,32,3584]{3,2,1,0:T(8,128)(2,1)} fusion(bf16[4,16,32,128]{3,2,1,0:T(8,128)(2,1)S(1)} %bitcast.39, bf16[4,16,128,3584]{3,2,1,0:T(8,128)(2,1)} %bitcast.34), kind=kOutput, calls=%fused_computation.3 | convolution fusion | flops 1886388224 | bytes 73924608 | tf_op jit(solution)/shard_map/lbxe,lbed->lbxd/dot_general | solution.py:74
  156.1 23.6 %reshape.63 = bf16[4,16,8,4,3584]{4,3,2,1,0:T(4,128)(2,1)} reshape(bf16[4,16,32,3584]{3,2,1,0:T(8,128)(2,1)} %convolution_convert_fusion) | data formatting | bytes 29360128 | tf_op jit(solution)/shard_map/reshape | solution.py:80
  179.7 17.6 %bitcast_convert_fusion = bf16[8,128,3584]{2,1,0:T(8,128)(2,1)} fusion(bf16[4,16,8,4,3584]{4,3,2,1,0:T(4,128)(2,1)} %reshape.63, pred[4,8,128,16,4]{2,1,4,3,0:T(8,128)(4,1)S(1)} %broadcast_and_fusion), kind=kOutput, calls=%fused_computation | convolution fusion | flops 1882718208 | bytes 22282240 | tf_op jit(solution)/shard_map/lstbr,lbsrd->std/dot_general | solution.py:83
  197.3 0.0 copy-start.1
  197.3 0.0 copy-start
  197.3 0.0 reduce-scatter.2.cloned.1.call-update
  197.3 0.7 copy-done.1
  198.1 76.8 %reduce-scatter.2.cloned.1.call-done = bf16[128,3584]{1,0:T(8,128)(2,1)} async-done(((bf16[1024,3584]{1,0:T(8,128)(2,1)}), bf16[128,3584]{1,0:T(8,128)(2,1)}) %reduce-scatter.2.cloned.1.call-update) | async-done | bytes 917520 | tf_op jit(solution)/shard_map/reduce_scatter | solution.py:85
  274.9 0.0 copy-done
  274.9 2.5 fusion.6
  277.4 0.5 multiply_bitcast_fusion
  (6 shorter events, 0.1 us)
Async XLA Ops:
  7.2 78.6 %all-gather.4.cloned.1.call-start = ((), (), s32[]{:S(2)}) async-start(), calls=%async_computation.2 | async-start | bytes 8257536 | tf_op jit(solution)/shard_map/all_gather | solution.py:67
  7.9 267.0 %reduce-scatter.2.cloned.1.call-start = ((), (), s32[]{:S(2)}) async-start(), calls=%async_computation.1 | async-start | bytes 8257536 | tf_op jit(solution)/shard_map/reduce_scatter | solution.py:85
  197.3 0.7 copy-start.1
  197.3 77.6 %copy-start = (bf16[1,128,3584]{2,1,0:T(8,128)(2,1)S(1)}, bf16[1,128,3584]{2,1,0:T(8,128)(2,1)}, u32[]{:S(2)}) copy-start(bf16[1,128,3584]{2,1,0:T(8,128)(2,1)} %param.8) | copy-start | bytes 2752516
Sparse Core Ops, SparseCore 0:
  9.6 76.1 all-gather.3
  197.5 77.3 reduce-scatter.1

commit v3 on v2

--- a/solution.py
+++ b/solution.py
@@ -57,32 +57,46 @@
     cap = max(2, 2 * tok_rows * topk // blocks)
     per_src = per_owner * cap
     tokens = tok_rows * tok_count
+    slot_count = per_owner * tok_count * cap
 
     codes_own = pair_slots(block_ids, per_owner, cap)
     codes_all = lax.all_gather(codes_own, "tok", axis=1, tiled=True)
     local = codes_all.reshape(layers, tok_count, tok_rows, topk) - tok_index * per_src
-    hit = local[..., None] == jnp.arange(per_src, dtype=jnp.int32)
-    pick = jnp.any(hit, axis=3)
+    src_of = jnp.arange(tok_count, dtype=jnp.int32)[:, None]
+    slot_of = jnp.where(
+        (local >= 0) & (local < per_src),
+        (local // cap) * (tok_count * cap) + src_of[None, :, :, None] * cap + local % cap,
+        slot_count,
+    ).reshape(layers, tokens, topk)
+    onehot = jnp.any(slot_of[..., None] == jnp.arange(slot_count, dtype=jnp.int32), axis=2)
 
-    res_all = lax.all_gather(residual[0], "tok", axis=0, tiled=True).reshape(tok_count, tok_rows, width)
-    own_pick = lax.dynamic_index_in_dim(pick, layer_index, 0, keepdims=False).astype(jnp.bfloat16)
-    rows = jnp.einsum("stx,std->sxd", own_pick, res_all, preferred_element_type=jnp.float32).astype(jnp.bfloat16)
-    rows = rows.reshape(tok_count, per_owner, cap, width).transpose(1, 0, 2, 3).reshape(per_owner, tok_count * cap, width)
-    codes = encode(rows, encoder_weight[0], encoder_bias[0].reshape(1, -1))
+    res_all = lax.all_gather(residual[0], "tok", axis=0, tiled=True)
+    own_onehot = lax.dynamic_index_in_dim(onehot, layer_index, 0, keepdims=False).astype(jnp.bfloat16)
+    rows = jnp.einsum("tx,td->xd", own_onehot, res_all, preferred_element_type=jnp.float32).astype(jnp.bfloat16)
+    codes = encode(rows.reshape(per_owner, tok_count * cap, width), encoder_weight[0], encoder_bias[0].reshape(1, -1))
     gathered = lax.all_gather(codes, "layer", axis=0, tiled=False)
 
-    terms = jnp.einsum(
-        "lbxe,lbed->lbxd",
-        gathered,
-        decoder_weight[0].reshape(layers, per_owner, BLOCK, width),
-        preferred_element_type=jnp.float32,
-    ).astype(jnp.bfloat16)
-    terms = terms.reshape(layers, per_owner, tok_count, cap, width)
     valid = jnp.arange(layers, dtype=jnp.int32) <= layer_index
-    combine = (pick & valid[:, None, None, None]).astype(jnp.bfloat16).reshape(layers, tok_count, tok_rows, per_owner, cap)
-    partial = jnp.einsum("lstbr,lbsrd->std", combine, terms, preferred_element_type=jnp.float32)
-    partial = partial.reshape(tokens, width).astype(jnp.bfloat16)
-    summed = lax.psum_scatter(partial, "tok", scatter_dimension=0, tiled=True)
+    combine = (onehot & valid[:, None, None]).astype(jnp.bfloat16)
+    weights = decoder_weight[0].reshape(layers, per_owner, BLOCK, width)
+    chunks = 4 if width % (4 * BLOCK) == 0 else 1
+    step = width // chunks
+    pieces = []
+    for c in range(chunks):
+        terms = jnp.einsum(
+            "lbxe,lbed->lbxd",
+            gathered,
+            weights[..., c * step:(c + 1) * step],
+            preferred_element_type=jnp.float32,
+        ).astype(jnp.bfloat16)
+        partial = jnp.einsum(
+            "ltx,lxd->td",
+            combine,
+            terms.reshape(layers, slot_count, step),
+            preferred_element_type=jnp.float32,
+        ).astype(jnp.bfloat16)
+        pieces.append(lax.psum_scatter(partial, "tok", scatter_dimension=0, tiled=True))
+    summed = jnp.concatenate(pieces, axis=1)
     recon32 = decoder_bias[0][None, :] + summed.astype(jnp.float32)
     difference = recon32 - targets[0].astype(jnp.float32)
     error = jnp.mean(difference * difference, axis=1)

time: 286 us -> 278 us (0.972)
  local copies, waits for them, and re-layouts: 44.9 us -> 1.24 us
  waiting for transfers between devices: 138 us -> 158 us
  matrix products: 49.5 us -> 61.7 us
  other arithmetic: 4.91 us -> 8.44 us
    reshape x4 -> x0, local copies, waits for them, and re-layouts: 42.9 us -> none  [the longest x1 23.6 us: body(): terms = terms.reshape(layers, per_owner, tok_count, cap, width)]
    reduce_scatter x1 -> x4, waiting for transfers between devices: 76.8 us -> 99.1 us  [body(): lax.psum_scatter(partial, 'tok', scatter_dimension=0, tiled=True)]
    dot_general x3 -> x9, matrix products: 49.5 us -> 61.7 us  [the longest x4 30.2 us: body(): jnp.einsum('lbxe,lbed->lbxd', gathered, weights[..., c * step:(c + 1) * s...]
  transfers between devices with their start and end apart: 2 -> 5, of which waited for: 2 -> 4; matrix products, arithmetic and copies ran while one was open for 1% -> 16% of each run, Pallas kernels for 0% -> 0%
where the time goes in v3:
time: 278 us
  waiting for transfers between devices  158 us (57%)
  matrix products  61.7 us (22%)
  blocking collectives  25.4 us (9%)
  between operations  13.9 us (5%)
  other arithmetic  8.44 us (3%)
  Pallas kernels  8.03 us (3%)
    reduce_scatter x4, waiting for transfers between devices, body(): lax.psum_scatter(partial, 'tok', scatter_dimension=0, tiled=True)  99.1 us
    all_gather x1, waiting for transfers between devices, body(): res_all = lax.all_gather(residual[0], 'tok', axis=0, tiled=True)  58.4 us
    dot_general x4, matrix products, body(): jnp.einsum('lbxe,lbed->lbxd', gathered, weights[..., c * step:(c + 1) * s...  30.2 us
    dot_general x4, matrix products, body(): jnp.einsum('ltx,lxd->td', combine, terms.reshape(layers, slot_count, step...  22.8 us
    all_gather x1, blocking collectives, body(): codes_all = lax.all_gather(codes_own, 'tok', axis=1, tiled=True)  14.4 us
    all_gather x1, blocking collectives, body(): gathered = lax.all_gather(codes, 'layer', axis=0, tiled=False)  11 us
    dot_general x1, matrix products, body(): jnp.einsum('tx,td->xd', own_onehot, res_all, preferred_element_type=jnp.f...  8.58 us
    pallas_call x1, Pallas kernels, encode(): pl.pallas_call(encode_kernel, grid=(per_owner // group,), in_specs=[pl.Bl...  8.03 us
  transfers between devices with their start and end apart: 5, of which 4 were waited for; matrix products, arithmetic and copies ran while one was open for 16% of the time, Pallas kernels for 0%

profile of v3, /device:TPU:0, one launch (start us, length us, event | category | flops | bytes accessed | tf_op | source)
XLA Modules:
  0.0 277.5 jit_solution(12500483933215530243)
XLA Ops:
  7.2 0.7 all-gather.4.cloned.1.call-update
  7.9 0.8 copy.32
  8.8 0.1 copy.33
  8.9 0.4 convert_reduce_fusion
  9.3 0.1 copy.35
  9.5 0.1 copy.36
  9.5 0.7 fusion.36
  10.2 14.4 %all_gather.12 = s32[4,1024,2]{1,0,2:T(4,128)S(1)} all-gather(s32[4,128,2]{1,0,2:T(4,128)S(1)} %fusion.36), channel_id=1, replica_groups=mesh['layer'=4,'tok'=8] {'tok'}, dimensions={1}, use_global_device_ids=true | all-gather | bytes 36864 | tf_op jit(solution)/shard_map/all_gather | solution.py:63
  24.6 0.1 broadcast_bitcast_fusion
  24.7 0.1 fusion.33
  24.9 2.6 fusion
  27.4 58.4 %all-gather.4.cloned.1.call-done = bf16[1,1024,3584]{2,1,0:T(8,128)(2,1)} async-done(((bf16[1,128,3584]{2,1,0:T(8,128)(2,1)}), bf16[1,1024,3584]{2,1,0:T(8,128)(2,1)}) %all-gather.4.cloned.1.call-update) | async-done | bytes 7340048 | tf_op jit(solution)/shard_map/all_gather | solution.py:73
  85.8 8.6 %fusion.11 = bf16[512,3584]{1,0:T(8,128)(2,1)} fusion(bf16[1,1024,3584]{2,1,0:T(8,128)(2,1)} %all-gather.4.cloned.1.call-done, pred[4,1024,512]{2,1,0:T(8,128)(4,1)S(1)} %fusion, s32[]{:T(128)S(6)} %select_n.29), kind=kOutput, calls=%fused_computation.12 | convolution fusion | flops 3759931392 | bytes 11534340 | tf_op jit(solution)/shard_map/tx,td->xd/dot_general | solution.py:75
  94.4 8.0 %shard_map.86 = bf16[16,32,128]{2,1,0:T(8,128)(2,1)} custom-call(bf16[16,32,3584]{2,1,0:T(8,128)(2,1)} %bitcast.58, bf16[3584,2048]{1,0:T(8,128)(2,1)} %bitcast.49, f32[1,2048]{1,0:T(1,128)} %b_ref.1), custom_call_target="tpu_custom_call" | custom-call | tf_op jit(solution)/shard_map/pallas_call | solution.py:24
  102.4 11.0 %all-gather.1 = bf16[64,32,128]{2,1,0:T(8,128)(2,1)S(1)} all-gather(bf16[16,32,128]{2,1,0:T(8,128)(2,1)} %shard_map.86), channel_id=3, replica_groups=mesh['layer'=4,'tok'=8] {'layer'}, dimensions={0}, use_global_device_ids=true | all-gather | bytes 655360 | tf_op jit(solution)/shard_map/all_gather | solution.py:77
  113.4 7.5 %fusion.14 = bf16[4,16,32,896]{3,2,1,0:T(8,128)(2,1)S(1)} fusion(bf16[4,16,32,128]{3,2,1,0:T(8,128)(2,1)S(1)} %bitcast.50, bf16[4,16,128,3584]{3,2,1,0:T(8,128)(2,1)} %bitcast.45), kind=kOutput, calls=%fused_computation.18 | convolution fusion | flops 471597056 | bytes 18874368 | tf_op jit(solution)/shard_map/lbxe,lbed->lbxd/dot_general | solution.py:86
  120.9 5.7 %bitcast_convert_fusion.3 = bf16[1024,896]{1,0:T(8,128)(2,1)} fusion(bf16[4,512,896]{2,1,0:T(8,128)(2,1)S(1)} %bitcast.55, pred[4,1024,512]{2,1,0:T(8,128)(4,1)S(1)} %fusion, pred[4]{0:T(512)(128)(4,1)S(1)} %iota_compare_fusion.2), kind=kOutput, calls=%fused_computation.17 | convolution fusion | flops 3761111040 | bytes 7602180 | tf_op jit(solution)/shard_map/ltx,lxd->td/dot_general | solution.py:92
  126.7 0.2 reduce-scatter.7.cloned.1.call-start
  126.9 7.7 %fusion.17 = bf16[4,16,32,896]{3,2,1,0:T(8,128)(2,1)S(1)} fusion(bf16[4,16,32,128]{3,2,1,0:T(8,128)(2,1)S(1)} %bitcast.51, bf16[4,16,128,3584]{3,2,1,0:T(8,128)(2,1)} %bitcast.46), kind=kOutput, calls=%fused_computation.19 | convolution fusion | flops 471597056 | bytes 18874368 | tf_op jit(solution)/shard_map/lbxe,lbed->lbxd/dot_general | solution.py:86
  134.6 5.7 %bitcast_convert_fusion.2 = bf16[1024,896]{1,0:T(8,128)(2,1)} fusion(bf16[4,512,896]{2,1,0:T(8,128)(2,1)S(1)} %bitcast.56, pred[4,1024,512]{2,1,0:T(8,128)(4,1)S(1)} %fusion, pred[4]{0:T(512)(128)(4,1)S(1)} %iota_compare_fusion.2), kind=kOutput, calls=%fused_computation.16 | convolution fusion | flops 3761111040 | bytes 7602180 | tf_op jit(solution)/shard_map/ltx,lxd->td/dot_general | solution.py:92
  140.3 0.0 reduce-scatter.9.cloned.1.call-start
  140.4 7.6 %fusion.20 = bf16[4,16,32,896]{3,2,1,0:T(8,128)(2,1)S(1)} fusion(bf16[4,16,32,128]{3,2,1,0:T(8,128)(2,1)S(1)} %bitcast.52, bf16[4,16,128,3584]{3,2,1,0:T(8,128)(2,1)} %bitcast.47), kind=kOutput, calls=%fused_computation.20 | convolution fusion | flops 471597056 | bytes 18874368 | tf_op jit(solution)/shard_map/lbxe,lbed->lbxd/dot_general | solution.py:86
  147.9 5.7 %bitcast_convert_fusion.1 = bf16[1024,896]{1,0:T(8,128)(2,1)} fusion(bf16[4,512,896]{2,1,0:T(8,128)(2,1)S(1)} %bitcast.57, pred[4,1024,512]{2,1,0:T(8,128)(4,1)S(1)} %fusion, pred[4]{0:T(512)(128)(4,1)S(1)} %iota_compare_fusion.2), kind=kOutput, calls=%fused_computation.15 | convolution fusion | flops 3761111040 | bytes 7602180 | tf_op jit(solution)/shard_map/ltx,lxd->td/dot_general | solution.py:92
  153.6 0.3 reduce-scatter.11.cloned.1.call-start
  153.9 7.5 %fusion.23 = bf16[4,16,32,896]{3,2,1,0:T(8,128)(2,1)S(1)} fusion(bf16[4,16,32,128]{3,2,1,0:T(8,128)(2,1)S(1)} %bitcast.53, bf16[4,16,128,3584]{3,2,1,0:T(8,128)(2,1)} %bitcast.48), kind=kOutput, calls=%fused_computation.21 | convolution fusion | flops 471597056 | bytes 18874368 | tf_op jit(solution)/shard_map/lbxe,lbed->lbxd/dot_general | solution.py:86
  161.5 5.7 %bitcast_convert_fusion = bf16[1024,896]{1,0:T(8,128)(2,1)} fusion(bf16[4,512,896]{2,1,0:T(8,128)(2,1)S(1)} %bitcast.54, pred[4,1024,512]{2,1,0:T(8,128)(4,1)S(1)} %fusion, pred[4]{0:T(512)(128)(4,1)S(1)} %iota_compare_fusion.2), kind=kOutput, calls=%fused_computation.14 | convolution fusion | flops 3761111040 | bytes 7602180 | tf_op jit(solution)/shard_map/ltx,lxd->td/dot_general | solution.py:92
  167.3 28.0 %reduce-scatter.7.cloned.1.call-done = bf16[128,896]{1,0:T(8,128)(2,1)} async-done(((bf16[1024,896]{1,0:T(8,128)(2,1)}), bf16[128,896]{1,0:T(8,128)(2,1)}) %reduce-scatter.7.cloned.1.call-update) | async-done | bytes 229392 | tf_op jit(solution)/shard_map/reduce_scatter | solution.py:98
  195.3 35.5 %reduce-scatter.9.cloned.1.call-done = bf16[128,896]{1,0:T(8,128)(2,1)} async-done(((bf16[1024,896]{1,0:T(8,128)(2,1)}), bf16[128,896]{1,0:T(8,128)(2,1)}) %reduce-scatter.9.cloned.1.call-update) | async-done | bytes 229392 | tf_op jit(solution)/shard_map/reduce_scatter | solution.py:98
  230.8 35.6 %reduce-scatter.11.cloned.1.call-done = bf16[128,896]{1,0:T(8,128)(2,1)} async-done(((bf16[1024,896]{1,0:T(8,128)(2,1)}), bf16[128,896]{1,0:T(8,128)(2,1)}) %reduce-scatter.11.cloned.1.call-update) | async-done | bytes 229392 | tf_op jit(solution)/shard_map/reduce_scatter | solution.py:98
  266.4 1.7 fusion.29
  268.1 0.5 multiply_bitcast_fusion
  268.6 2.4 add_convert_fusion
  (16 shorter events, 0.3 us)
Async XLA Ops:
  7.2 78.6 %all-gather.4.cloned.1.call-start = ((), (), s32[]{:S(2)}) async-start(), calls=%async_computation.8 | async-start | bytes 8257536 | tf_op jit(solution)/shard_map/all_gather | solution.py:73
  7.9 159.4 %reduce-scatter.5.cloned.1.call-start = ((), (), s32[]{:S(2)}) async-start(), calls=%async_computation.4 | async-start | bytes 2064384 | tf_op jit(solution)/shard_map/reduce_scatter | solution.py:98
  126.7 68.6 %reduce-scatter.7.cloned.1.call-start = ((), (), s32[]{:S(2)}) async-start(), calls=%async_computation.5 | async-start | bytes 2064384 | tf_op jit(solution)/shard_map/reduce_scatter | solution.py:98
  140.3 90.5 %reduce-scatter.9.cloned.1.call-start = ((), (), s32[]{:S(2)}) async-start(), calls=%async_computation.6 | async-start | bytes 2064384 | tf_op jit(solution)/shard_map/reduce_scatter | solution.py:98
  153.6 112.8 %reduce-scatter.11.cloned.1.call-start = ((), (), s32[]{:S(2)}) async-start(), calls=%async_computation.7 | async-start | bytes 2064384 | tf_op jit(solution)/shard_map/reduce_scatter | solution.py:98
  161.5 5.8 %copy-start.1 = (f32[1,3584]{1,0:T(1,128)S(1)}, f32[1,3584]{1,0:T(1,128)}, u32[]{:S(2)}) copy-start(f32[1,3584]{1,0:T(1,128)} %param.13) | copy-start | bytes 43012
  161.5 104.9 %copy-start = (bf16[1,128,3584]{2,1,0:T(8,128)(2,1)S(1)}, bf16[1,128,3584]{2,1,0:T(8,128)(2,1)}, u32[]{:S(2)}) copy-start(bf16[1,128,3584]{2,1,0:T(8,128)(2,1)} %param.8) | copy-start | bytes 2752516
Sparse Core Ops, SparseCore 0:
  9.6 76.1 all-gather.3
  126.8 32.7 reduce-scatter.4
  162.0 33.2 reduce-scatter.6
  197.4 33.3 reduce-scatter.8
  233.0 33.3 reduce-scatter.10

commit v4 on v3

--- a/solution.py
+++ b/solution.py
@@ -4,6 +4,7 @@
 import jax.numpy as jnp
 from jax import lax
 from jax.experimental import pallas as pl
+from jax.experimental.pallas import tpu as pltpu
 from jax.sharding import PartitionSpec as P
 
 BLOCK = 128
@@ -32,6 +33,58 @@
         out_specs=pl.BlockSpec((group, capacity, BLOCK), lambda g: (g, 0, 0)),
         out_shape=jax.ShapeDtypeStruct((per_owner, capacity, BLOCK), jnp.bfloat16),
     )(rows, weight, bias)
+
+
+def decode_kernel(codes_ref, w_ref, c_ref, o_ref, t_ref, acc_ref):
+    l = pl.program_id(1)
+    b = pl.program_id(2)
+    rows = codes_ref.shape[2]
+    term = jnp.dot(codes_ref[0, 0], w_ref[0], preferred_element_type=jnp.float32)
+    t_ref[pl.ds(pl.multiple_of(b * rows, rows), rows), :] = term.astype(t_ref.dtype)
+
+    @pl.when(b == pl.num_programs(2) - 1)
+    def _():
+        width = t_ref.shape[1]
+        step = 512 if width % 512 == 0 else BLOCK
+        for c0 in range(0, width, step):
+            cols = slice(c0, c0 + step)
+            part = jnp.dot(c_ref[0], t_ref[:, cols], preferred_element_type=jnp.float32)
+
+            @pl.when(l == 0)
+            def _():
+                acc_ref[:, cols] = part
+
+            @pl.when(l > 0)
+            def _():
+                acc_ref[:, cols] += part
+
+        @pl.when(l == pl.num_programs(1) - 1)
+        def _():
+            for c0 in range(0, width, step):
+                cols = slice(c0, c0 + step)
+                o_ref[:, cols] = acc_ref[:, cols].astype(o_ref.dtype)
+
+
+def decode(codes, weights, combine):
+    layers, per_owner, rows, _ = codes.shape
+    width = weights.shape[2]
+    tokens, slot_count = combine.shape[1], combine.shape[2]
+    tile = min(tokens, 1024)
+    return pl.pallas_call(
+        decode_kernel,
+        grid=(tokens // tile, layers, per_owner),
+        in_specs=[
+            pl.BlockSpec((1, 1, rows, BLOCK), lambda t, l, b: (l, b, 0, 0)),
+            pl.BlockSpec((1, BLOCK, width), lambda t, l, b: (l, b, 0)),
+            pl.BlockSpec((1, tile, slot_count), lambda t, l, b: (l, t, 0)),
+        ],
+        out_specs=pl.BlockSpec((tile, width), lambda t, l, b: (t, 0)),
+        out_shape=jax.ShapeDtypeStruct((tokens, width), jnp.bfloat16),
+        scratch_shapes=[
+            pltpu.VMEM((slot_count, width), jnp.bfloat16),
+            pltpu.VMEM((tile, width), jnp.float32),
+        ],
+    )(codes, weights, combine)
 
 
 def pair_slots(ids, per_owner, cap):
@@ -78,25 +131,8 @@
 
     valid = jnp.arange(layers, dtype=jnp.int32) <= layer_index
     combine = (onehot & valid[:, None, None]).astype(jnp.bfloat16)
-    weights = decoder_weight[0].reshape(layers, per_owner, BLOCK, width)
-    chunks = 4 if width % (4 * BLOCK) == 0 else 1
-    step = width // chunks
-    pieces = []
-    for c in range(chunks):
-        terms = jnp.einsum(
-            "lbxe,lbed->lbxd",
-            gathered,
-            weights[..., c * step:(c + 1) * step],
-            preferred_element_type=jnp.float32,
-        ).astype(jnp.bfloat16)
-        partial = jnp.einsum(
-            "ltx,lxd->td",
-            combine,
-            terms.reshape(layers, slot_count, step),
-            preferred_element_type=jnp.float32,
-        ).astype(jnp.bfloat16)
-        pieces.append(lax.psum_scatter(partial, "tok", scatter_dimension=0, tiled=True))
-    summed = jnp.concatenate(pieces, axis=1)
+    partial = decode(gathered, decoder_weight[0], combine)
+    summed = lax.psum_scatter(partial, "tok", scatter_dimension=0, tiled=True)
     recon32 = decoder_bias[0][None, :] + summed.astype(jnp.float32)
     difference = recon32 - targets[0].astype(jnp.float32)
     error = jnp.mean(difference * difference, axis=1)

time: 278 us -> 280 us (level)
  Pallas kernels: 8.03 us -> 84.6 us
  matrix products: 61.7 us -> 8.56 us
  waiting for transfers between devices: 158 us -> 133 us
    pallas_call x0 -> x1, Pallas kernels: none -> 76.5 us  [decode(): pl.pallas_call(decode_kernel, grid=(tokens // tile, layers, per_owner), i...]
    dot_general x8 -> x0, matrix products: 53.1 us -> none  [the longest x4 30.2 us: body(): jnp.einsum('lbxe,lbed->lbxd', gathered, weights[..., c * step:(c + 1) * s...]
    reduce_scatter x4 -> x1, waiting for transfers between devices: 99.1 us -> 76.8 us  [body(): summed = lax.psum_scatter(partial, 'tok', scatter_dimension=0, tiled=True)]
    all_gather x1, waiting for transfers between devices: 58.4 us -> 55.2 us  [body(): res_all = lax.all_gather(residual[0], 'tok', axis=0, tiled=True)]
  transfers between devices with their start and end apart: 5 -> 2, of which waited for: 4 -> 2; matrix products, arithmetic and copies ran while one was open for 16% -> 3% of each run, Pallas kernels for 0% -> 0%
where the time goes in v4:
time: 280 us; the launch traced here: 279 us
  waiting for transfers between devices  133 us (48%)
  Pallas kernels  84.6 us (30%)
  blocking collectives  26.8 us (10%)
  between operations  14.1 us (5%)
  other arithmetic  10 us (4%)
  matrix products  8.56 us (3%)
    reduce_scatter x1, waiting for transfers between devices, body(): summed = lax.psum_scatter(partial, 'tok', scatter_dimension=0, tiled=True)  76.8 us
    pallas_call x1, Pallas kernels, decode(): pl.pallas_call(decode_kernel, grid=(tokens // tile, layers, per_owner), i...  76.5 us
    all_gather x1, waiting for transfers between devices, body(): res_all = lax.all_gather(residual[0], 'tok', axis=0, tiled=True)  55.2 us
    all_gather x1, blocking collectives, body(): codes_all = lax.all_gather(codes_own, 'tok', axis=1, tiled=True)  14.4 us
    all_gather x1, blocking collectives, body(): gathered = lax.all_gather(codes, 'layer', axis=0, tiled=False)  12.4 us
    dot_general x1, matrix products, body(): jnp.einsum('tx,td->xd', own_onehot, res_all, preferred_element_type=jnp.f...  8.56 us
    pallas_call x1, Pallas kernels, encode(): pl.pallas_call(encode_kernel, grid=(per_owner // group,), in_specs=[pl.Bl...  8.03 us
  transfers between devices with their start and end apart: 2, of which 2 were waited for; matrix products, arithmetic and copies ran while one was open for 3% of the time, Pallas kernels for 0%

profile of v4, /device:TPU:0, one launch (start us, length us, event | category | flops | bytes accessed | tf_op | source)
XLA Modules:
  0.0 278.8 jit_solution(2336355443977170651)
XLA Ops:
  7.2 0.0 all-gather.4.cloned.1.call-start
  7.2 0.7 all-gather.4.cloned.1.call-update
  7.9 0.0 reduce-scatter.2.cloned.1.call-start
  7.9 0.8 copy.32
  8.8 0.1 copy.33
  8.9 0.4 convert_reduce_fusion
  9.3 0.1 copy.35
  9.5 0.1 copy.36
  9.5 0.7 fusion.18
  10.2 14.4 %all_gather.12 = s32[4,1024,2]{1,0,2:T(4,128)S(1)} all-gather(s32[4,128,2]{1,0,2:T(4,128)S(1)} %fusion.18), channel_id=1, replica_groups=mesh['layer'=4,'tok'=8] {'tok'}, dimensions={1}, use_global_device_ids=true | all-gather | bytes 36864 | tf_op jit(solution)/shard_map/all_gather | solution.py:116
  24.6 0.1 broadcast_bitcast_fusion
  24.7 0.1 fusion.15
  24.9 2.6 fusion
  27.4 3.2 %and_convert_fusion.c_ref = bf16[4,1024,512]{2,1,0:T(8,128)(2,1)} fusion(pred[4,1024,512]{2,1,0:T(8,128)(4,1)S(1)} %fusion, pred[4]{0:T(512)(128)(4,1)S(1)} %iota_compare_fusion.2), kind=kLoop, calls=%fused_computation.2 | loop fusion | flops 4194304 | bytes 6291460 | tf_op jit(solution)/shard_map/convert_element_type | solution.py:133
  30.6 55.2 %all-gather.4.cloned.1.call-done = bf16[1,1024,3584]{2,1,0:T(8,128)(2,1)} async-done(((bf16[1,128,3584]{2,1,0:T(8,128)(2,1)}), bf16[1,1024,3584]{2,1,0:T(8,128)(2,1)}) %all-gather.4.cloned.1.call-update) | async-done | bytes 7340048 | tf_op jit(solution)/shard_map/all_gather | solution.py:126
  85.8 8.6 %fusion.3 = bf16[512,3584]{1,0:T(8,128)(2,1)} fusion(bf16[1,1024,3584]{2,1,0:T(8,128)(2,1)} %all-gather.4.cloned.1.call-done, pred[4,1024,512]{2,1,0:T(8,128)(4,1)S(1)} %fusion, s32[]{:T(128)S(6)} %select_n.29), kind=kOutput, calls=%fused_computation.5 | convolution fusion | flops 3759931392 | bytes 11534340 | tf_op jit(solution)/shard_map/tx,td->xd/dot_general | solution.py:128
  94.4 8.0 %shard_map.86 = bf16[16,32,128]{2,1,0:T(8,128)(2,1)} custom-call(bf16[16,32,3584]{2,1,0:T(8,128)(2,1)} %bitcast.25, bf16[3584,2048]{1,0:T(8,128)(2,1)} %bitcast.24, f32[1,2048]{1,0:T(1,128)} %b_ref.1), custom_call_target="tpu_custom_call" | custom-call | tf_op jit(solution)/shard_map/pallas_call | solution.py:25
  102.4 12.4 %all-gather.1 = bf16[64,32,128]{2,1,0:T(8,128)(2,1)} all-gather(bf16[16,32,128]{2,1,0:T(8,128)(2,1)} %shard_map.86), channel_id=3, replica_groups=mesh['layer'=4,'tok'=8] {'layer'}, dimensions={0}, use_global_device_ids=true | all-gather | bytes 655360 | tf_op jit(solution)/shard_map/all_gather | solution.py:130
  114.8 76.5 %shard_map.87 = bf16[1024,3584]{1,0:T(8,128)(2,1)} custom-call(bf16[4,16,32,128]{3,2,1,0:T(8,128)(2,1)} %bitcast.26, bf16[4,2048,3584]{2,1,0:T(8,128)(2,1)} %bitcast.23, bf16[4,1024,512]{2,1,0:T(8,128)(2,1)} %and_convert_fusion.c_ref), custom_call_target="tpu_custom_call" | custom-call | tf_op jit(solution)/shard_map/pallas_call | solution.py:73
  191.4 0.0 copy-start.1
  191.4 0.0 copy-start
  191.4 0.0 reduce-scatter.2.cloned.1.call-update
  191.4 0.7 copy-done.1
  192.1 76.8 %reduce-scatter.2.cloned.1.call-done = bf16[128,3584]{1,0:T(8,128)(2,1)} async-done(((bf16[1024,3584]{1,0:T(8,128)(2,1)}), bf16[128,3584]{1,0:T(8,128)(2,1)}) %reduce-scatter.2.cloned.1.call-update) | async-done | bytes 917520 | tf_op jit(solution)/shard_map/reduce_scatter | solution.py:135
  268.9 0.0 copy-done
  268.9 2.5 fusion.9
  271.4 0.5 multiply_bitcast_fusion
  (5 shorter events, 0.1 us)
Async XLA Ops:
  7.2 78.6 %all-gather.4.cloned.1.call-start = ((), (), s32[]{:S(2)}) async-start(), calls=%async_computation.2 | async-start | bytes 8257536 | tf_op jit(solution)/shard_map/all_gather | solution.py:126
  7.9 261.0 %reduce-scatter.2.cloned.1.call-start = ((), (), s32[]{:S(2)}) async-start(), calls=%async_computation.1 | async-start | bytes 8257536 | tf_op jit(solution)/shard_map/reduce_scatter | solution.py:135
  191.4 0.7 copy-start.1
  191.4 77.6 %copy-start = (bf16[1,128,3584]{2,1,0:T(8,128)(2,1)S(1)}, bf16[1,128,3584]{2,1,0:T(8,128)(2,1)}, u32[]{:S(2)}) copy-start(bf16[1,128,3584]{2,1,0:T(8,128)(2,1)} %param.8) | copy-start | bytes 2752516
Sparse Core Ops, SparseCore 0:
  9.6 76.1 all-gather.3
  191.5 77.3 reduce-scatter.1

commit v5 on v3

--- a/solution.py
+++ b/solution.py
@@ -78,25 +78,19 @@
 
     valid = jnp.arange(layers, dtype=jnp.int32) <= layer_index
     combine = (onehot & valid[:, None, None]).astype(jnp.bfloat16)
-    weights = decoder_weight[0].reshape(layers, per_owner, BLOCK, width)
-    chunks = 4 if width % (4 * BLOCK) == 0 else 1
-    step = width // chunks
-    pieces = []
-    for c in range(chunks):
-        terms = jnp.einsum(
-            "lbxe,lbed->lbxd",
-            gathered,
-            weights[..., c * step:(c + 1) * step],
-            preferred_element_type=jnp.float32,
-        ).astype(jnp.bfloat16)
-        partial = jnp.einsum(
-            "ltx,lxd->td",
-            combine,
-            terms.reshape(layers, slot_count, step),
-            preferred_element_type=jnp.float32,
-        ).astype(jnp.bfloat16)
-        pieces.append(lax.psum_scatter(partial, "tok", scatter_dimension=0, tiled=True))
-    summed = jnp.concatenate(pieces, axis=1)
+    terms = jnp.einsum(
+        "lbxe,lbed->lbxd",
+        gathered,
+        decoder_weight[0].reshape(layers, per_owner, BLOCK, width),
+        preferred_element_type=jnp.float32,
+    ).astype(jnp.bfloat16)
+    partial = jnp.einsum(
+        "ltx,lxd->td",
+        combine,
+        terms.reshape(layers, slot_count, width),
+        preferred_element_type=jnp.float32,
+    ).astype(jnp.bfloat16)
+    summed = lax.psum_scatter(partial, "tok", scatter_dimension=0, tiled=True)
     recon32 = decoder_bias[0][None, :] + summed.astype(jnp.float32)
     difference = recon32 - targets[0].astype(jnp.float32)
     error = jnp.mean(difference * difference, axis=1)

time: 278 us -> 248 us (0.89)
  waiting for transfers between devices: 158 us -> 136 us
  matrix products: 61.7 us -> 55.2 us
    reduce_scatter x4 -> x1, waiting for transfers between devices: 99.1 us -> 76.8 us  [body(): summed = lax.psum_scatter(partial, 'tok', scatter_dimension=0, tiled=True)]
    dot_general x8 -> x2, matrix products: 53.1 us -> 46.6 us  [the longest x1 25.9 us: body(): jnp.einsum('lbxe,lbed->lbxd', gathered, decoder_weight[0].reshape(layers,...]
  transfers between devices with their start and end apart: 5 -> 2, of which waited for: 4 -> 2; matrix products, arithmetic and copies ran while one was open for 16% -> 2% of each run, Pallas kernels for 0% -> 0%
where the time goes in v5:
time: 248 us
  waiting for transfers between devices  136 us (55%)
  matrix products  55.2 us (22%)
  blocking collectives  25.6 us (10%)
  between operations  14.1 us (6%)
  Pallas kernels  8.03 us (3%)
  other arithmetic  6.85 us (3%)
    reduce_scatter x1, waiting for transfers between devices, body(): summed = lax.psum_scatter(partial, 'tok', scatter_dimension=0, tiled=True)  76.8 us
    all_gather x1, waiting for transfers between devices, body(): res_all = lax.all_gather(residual[0], 'tok', axis=0, tiled=True)  58.4 us
    dot_general x1, matrix products, body(): jnp.einsum('lbxe,lbed->lbxd', gathered, decoder_weight[0].reshape(layers,...  25.9 us
    dot_general x1, matrix products, body(): jnp.einsum('ltx,lxd->td', combine, terms.reshape(layers, slot_count, widt...  20.7 us
    all_gather x1, blocking collectives, body(): codes_all = lax.all_gather(codes_own, 'tok', axis=1, tiled=True)  14.4 us
    all_gather x1, blocking collectives, body(): gathered = lax.all_gather(codes, 'layer', axis=0, tiled=False)  11.2 us
    dot_general x1, matrix products, body(): jnp.einsum('tx,td->xd', own_onehot, res_all, preferred_element_type=jnp.f...  8.58 us
    pallas_call x1, Pallas kernels, encode(): pl.pallas_call(encode_kernel, grid=(per_owner // group,), in_specs=[pl.Bl...  8.03 us
  transfers between devices with their start and end apart: 2, of which 2 were waited for; matrix products, arithmetic and copies ran while one was open for 2% of the time, Pallas kernels for 0%

profile of v5, /device:TPU:0, one launch (start us, length us, event | category | flops | bytes accessed | tf_op | source)
XLA Modules:
  0.0 247.6 jit_solution(4468655471588676510)
XLA Ops:
  7.2 0.0 all-gather.4.cloned.1.call-start
  7.2 0.7 all-gather.4.cloned.1.call-update
  7.9 0.0 reduce-scatter.2.cloned.1.call-start
  7.9 0.8 copy.32
  8.8 0.1 copy.33
  8.9 0.4 convert_reduce_fusion
  9.3 0.1 copy.35
  9.5 0.1 copy.36
  9.5 0.7 fusion.20
  10.2 14.4 %all_gather.12 = s32[4,1024,2]{1,0,2:T(4,128)S(1)} all-gather(s32[4,128,2]{1,0,2:T(4,128)S(1)} %fusion.20), channel_id=1, replica_groups=mesh['layer'=4,'tok'=8] {'tok'}, dimensions={1}, use_global_device_ids=true | all-gather | bytes 36864 | tf_op jit(solution)/shard_map/all_gather | solution.py:63
  24.6 0.1 broadcast_bitcast_fusion
  24.7 0.1 fusion.17
  24.9 2.6 %fusion = pred[4,1024,512]{2,1,0:T(8,128)(4,1)S(1)} fusion(s32[4,1024,2]{1,2,0:T(2,128)S(1)} %copy.37), kind=kLoop, calls=%fused_computation.1 | loop fusion | flops 6291456 | bytes 2129920 | tf_op jit(solution)/shard_map/reduce_or | solution.py:71
  27.4 58.4 %all-gather.4.cloned.1.call-done = bf16[1,1024,3584]{2,1,0:T(8,128)(2,1)} async-done(((bf16[1,128,3584]{2,1,0:T(8,128)(2,1)}), bf16[1,1024,3584]{2,1,0:T(8,128)(2,1)}) %all-gather.4.cloned.1.call-update) | async-done | bytes 7340048 | tf_op jit(solution)/shard_map/all_gather | solution.py:73
  85.8 8.6 %fusion.4 = bf16[512,3584]{1,0:T(8,128)(2,1)} fusion(bf16[1,1024,3584]{2,1,0:T(8,128)(2,1)} %all-gather.4.cloned.1.call-done, pred[4,1024,512]{2,1,0:T(8,128)(4,1)S(1)} %fusion, s32[]{:T(128)S(6)} %select_n.29), kind=kOutput, calls=%fused_computation.7 | convolution fusion | flops 3759931392 | bytes 11534340 | tf_op jit(solution)/shard_map/tx,td->xd/dot_general | solution.py:75
  94.4 8.0 %shard_map.86 = bf16[16,32,128]{2,1,0:T(8,128)(2,1)} custom-call(bf16[16,32,3584]{2,1,0:T(8,128)(2,1)} %bitcast.32, bf16[3584,2048]{1,0:T(8,128)(2,1)} %bitcast.31, f32[1,2048]{1,0:T(1,128)} %b_ref.1), custom_call_target="tpu_custom_call" | custom-call | tf_op jit(solution)/shard_map/pallas_call | solution.py:24
  102.4 11.2 %all-gather.1 = bf16[64,32,128]{2,1,0:T(8,128)(2,1)S(1)} all-gather(bf16[16,32,128]{2,1,0:T(8,128)(2,1)} %shard_map.86), channel_id=3, replica_groups=mesh['layer'=4,'tok'=8] {'layer'}, dimensions={0}, use_global_device_ids=true | all-gather | bytes 655360 | tf_op jit(solution)/shard_map/all_gather | solution.py:77
  113.6 25.9 %convolution_convert_fusion = bf16[4,16,32,3584]{3,2,1,0:T(8,128)(2,1)} fusion(bf16[4,16,32,128]{3,2,1,0:T(8,128)(2,1)S(1)} %bitcast.33, bf16[4,16,128,3584]{3,2,1,0:T(8,128)(2,1)} %bitcast.29), kind=kOutput, calls=%fused_computation.3 | convolution fusion | flops 1886388224 | bytes 73924608 | tf_op jit(solution)/shard_map/lbxe,lbed->lbxd/dot_general | solution.py:81
  139.5 20.7 %bitcast_convert_fusion = bf16[1024,3584]{1,0:T(8,128)(2,1)} fusion(bf16[4,512,3584]{2,1,0:T(8,128)(2,1)} %bitcast.30, pred[4,1024,512]{2,1,0:T(8,128)(4,1)S(1)} %fusion, pred[4]{0:T(512)(128)(4,1)S(1)} %iota_compare_fusion.2), kind=kOutput, calls=%fused_computation.2 | convolution fusion | flops 15038152704 | bytes 24117252 | tf_op jit(solution)/shard_map/ltx,lxd->td/dot_general | solution.py:87
  160.2 0.0 copy-start.1
  160.2 0.0 copy-start
  160.2 0.0 reduce-scatter.2.cloned.1.call-update
  160.3 0.7 copy-done.1
  161.0 76.8 %reduce-scatter.2.cloned.1.call-done = bf16[128,3584]{1,0:T(8,128)(2,1)} async-done(((bf16[1024,3584]{1,0:T(8,128)(2,1)}), bf16[128,3584]{1,0:T(8,128)(2,1)}) %reduce-scatter.2.cloned.1.call-update) | async-done | bytes 917520 | tf_op jit(solution)/shard_map/reduce_scatter | solution.py:93
  237.8 0.0 copy-done
  237.8 2.5 %fusion.11 = (f32[128]{0:T(128)S(1)}, bf16[1,128,3584]{2,1,0:T(8,128)(2,1)}) fusion(bf16[128,3584]{1,0:T(8,128)(2,1)} %reduce-scatter.2.cloned.1.call-done, bf16[1,128,3584]{2,1,0:T(8,128)(2,1)S(1)} %copy-done, f32[3584]{0:T(1024)S(1)} %reduce), kind=kLoop, calls=%fused_computation.13 | loop fusion | flops 3211136 | bytes 2767360 | tf_op jit(solution)/shard_map/reduce_sum | solution.py:96
  240.3 0.5 multiply_bitcast_fusion
  (5 shorter events, 0.1 us)
Async XLA Ops:
  7.2 78.6 %all-gather.4.cloned.1.call-start = ((), (), s32[]{:S(2)}) async-start(), calls=%async_computation.2 | async-start | bytes 8257536 | tf_op jit(solution)/shard_map/all_gather | solution.py:73
  7.9 229.9 %reduce-scatter.2.cloned.1.call-start = ((), (), s32[]{:S(2)}) async-start(), calls=%async_computation.1 | async-start | bytes 8257536 | tf_op jit(solution)/shard_map/reduce_scatter | solution.py:93
  160.2 0.7 copy-start.1
  160.2 77.6 %copy-start = (bf16[1,128,3584]{2,1,0:T(8,128)(2,1)S(1)}, bf16[1,128,3584]{2,1,0:T(8,128)(2,1)}, u32[]{:S(2)}) copy-start(bf16[1,128,3584]{2,1,0:T(8,128)(2,1)} %param.8) | copy-start | bytes 2752516
Sparse Core Ops, SparseCore 0:
  9.6 76.1 all-gather.3
  160.4 77.3 reduce-scatter.1

commit v6 on v5

--- a/solution.py
+++ b/solution.py
@@ -74,22 +74,33 @@
     own_onehot = lax.dynamic_index_in_dim(onehot, layer_index, 0, keepdims=False).astype(jnp.bfloat16)
     rows = jnp.einsum("tx,td->xd", own_onehot, res_all, preferred_element_type=jnp.float32).astype(jnp.bfloat16)
     codes = encode(rows.reshape(per_owner, tok_count * cap, width), encoder_weight[0], encoder_bias[0].reshape(1, -1))
-    gathered = lax.all_gather(codes, "layer", axis=0, tiled=False)
+    received = [codes] + [
+        lax.ppermute(codes, "layer", [(i, i + shift) for i in range(layers - shift)])
+        for shift in range(1, layers)
+    ]
+    shifts = (layer_index - jnp.arange(layers, dtype=jnp.int32)) % layers
+    gathered = jnp.take(jnp.stack(received), shifts, axis=0)
 
     valid = jnp.arange(layers, dtype=jnp.int32) <= layer_index
-    combine = (onehot & valid[:, None, None]).astype(jnp.bfloat16)
     terms = jnp.einsum(
         "lbxe,lbed->lbxd",
         gathered,
         decoder_weight[0].reshape(layers, per_owner, BLOCK, width),
         preferred_element_type=jnp.float32,
     ).astype(jnp.bfloat16)
+    halves = 2 if (tok_count % 2 == 0 and (tok_count // 2) * cap % 16 == 0) else 1
+    rows_half = tok_count * cap // halves
+    used = (slot_of < slot_count) & valid[:, None, None]
+    block_hit = (slot_of // (tok_count * cap))[..., None] == jnp.arange(per_owner, dtype=jnp.int32)
+    row_hit = (slot_of % rows_half)[..., None] == jnp.arange(rows_half, dtype=jnp.int32)
+    combine = jnp.any(block_hit[..., :, None] & row_hit[..., None, :] & used[..., None, None], axis=2)
+    combine = combine.astype(jnp.bfloat16).reshape(layers, halves, tokens // halves, per_owner, rows_half)
     partial = jnp.einsum(
-        "ltx,lxd->td",
+        "lgtbx,lbgxd->gtd",
         combine,
-        terms.reshape(layers, slot_count, width),
+        terms.reshape(layers, per_owner, halves, rows_half, width),
         preferred_element_type=jnp.float32,
-    ).astype(jnp.bfloat16)
+    ).reshape(tokens, width).astype(jnp.bfloat16)
     summed = lax.psum_scatter(partial, "tok", scatter_dimension=0, tiled=True)
     recon32 = decoder_bias[0][None, :] + summed.astype(jnp.float32)
     difference = recon32 - targets[0].astype(jnp.float32)

time: 248 us -> 245 us (0.988)
  blocking collectives: 25.6 us -> 14.4 us
  starting transfers between devices: 0.08 us -> 8.3 us
  matrix products: 55.2 us -> 49.6 us
  other arithmetic: 6.85 us -> 9.65 us
  local copies, waits for them, and re-layouts: 1.92 us -> 4.53 us
    all_gather x1 -> x0, blocking collectives: 11.2 us -> none  [body(): gathered = lax.all_gather(codes, 'layer', axis=0, tiled=False)]
    ppermute x0 -> x3, starting transfers between devices: none -> 8.22 us  [body(): lax.ppermute(codes, 'layer', [(i, i + shift) for i in range(layers - shif...]
    dot_general x1, matrix products: 20.7 us -> 15.1 us  [body(): jnp.einsum('lgtbx,lbgxd->gtd', combine, terms.reshape(layers, per_owner,...]
  transfers between devices with their start and end apart: 2 -> 5, of which waited for: 2 -> 4; matrix products, arithmetic and copies ran while one was open for 2% -> 4% of each run, Pallas kernels for 0% -> 0%
where the time goes in v6:
time: 245 us
  waiting for transfers between devices  136 us (56%)
  matrix products  49.6 us (20%)
  blocking collectives  14.4 us (6%)
  between operations  14.2 us (6%)
  other arithmetic  9.65 us (4%)
  starting transfers between devices  8.3 us (3%)
  Pallas kernels  8.03 us (3%)
  local copies, waits for them, and re-layouts  4.53 us (2%)
    reduce_scatter x1, waiting for transfers between devices, body(): summed = lax.psum_scatter(partial, 'tok', scatter_dimension=0, tiled=True)  77.9 us
    all_gather x1, waiting for transfers between devices, body(): res_all = lax.all_gather(residual[0], 'tok', axis=0, tiled=True)  56.4 us
    dot_general x1, matrix products, body(): jnp.einsum('lbxe,lbed->lbxd', gathered, decoder_weight[0].reshape(layers,...  26 us
    dot_general x1, matrix products, body(): jnp.einsum('lgtbx,lbgxd->gtd', combine, terms.reshape(layers, per_owner,...  15.1 us
    all_gather x1, blocking collectives, body(): codes_all = lax.all_gather(codes_own, 'tok', axis=1, tiled=True)  14.4 us
    dot_general x1, matrix products, body(): jnp.einsum('tx,td->xd', own_onehot, res_all, preferred_element_type=jnp.f...  8.58 us
    ppermute x3, starting transfers between devices, body(): lax.ppermute(codes, 'layer', [(i, i + shift) for i in range(layers - shif...  8.22 us
    pallas_call x1, Pallas kernels, encode(): pl.pallas_call(encode_kernel, grid=(per_owner // group,), in_specs=[pl.Bl...  8.03 us
  transfers between devices with their start and end apart: 5, of which 4 were waited for; matrix products, arithmetic and copies ran while one was open for 4% of the time, Pallas kernels for 0%

profile of v6, /device:TPU:0, one launch (start us, length us, event | category | flops | bytes accessed | tf_op | source)
XLA Modules:
  0.0 244.9 jit_solution(1120910023749867577)
XLA Ops:
  7.2 0.7 all-gather.3.cloned.1.call-update
  7.9 0.0 reduce-scatter.2.cloned.1.call-start
  7.9 0.8 copy.51
  8.8 0.1 copy.52
  8.9 0.4 convert_reduce_fusion
  9.3 0.1 copy.54
  9.5 0.1 copy.55
  9.5 0.7 fusion.28
  10.2 14.4 %all_gather.6 = s32[4,1024,2]{1,0,2:T(4,128)S(1)} all-gather(s32[4,128,2]{1,0,2:T(4,128)S(1)} %fusion.28), channel_id=1, replica_groups=mesh['layer'=4,'tok'=8] {'tok'}, dimensions={1}, use_global_device_ids=true | all-gather | bytes 36864 | tf_op jit(solution)/shard_map/all_gather | solution.py:63
  24.6 0.1 broadcast_bitcast_fusion
  24.7 0.1 add_select_fusion.1
  24.9 0.1 compare_and_fusion
  25.1 0.1 iota_compare_fusion.1
  25.3 1.5 and_reduce_fusion
  26.8 2.6 %fusion = pred[4,1024,512]{2,1,0:T(8,128)(4,1)S(1)} fusion(s32[4,1024,2]{1,2,0:T(2,128)S(1)} %copy.59), kind=kLoop, calls=%fused_computation.2 | loop fusion | flops 6291456 | bytes 2129920 | tf_op jit(solution)/shard_map/reduce_or | solution.py:71
  29.4 56.4 %all-gather.3.cloned.1.call-done = bf16[1,1024,3584]{2,1,0:T(8,128)(2,1)} async-done(((bf16[1,128,3584]{2,1,0:T(8,128)(2,1)}), bf16[1,1024,3584]{2,1,0:T(8,128)(2,1)}) %all-gather.3.cloned.1.call-update) | async-done | bytes 7340048 | tf_op jit(solution)/shard_map/all_gather | solution.py:73
  85.8 8.6 %fusion.7 = bf16[512,3584]{1,0:T(8,128)(2,1)} fusion(bf16[1,1024,3584]{2,1,0:T(8,128)(2,1)} %all-gather.3.cloned.1.call-done, pred[4,1024,512]{2,1,0:T(8,128)(4,1)S(1)} %fusion, s32[]{:T(128)S(6)} %select_n.84), kind=kOutput, calls=%fused_computation.10 | convolution fusion | flops 3759931392 | bytes 11534340 | tf_op jit(solution)/shard_map/tx,td->xd/dot_general | solution.py:75
  94.4 8.0 %shard_map.86 = bf16[16,32,128]{2,1,0:T(8,128)(2,1)} custom-call(bf16[16,32,3584]{2,1,0:T(8,128)(2,1)} %bitcast.43, bf16[3584,2048]{1,0:T(8,128)(2,1)} %bitcast.41, f32[1,2048]{1,0:T(1,128)} %b_ref.1), custom_call_target="tpu_custom_call" | custom-call | tf_op jit(solution)/shard_map/pallas_call | solution.py:24
  102.4 4.3 %collective-permute-start.2 = (bf16[16,32,128]{2,1,0:T(8,128)(2,1)}, bf16[16,32,128]{2,1,0:T(8,128)(2,1)S(1)}, u32[]{:S(2)}, u32[]{:S(2)}) collective-permute-start(bf16[16,32,128]{2,1,0:T(8,128)(2,1)} %shard_map.86), channel_id=1, source_target_pairs={{0,24},{1,25},{2,26},{3,27},{4,28},{5,29},{6,30},{7,31}} | collective-permute-start | bytes 393224 | tf_op jit(solution)/shard_map/ppermute | solution.py:78
  106.7 1.3 collective-permute-start
  108.0 2.6 %collective-permute-start.1 = (bf16[16,32,128]{2,1,0:T(8,128)(2,1)}, bf16[16,32,128]{2,1,0:T(8,128)(2,1)S(1)}, u32[]{:S(2)}, u32[]{:S(2)}) collective-permute-start(bf16[16,32,128]{2,1,0:T(8,128)(2,1)} %shard_map.86), channel_id=1, source_target_pairs={{0,16},{8,24},{1,17},{9,25},{2,18},{10,26},{3,19},{11,27},{4,20},{... | collective-permute-start | bytes 393224 | tf_op jit(solution)/shard_map/ppermute | solution.py:78
  110.7 1.9 reshape.155
  112.6 0.4 collective-permute-done
  113.0 0.7 collective-permute-done.1
  113.7 1.0 pad_maximum_fusion
  114.6 0.6 gather_fusion
  115.3 26.0 %convolution_convert_fusion = bf16[4,16,32,3584]{3,2,1,0:T(8,128)(2,1)} fusion(bf16[4,16,128,3584]{3,2,1,0:T(8,128)(2,1)} %bitcast.39, bf16[4,16,32,128]{3,2,1,0:T(8,128)(2,1)S(1)} %gather_fusion, pred[4]{0:T(512)(128)(4,1)S(1)} %compare_and_fusion.1), kind=kOutput, calls=%fused_computation.6 | convolution fusion | flops 1886650368 | bytes 73924608 | tf_op jit(solution)/shard_map/lbxe,lbed->lbxd/dot_general | solution.py:85
  141.2 15.1 %bitcast_convert_fusion = bf16[2,512,3584]{2,1,0:T(8,128)(2,1)} fusion(bf16[4,16,2,16,3584]{4,3,2,1,0:T(8,128)(2,1)} %bitcast.40, pred[4,2,512,16,16]{2,1,4,3,0:T(4,128)(4,1)S(1)} %reshape.155), kind=kOutput, calls=%fused_computation.3 | convolution fusion | flops 7519862784 | bytes 23068672 | tf_op jit(solution)/shard_map/lgtbx,lbgxd->gtd/dot_general | solution.py:98
  156.4 0.7 copy-done.1
  157.1 77.9 %reduce-scatter.2.cloned.1.call-done = bf16[128,3584]{1,0:T(8,128)(2,1)} async-done(((bf16[1024,3584]{1,0:T(8,128)(2,1)}), bf16[128,3584]{1,0:T(8,128)(2,1)}) %reduce-scatter.2.cloned.1.call-update) | async-done | bytes 917520 | tf_op jit(solution)/shard_map/reduce_scatter | solution.py:104
  235.0 2.5 %fusion.14 = (f32[128]{0:T(128)S(1)}, bf16[1,128,3584]{2,1,0:T(8,128)(2,1)}) fusion(bf16[128,3584]{1,0:T(8,128)(2,1)} %reduce-scatter.2.cloned.1.call-done, bf16[1,128,3584]{2,1,0:T(8,128)(2,1)S(1)} %copy-done, f32[3584]{0:T(1024)S(1)} %reduce), kind=kLoop, calls=%fused_computation.16 | loop fusion | flops 3211136 | bytes 2767360 | tf_op jit(solution)/shard_map/reduce_sum | solution.py:107
  237.5 0.5 multiply_bitcast_fusion
  (18 shorter events, 0.3 us)
Async XLA Ops:
  7.2 78.6 %all-gather.3.cloned.1.call-start = ((), (), s32[]{:S(2)}) async-start(), calls=%async_computation.2 | async-start | bytes 8257536 | tf_op jit(solution)/shard_map/all_gather | solution.py:73
  7.9 227.1 %reduce-scatter.2.cloned.1.call-start = ((), (), s32[]{:S(2)}) async-start(), calls=%async_computation.1 | async-start | bytes 8257536 | tf_op jit(solution)/shard_map/reduce_scatter | solution.py:104
  102.4 10.2 %collective-permute-start.2 = (bf16[16,32,128]{2,1,0:T(8,128)(2,1)}, bf16[16,32,128]{2,1,0:T(8,128)(2,1)S(1)}, u32[]{:S(2)}, u32[]{:S(2)}) collective-permute-start(bf16[16,32,128]{2,1,0:T(8,128)(2,1)} %shard_map.86), channel_id=1, source_target_pairs={{0,24},{1,25},{2,26},{3,27},{4,28},{5,29},{6,30},{7,31}} | collective-permute-start | bytes 393224 | tf_op jit(solution)/shard_map/ppermute | solution.py:78
  106.7 6.3 %collective-permute-start = (bf16[16,32,128]{2,1,0:T(8,128)(2,1)}, bf16[16,32,128]{2,1,0:T(8,128)(2,1)S(1)}, u32[]{:S(2)}, u32[]{:S(2)}) collective-permute-start(bf16[16,32,128]{2,1,0:T(8,128)(2,1)} %shard_map.86), channel_id=1, source_target_pairs={{0,8},{8,16},{16,24},{1,9},{9,17},{17,25},{2,10},{10,18},{18,26},{... | collective-permute-start | bytes 393224 | tf_op jit(solution)/shard_map/ppermute | solution.py:78
  108.0 5.6 %collective-permute-start.1 = (bf16[16,32,128]{2,1,0:T(8,128)(2,1)}, bf16[16,32,128]{2,1,0:T(8,128)(2,1)S(1)}, u32[]{:S(2)}, u32[]{:S(2)}) collective-permute-start(bf16[16,32,128]{2,1,0:T(8,128)(2,1)} %shard_map.86), channel_id=1, source_target_pairs={{0,16},{8,24},{1,17},{9,25},{2,18},{10,26},{3,19},{11,27},{4,20},{... | collective-permute-start | bytes 393224 | tf_op jit(solution)/shard_map/ppermute | solution.py:78
  156.3 0.7 copy-start.1
  156.3 78.7 %copy-start = (bf16[1,128,3584]{2,1,0:T(8,128)(2,1)S(1)}, bf16[1,128,3584]{2,1,0:T(8,128)(2,1)}, u32[]{:S(2)}) copy-start(bf16[1,128,3584]{2,1,0:T(8,128)(2,1)} %param.8) | copy-start | bytes 2752516
Sparse Core Ops, SparseCore 0:
  9.6 76.1 all-gather.2
  156.5 78.4 reduce-scatter.1

commit v7 on v6

--- a/solution.py
+++ b/solution.py
@@ -32,6 +32,32 @@
         out_specs=pl.BlockSpec((group, capacity, BLOCK), lambda g: (g, 0, 0)),
         out_shape=jax.ShapeDtypeStruct((per_owner, capacity, BLOCK), jnp.bfloat16),
     )(rows, weight, bias)
+
+
+def line_reduce_scatter(partial, tok_index, tok_count):
+    chips = tok_count // 2
+    rows = partial.shape[0] // tok_count
+    chip = tok_index // 2
+    core = tok_index % 2
+    blocks = partial.reshape(chips, 2, rows, partial.shape[1])
+    mine = lax.dynamic_index_in_dim(blocks, core, 1, keepdims=False)
+    other = lax.dynamic_index_in_dim(blocks, 1 - core, 1, keepdims=False).astype(jnp.bfloat16)
+    swapped = lax.ppermute(other, "tok", [(i, i ^ 1) for i in range(tok_count)])
+    q = mine + swapped.astype(jnp.float32)
+    right = jnp.zeros(q.shape[1:], jnp.float32)
+    left = jnp.zeros(q.shape[1:], jnp.float32)
+    for r in range(1, chips):
+        d = jnp.clip(chip + chips - r, 0, chips - 1)
+        send = (lax.dynamic_index_in_dim(q, d, 0, keepdims=False) + right).astype(jnp.bfloat16)
+        e = jnp.clip(chip - (chips - r), 0, chips - 1)
+        send_left = (lax.dynamic_index_in_dim(q, e, 0, keepdims=False) + left).astype(jnp.bfloat16)
+        right = lax.ppermute(
+            send, "tok", [(2 * c + k, 2 * (c + 1) + k) for c in range(r) for k in range(2)]
+        ).astype(jnp.float32)
+        left = lax.ppermute(
+            send_left, "tok", [(2 * c + k, 2 * (c - 1) + k) for c in range(chips - r, chips) for k in range(2)]
+        ).astype(jnp.float32)
+    return lax.dynamic_index_in_dim(q, chip, 0, keepdims=False) + right + left
 
 
 def pair_slots(ids, per_owner, cap):
@@ -100,8 +126,11 @@
         combine,
         terms.reshape(layers, per_owner, halves, rows_half, width),
         preferred_element_type=jnp.float32,
-    ).reshape(tokens, width).astype(jnp.bfloat16)
-    summed = lax.psum_scatter(partial, "tok", scatter_dimension=0, tiled=True)
+    ).reshape(tokens, width)
+    if tok_count % 2 == 0 and tok_count <= 8:
+        summed = line_reduce_scatter(partial, tok_index, tok_count)
+    else:
+        summed = lax.psum_scatter(partial.astype(jnp.bfloat16), "tok", scatter_dimension=0, tiled=True)
     recon32 = decoder_bias[0][None, :] + summed.astype(jnp.float32)
     difference = recon32 - targets[0].astype(jnp.float32)
     error = jnp.mean(difference * difference, axis=1)

time: 245 us -> 289 us (1.18)
  starting transfers between devices: 8.3 us -> 23.9 us
  other arithmetic: 9.65 us -> 24.1 us
  local copies, waits for them, and re-layouts: 4.53 us -> 12.3 us
  waiting for transfers between devices: 136 us -> 141 us
    ppermute x0 -> x7, waiting for transfers between devices: none -> 82.8 us  [the longest x3 51.2 us: line_reduce_scatter(): lax.ppermute(send, 'tok', [(2 * c + k, 2 * (c + 1) + k) for c in range(r)...]
    reduce_scatter x1 -> x0, waiting for transfers between devices: 77.9 us -> none  [body(): summed = lax.psum_scatter(partial, 'tok', scatter_dimension=0, tiled=True)]
    ppermute x0 -> x7, starting transfers between devices: none -> 15.6 us  [the longest x3 11.9 us: line_reduce_scatter(): lax.ppermute(send, 'tok', [(2 * c + k, 2 * (c + 1) + k) for c in range(r)...]
    convert_element_type x0 -> x3, other arithmetic: none -> 8.46 us  [the longest x2 5.6 us: line_reduce_scatter(): (lax.dynamic_index_in_dim(q, d, 0, keepdims=False) + right).astype(jnp.bf...]
    convert_element_type x0 -> x2, local copies, waits for them, and re-layouts: none -> 5.49 us  [the longest x1 5.31 us: line_reduce_scatter(): lax.dynamic_index_in_dim(blocks, 1 - core, 1, keepdims=False)]
    add x0 -> x1, other arithmetic: none -> 5.21 us  [line_reduce_scatter(): q = mine + swapped.astype(jnp.float32)]
  transfers between devices with their start and end apart: 5 -> 11, of which waited for: 4 -> 8; matrix products, arithmetic and copies ran while one was open for 4% -> 5% of each run, Pallas kernels for 0% -> 0%
where the time goes in v7:
time: 289 us
  waiting for transfers between devices  141 us (49%)
  matrix products  50.7 us (18%)
  other arithmetic  24.1 us (8%)
  starting transfers between devices  23.9 us (8%)
  blocking collectives  14.4 us (5%)
  between operations  14.3 us (5%)
  local copies, waits for them, and re-layouts  12.3 us (4%)
  Pallas kernels  8.03 us (3%)
    all_gather x1, waiting for transfers between devices, body(): res_all = lax.all_gather(residual[0], 'tok', axis=0, tiled=True)  56.5 us
    ppermute x3, waiting for transfers between devices, line_reduce_scatter(): lax.ppermute(send, 'tok', [(2 * c + k, 2 * (c + 1) + k) for c in range(r)...  51.2 us
    dot_general x1, matrix products, body(): jnp.einsum('lbxe,lbed->lbxd', gathered, decoder_weight[0].reshape(layers,...  25.9 us
    ppermute x3, waiting for transfers between devices, line_reduce_scatter(): lax.ppermute(send_left, 'tok', [(2 * c + k, 2 * (c - 1) + k) for c in ran...  24.9 us
    dot_general x1, matrix products, body(): jnp.einsum('lgtbx,lbgxd->gtd', combine, terms.reshape(layers, per_owner,...  16.2 us
    all_gather x1, blocking collectives, body(): codes_all = lax.all_gather(codes_own, 'tok', axis=1, tiled=True)  14.4 us
    ppermute x3, starting transfers between devices, line_reduce_scatter(): lax.ppermute(send, 'tok', [(2 * c + k, 2 * (c + 1) + k) for c in range(r)...  11.9 us
    dot_general x1, matrix products, body(): jnp.einsum('tx,td->xd', own_onehot, res_all, preferred_element_type=jnp.f...  8.58 us
  transfers between devices with their start and end apart: 11, of which 8 were waited for; matrix products, arithmetic and copies ran while one was open for 5% of the time, Pallas kernels for 0%

profile of v7, /device:TPU:0, one launch (start us, length us, event | category | flops | bytes accessed | tf_op | source)
XLA Modules:
  0.0 288.7 jit_solution(4387520094805522853)
XLA Ops:
  7.9 0.8 copy.55
  9.5 0.7 fusion.33
  10.2 14.4 %all_gather.6 = s32[4,1024,2]{1,0,2:T(4,128)S(1)} all-gather(s32[4,128,2]{1,0,2:T(4,128)S(1)} %fusion.33), channel_id=1, replica_groups=mesh['layer'=4,'tok'=8] {'tok'}, dimensions={1}, use_global_device_ids=true | all-gather | bytes 36864 | tf_op jit(solution)/shard_map/all_gather | solution.py:89
  25.2 1.5 and_reduce_fusion
  26.7 2.6 fusion
  29.3 56.5 %all-gather.3.cloned.1.call-done = bf16[1,1024,3584]{2,1,0:T(8,128)(2,1)} async-done(((bf16[1,128,3584]{2,1,0:T(8,128)(2,1)}), bf16[1,1024,3584]{2,1,0:T(8,128)(2,1)}) %all-gather.3.cloned.1.call-update) | async-done | bytes 7340048 | tf_op jit(solution)/shard_map/all_gather | solution.py:99
  85.8 8.6 %fusion.5 = bf16[512,3584]{1,0:T(8,128)(2,1)} fusion(bf16[1,1024,3584]{2,1,0:T(8,128)(2,1)} %all-gather.3.cloned.1.call-done, pred[4,1024,512]{2,1,0:T(8,128)(4,1)S(1)} %fusion, s32[]{:T(128)S(6)} %select_n.111), kind=kOutput, calls=%fused_computation.11 | convolution fusion | flops 3759931392 | bytes 11534340 | tf_op jit(solution)/shard_map/tx,td->xd/dot_general | solution.py:101
  94.4 8.0 %shard_map.86 = bf16[16,32,128]{2,1,0:T(8,128)(2,1)} custom-call(bf16[16,32,3584]{2,1,0:T(8,128)(2,1)} %bitcast.82, bf16[3584,2048]{1,0:T(8,128)(2,1)} %bitcast.79, f32[1,2048]{1,0:T(1,128)} %b_ref.1), custom_call_target="tpu_custom_call" | custom-call | tf_op jit(solution)/shard_map/pallas_call | solution.py:24
  102.4 4.3 %collective-permute-start.2 = (bf16[16,32,128]{2,1,0:T(8,128)(2,1)}, bf16[16,32,128]{2,1,0:T(8,128)(2,1)S(1)}, u32[]{:S(2)}, u32[]{:S(2)}) collective-permute-start(bf16[16,32,128]{2,1,0:T(8,128)(2,1)} %shard_map.86), channel_id=1, source_target_pairs={{0,24},{1,25},{2,26},{3,27},{4,28},{5,29},{6,30},{7,31}} | collective-permute-start | bytes 393224 | tf_op jit(solution)/shard_map/ppermute | solution.py:104
  106.7 1.3 collective-permute-start
  108.0 2.6 collective-permute-start.1
  110.7 1.9 reshape.156
  113.7 1.0 pad_maximum_fusion
  115.3 25.9 %convolution_convert_fusion = bf16[4,16,32,3584]{3,2,1,0:T(8,128)(2,1)} fusion(bf16[4,16,128,3584]{3,2,1,0:T(8,128)(2,1)} %bitcast.77, bf16[4,16,32,128]{3,2,1,0:T(8,128)(2,1)S(1)} %gather_fusion, pred[4]{0:T(512)(128)(4,1)S(1)} %compare_and_fusion.1), kind=kOutput, calls=%fused_computation.5 | convolution fusion | flops 1886650368 | bytes 73924608 | tf_op jit(solution)/shard_map/lbxe,lbed->lbxd/dot_general | solution.py:111
  141.1 16.2 %fusion.1 = f32[2,512,3584,1,1]{2,1,4,3,0:T(8,128)} fusion(bf16[4,16,2,16,3584]{4,3,2,1,0:T(8,128)(2,1)} %bitcast.78, pred[4,2,512,16,16]{2,1,4,3,0:T(4,128)(4,1)S(1)} %reshape.156), kind=kOutput, calls=%fused_computation.3 | convolution fusion | flops 7516192768 | bytes 30408704 | tf_op jit(solution)/shard_map/lgtbx,lbgxd->gtd/dot_general | solution.py:124
  157.4 5.3 %fusion.9 = bf16[4,128,3584]{2,1,0:T(8,128)(2,1)} fusion(f32[4,2,128,3584]{3,2,1,0:T(8,128)} %bitcast.80, s32[]{:T(128)S(6)} %select_n.117), kind=kLoop, calls=%fused_computation.13 | loop fusion | bytes 7340036 | tf_op jit(solution)/shard_map/convert_element_type | solution.py:44
  162.7 6.7 %collective-permute-done.3 = bf16[4,128,3584]{2,1,0:T(8,128)(2,1)} collective-permute-done((bf16[4,128,3584]{2,1,0:T(8,128)(2,1)}, bf16[4,128,3584]{2,1,0:T(8,128)(2,1)}, u32[]{:S(2)}, u32[]{:S(2)}) %collective-permute-start.3) | collective-permute-done | bytes 3670048 | tf_op jit(solution)/shard_map/ppermute | solution.py:45
  169.4 5.2 %bitcast_add_fusion = f32[4,128,3584]{2,1,0:T(8,128)S(1)} fusion(bf16[4,128,3584]{2,1,0:T(8,128)(2,1)} %collective-permute-done.3, f32[4,2,128,3584]{3,2,1,0:T(8,128)} %bitcast.81, s32[]{:T(128)S(6)} %select_n.116), kind=kLoop, calls=%fused_computation.8 | loop fusion | flops 3670016 | bytes 18350084 | tf_op jit(solution)/shard_map/add | solution.py:46
  174.7 2.9 %copy-done = f32[4,128,3584]{2,1,0:T(8,128)} copy-done((f32[4,128,3584]{2,1,0:T(8,128)}, f32[4,128,3584]{2,1,0:T(8,128)S(1)}, u32[]{:S(2)}) %copy-start) | copy-done | bytes 7340056
  177.8 2.2 collective-permute-start.4
  180.7 18.5 %collective-permute-done.4 = bf16[128,3584]{1,0:T(8,128)(2,1)} collective-permute-done((bf16[128,3584]{1,0:T(8,128)(2,1)S(1)}, bf16[128,3584]{1,0:T(8,128)(2,1)}, u32[]{:S(2)}, u32[]{:S(2)}) %collective-permute-start.4) | collective-permute-done | bytes 917536 | tf_op jit(solution)/shard_map/ppermute | solution.py:54
  199.3 1.9 fusion.16
  201.2 5.4 %collective-permute-start.5 = (bf16[128,3584]{1,0:T(8,128)(2,1)S(1)}, bf16[128,3584]{1,0:T(8,128)(2,1)}, u32[]{:S(2)}, u32[]{:S(2)}) collective-permute-start(bf16[128,3584]{1,0:T(8,128)(2,1)S(1)} %fusion.16), channel_id=1, source_target_pairs={{0,2},{1,3},{2,4},{3,5},{8,10},{9,11},{10,12},{11,13},{16,18},{17,... | collective-permute-start | bytes 2752520 | tf_op jit(solution)/shard_map/ppermute | solution.py:54
  206.6 18.4 %collective-permute-done.5 = bf16[128,3584]{1,0:T(8,128)(2,1)} collective-permute-done((bf16[128,3584]{1,0:T(8,128)(2,1)S(1)}, bf16[128,3584]{1,0:T(8,128)(2,1)}, u32[]{:S(2)}, u32[]{:S(2)}) %collective-permute-start.5) | collective-permute-done | bytes 917536 | tf_op jit(solution)/shard_map/ppermute | solution.py:54
  225.1 3.7 %fusion.17 = (bf16[128,3584]{1,0:T(8,128)(2,1)S(1)}, bf16[128,3584]{1,0:T(8,128)(2,1)}) fusion(bf16[128,3584]{1,0:T(8,128)(2,1)} %collective-permute-done.5, f32[4,128,3584]{2,1,0:T(8,128)} %copy-done, s32[]{:T(128)S(6)} %min.19, bf16[128,3584]{1,0:T(8,128)(2,1)S(1)} %collective-permute-done.7, s32[]{:T(128)S(6)} %min.23), kind=kLoop, calls=%fused_computation.26 | loop fusion | flops 2752512 | bytes 7340040 | tf_op jit(solution)/shard_map/convert_element_type | solution.py:51
  228.8 1.7 collective-permute-start.8
  230.5 4.3 %collective-permute-start.6 = (bf16[128,3584]{1,0:T(8,128)(2,1)S(1)}, bf16[128,3584]{1,0:T(8,128)(2,1)S(1)}, u32[]{:S(2)}, u32[]{:S(2)}) collective-permute-start(bf16[128,3584]{1,0:T(8,128)(2,1)S(1)} %get-tuple-element.6), channel_id=1, source_target_pairs={{0,2},{1,3},{2,4},{3,5},{4,6},{5,7},{8,10},{9,11},{10,12},{11,13},... | collective-permute-start | bytes 2752520 | tf_op jit(solution)/shard_map/ppermute | solution.py:54
  234.8 2.9 fusion.15
  237.6 1.3 collective-permute-start.9
  239.0 14.2 %collective-permute-done.6 = bf16[128,3584]{1,0:T(8,128)(2,1)S(1)} collective-permute-done((bf16[128,3584]{1,0:T(8,128)(2,1)S(1)}, bf16[128,3584]{1,0:T(8,128)(2,1)S(1)}, u32[]{:S(2)}, u32[]{:S(2)}) %collective-permute-start.6) | collective-permute-done | bytes 917536 | tf_op jit(solution)/shard_map/ppermute | solution.py:54
  253.2 24.9 %collective-permute-done.9 = bf16[128,3584]{1,0:T(8,128)(2,1)} collective-permute-done((bf16[128,3584]{1,0:T(8,128)(2,1)}, bf16[128,3584]{1,0:T(8,128)(2,1)}, u32[]{:S(2)}, u32[]{:S(2)}) %collective-permute-start.9) | collective-permute-done | bytes 917536 | tf_op jit(solution)/shard_map/ppermute | solution.py:57
  278.0 3.3 %fusion.13 = (f32[128]{0:T(128)S(1)}, bf16[1,128,3584]{2,1,0:T(8,128)(2,1)}) fusion(bf16[1,128,3584]{2,1,0:T(8,128)(2,1)S(1)} %copy-done.1, bf16[128,3584]{1,0:T(8,128)(2,1)} %collective-permute-done.9, bf16[128,3584]{1,0:T(8,128)(2,1)S(1)} %collective-permute-done.6, f32[4,128,3584]{2,1,0:T(8,128)} %copy-done, s32[]{:T(128)S(6)} %select_n.119, f32[3584]{0:T(1024)S(1)} %reduce), kind=kLoop, calls=%fused_computation.18 | loop fusion | flops 4587392 | bytes 5519876 | tf_op jit(solution)/shard_map/reduce_sum | solution.py:136
  (37 shorter events, 5.2 us)
Async XLA Ops:
  7.2 78.6 %all-gather.3.cloned.1.call-start = ((), (), s32[]{:S(2)}) async-start(), calls=%async_computation | async-start | bytes 8257536 | tf_op jit(solution)/shard_map/all_gather | solution.py:99
  102.4 10.2 %collective-permute-start.2 = (bf16[16,32,128]{2,1,0:T(8,128)(2,1)}, bf16[16,32,128]{2,1,0:T(8,128)(2,1)S(1)}, u32[]{:S(2)}, u32[]{:S(2)}) collective-permute-start(bf16[16,32,128]{2,1,0:T(8,128)(2,1)} %shard_map.86), channel_id=1, source_target_pairs={{0,24},{1,25},{2,26},{3,27},{4,28},{5,29},{6,30},{7,31}} | collective-permute-start | bytes 393224 | tf_op jit(solution)/shard_map/ppermute | solution.py:104
  106.7 6.3 %collective-permute-start = (bf16[16,32,128]{2,1,0:T(8,128)(2,1)}, bf16[16,32,128]{2,1,0:T(8,128)(2,1)S(1)}, u32[]{:S(2)}, u32[]{:S(2)}) collective-permute-start(bf16[16,32,128]{2,1,0:T(8,128)(2,1)} %shard_map.86), channel_id=1, source_target_pairs={{0,8},{8,16},{16,24},{1,9},{9,17},{17,25},{2,10},{10,18},{18,26},{... | collective-permute-start | bytes 393224 | tf_op jit(solution)/shard_map/ppermute | solution.py:104
  108.0 5.6 %collective-permute-start.1 = (bf16[16,32,128]{2,1,0:T(8,128)(2,1)}, bf16[16,32,128]{2,1,0:T(8,128)(2,1)S(1)}, u32[]{:S(2)}, u32[]{:S(2)}) collective-permute-start(bf16[16,32,128]{2,1,0:T(8,128)(2,1)} %shard_map.86), channel_id=1, source_target_pairs={{0,16},{8,24},{1,17},{9,25},{2,18},{10,26},{3,19},{11,27},{4,20},{... | collective-permute-start | bytes 393224 | tf_op jit(solution)/shard_map/ppermute | solution.py:104
  162.7 6.8 %collective-permute-start.3 = (bf16[4,128,3584]{2,1,0:T(8,128)(2,1)}, bf16[4,128,3584]{2,1,0:T(8,128)(2,1)}, u32[]{:S(2)}, u32[]{:S(2)}) collective-permute-start(bf16[4,128,3584]{2,1,0:T(8,128)(2,1)} %fusion.9), channel_id=1, source_target_pairs={{0,1},{1,0},{2,3},{3,2},{4,5},{5,4},{6,7},{7,6},{8,9},{9,8},{10,11... | collective-permute-start | bytes 11010056 | tf_op jit(solution)/shard_map/ppermute | solution.py:45
  174.7 3.0 %copy-start = (f32[4,128,3584]{2,1,0:T(8,128)}, f32[4,128,3584]{2,1,0:T(8,128)S(1)}, u32[]{:S(2)}) copy-start(f32[4,128,3584]{2,1,0:T(8,128)S(1)} %bitcast_add_fusion) | copy-start | bytes 22020100
  177.8 21.5 %collective-permute-start.4 = (bf16[128,3584]{1,0:T(8,128)(2,1)S(1)}, bf16[128,3584]{1,0:T(8,128)(2,1)}, u32[]{:S(2)}, u32[]{:S(2)}) collective-permute-start(bf16[128,3584]{1,0:T(8,128)(2,1)S(1)} %get-tuple-element.8), channel_id=1, source_target_pairs={{0,2},{1,3},{8,10},{9,11},{16,18},{17,19},{24,26},{25,27}} | collective-permute-start | bytes 2752520 | tf_op jit(solution)/shard_map/ppermute | solution.py:54
  180.0 26.6 %collective-permute-start.7 = (bf16[128,3584]{1,0:T(8,128)(2,1)S(1)}, bf16[128,3584]{1,0:T(8,128)(2,1)S(1)}, u32[]{:S(2)}, u32[]{:S(2)}) collective-permute-start(bf16[128,3584]{1,0:T(8,128)(2,1)S(1)} %get-tuple-element.9), channel_id=1, source_target_pairs={{6,4},{7,5},{14,12},{15,13},{22,20},{23,21},{30,28},{31,29}} | collective-permute-start | bytes 2752520 | tf_op jit(solution)/shard_map/ppermute | solution.py:57
  201.2 23.9 %collective-permute-start.5 = (bf16[128,3584]{1,0:T(8,128)(2,1)S(1)}, bf16[128,3584]{1,0:T(8,128)(2,1)}, u32[]{:S(2)}, u32[]{:S(2)}) collective-permute-start(bf16[128,3584]{1,0:T(8,128)(2,1)S(1)} %fusion.16), channel_id=1, source_target_pairs={{0,2},{1,3},{2,4},{3,5},{8,10},{9,11},{10,12},{11,13},{16,18},{17,... | collective-permute-start | bytes 2752520 | tf_op jit(solution)/shard_map/ppermute | solution.py:54
  228.8 10.2 %copy-start.2 = (f32[1,3584]{1,0:T(1,128)S(1)}, f32[1,3584]{1,0:T(1,128)}, u32[]{:S(2)}) copy-start(f32[1,3584]{1,0:T(1,128)} %param.13) | copy-start | bytes 43012
  228.8 49.3 %copy-start.1 = (bf16[1,128,3584]{2,1,0:T(8,128)(2,1)S(1)}, bf16[1,128,3584]{2,1,0:T(8,128)(2,1)}, u32[]{:S(2)}) copy-start(bf16[1,128,3584]{2,1,0:T(8,128)(2,1)} %param.8) | copy-start | bytes 2752516
  228.8 6.0 %collective-permute-start.8 = (bf16[128,3584]{1,0:T(8,128)(2,1)}, bf16[128,3584]{1,0:T(8,128)(2,1)}, u32[]{:S(2)}, u32[]{:S(2)}) collective-permute-start(bf16[128,3584]{1,0:T(8,128)(2,1)} %get-tuple-element.7), channel_id=1, source_target_pairs={{4,2},{5,3},{6,4},{7,5},{12,10},{13,11},{14,12},{15,13},{20,18},{2... | collective-permute-start | bytes 2752520 | tf_op jit(solution)/shard_map/ppermute | solution.py:57
  230.5 22.7 %collective-permute-start.6 = (bf16[128,3584]{1,0:T(8,128)(2,1)S(1)}, bf16[128,3584]{1,0:T(8,128)(2,1)S(1)}, u32[]{:S(2)}, u32[]{:S(2)}) collective-permute-start(bf16[128,3584]{1,0:T(8,128)(2,1)S(1)} %get-tuple-element.6), channel_id=1, source_target_pairs={{0,2},{1,3},{2,4},{3,5},{4,6},{5,7},{8,10},{9,11},{10,12},{11,13},... | collective-permute-start | bytes 2752520 | tf_op jit(solution)/shard_map/ppermute | solution.py:54
  237.6 40.4 %collective-permute-start.9 = (bf16[128,3584]{1,0:T(8,128)(2,1)}, bf16[128,3584]{1,0:T(8,128)(2,1)}, u32[]{:S(2)}, u32[]{:S(2)}) collective-permute-start(bf16[128,3584]{1,0:T(8,128)(2,1)} %fusion.15), channel_id=1, source_target_pairs={{2,0},{3,1},{4,2},{5,3},{6,4},{7,5},{10,8},{11,9},{12,10},{13,11},... | collective-permute-start | bytes 2752520 | tf_op jit(solution)/shard_map/ppermute | solution.py:57
Sparse Core Ops, SparseCore 0:
  9.6 76.1 all-gather.2

commit v8 on v6

--- a/solution.py
+++ b/solution.py
@@ -10,27 +10,28 @@
 
 
 def encode_kernel(rows_ref, w_ref, b_ref, o_ref):
-    group = rows_ref.shape[0]
+    halves, group, rows_half, width = rows_ref.shape
     for i in range(group):
         cols = slice(i * BLOCK, (i + 1) * BLOCK)
-        acc = jnp.dot(rows_ref[i], w_ref[:, cols], preferred_element_type=jnp.float32)
+        rows = rows_ref[:, i].reshape(halves * rows_half, width)
+        acc = jnp.dot(rows, w_ref[:, cols], preferred_element_type=jnp.float32)
         acc = acc + b_ref[:, cols]
         o_ref[i] = jnp.maximum(acc, 0.0).astype(o_ref.dtype)
 
 
 def encode(rows, weight, bias):
-    per_owner, capacity, width = rows.shape
+    halves, per_owner, rows_half, width = rows.shape
     group = math.gcd(per_owner, 4)
     return pl.pallas_call(
         encode_kernel,
         grid=(per_owner // group,),
         in_specs=[
-            pl.BlockSpec((group, capacity, width), lambda g: (g, 0, 0)),
+            pl.BlockSpec((halves, group, rows_half, width), lambda g: (0, g, 0, 0)),
             pl.BlockSpec((width, group * BLOCK), lambda g: (0, g)),
             pl.BlockSpec((1, group * BLOCK), lambda g: (0, g)),
         ],
-        out_specs=pl.BlockSpec((group, capacity, BLOCK), lambda g: (g, 0, 0)),
-        out_shape=jax.ShapeDtypeStruct((per_owner, capacity, BLOCK), jnp.bfloat16),
+        out_specs=pl.BlockSpec((group, halves * rows_half, BLOCK), lambda g: (g, 0, 0)),
+        out_shape=jax.ShapeDtypeStruct((per_owner, halves * rows_half, BLOCK), jnp.bfloat16),
     )(rows, weight, bias)
 
 
@@ -68,12 +69,22 @@
         (local // cap) * (tok_count * cap) + src_of[None, :, :, None] * cap + local % cap,
         slot_count,
     ).reshape(layers, tokens, topk)
-    onehot = jnp.any(slot_of[..., None] == jnp.arange(slot_count, dtype=jnp.int32), axis=2)
+    halves = 2 if (tok_count % 2 == 0 and (tok_count // 2) * cap % 16 == 0) else 1
+    rows_half = tok_count * cap // halves
+    block_hit = (slot_of // (tok_count * cap))[..., None] == jnp.arange(per_owner, dtype=jnp.int32)
+    row_hit = (slot_of % rows_half)[..., None] == jnp.arange(rows_half, dtype=jnp.int32)
+    used = slot_of < slot_count
+    hits = jnp.any(block_hit[..., :, None] & row_hit[..., None, :] & used[..., None, None], axis=2)
 
     res_all = lax.all_gather(residual[0], "tok", axis=0, tiled=True)
-    own_onehot = lax.dynamic_index_in_dim(onehot, layer_index, 0, keepdims=False).astype(jnp.bfloat16)
-    rows = jnp.einsum("tx,td->xd", own_onehot, res_all, preferred_element_type=jnp.float32).astype(jnp.bfloat16)
-    codes = encode(rows.reshape(per_owner, tok_count * cap, width), encoder_weight[0], encoder_bias[0].reshape(1, -1))
+    own_hits = lax.dynamic_index_in_dim(hits, layer_index, 0, keepdims=False).astype(jnp.bfloat16)
+    rows = jnp.einsum(
+        "gtbx,gtd->gbxd",
+        own_hits.reshape(halves, tokens // halves, per_owner, rows_half),
+        res_all.reshape(halves, tokens // halves, width),
+        preferred_element_type=jnp.float32,
+    ).astype(jnp.bfloat16)
+    codes = encode(rows, encoder_weight[0], encoder_bias[0].reshape(1, -1))
     received = [codes] + [
         lax.ppermute(codes, "layer", [(i, i + shift) for i in range(layers - shift)])
         for shift in range(1, layers)
@@ -88,13 +99,8 @@
         decoder_weight[0].reshape(layers, per_owner, BLOCK, width),
         preferred_element_type=jnp.float32,
     ).astype(jnp.bfloat16)
-    halves = 2 if (tok_count % 2 == 0 and (tok_count // 2) * cap % 16 == 0) else 1
-    rows_half = tok_count * cap // halves
-    used = (slot_of < slot_count) & valid[:, None, None]
-    block_hit = (slot_of // (tok_count * cap))[..., None] == jnp.arange(per_owner, dtype=jnp.int32)
-    row_hit = (slot_of % rows_half)[..., None] == jnp.arange(rows_half, dtype=jnp.int32)
-    combine = jnp.any(block_hit[..., :, None] & row_hit[..., None, :] & used[..., None, None], axis=2)
-    combine = combine.astype(jnp.bfloat16).reshape(layers, halves, tokens // halves, per_owner, rows_half)
+    combine = (hits & valid[:, None, None, None]).astype(jnp.bfloat16)
+    combine = combine.reshape(layers, halves, tokens // halves, per_owner, rows_half)
     partial = jnp.einsum(
         "lgtbx,lbgxd->gtd",
         combine,

time: 245 us -> 244 us (level)
    and x1, other arithmetic: 0.08 us -> 3.59 us  [body(): combine = (hits & valid[:, None, None, None]).astype(jnp.bfloat16)]
    all_gather x1, waiting for transfers between devices: 56.4 us -> 53.1 us  [body(): res_all = lax.all_gather(residual[0], 'tok', axis=0, tiled=True)]
    reduce_or x1 -> x0, other arithmetic: 2.58 us -> none  [body(): jnp.any(slot_of[..., None] == jnp.arange(slot_count, dtype=jnp.int32), ax...]
  transfers between devices with their start and end apart: 5 -> 5, of which waited for: 4 -> 5; matrix products, arithmetic and copies ran while one was open for 4% -> 4% of each run, Pallas kernels for 0% -> 0%
where the time goes in v8:
time: 244 us
  waiting for transfers between devices  135 us (55%)
  matrix products  48.2 us (20%)
  blocking collectives  14.4 us (6%)
  between operations  14.2 us (6%)
  other arithmetic  10.6 us (4%)
  starting transfers between devices  8.3 us (3%)
  Pallas kernels  8.17 us (3%)
  local copies, waits for them, and re-layouts  5.02 us (2%)
    reduce_scatter x1, waiting for transfers between devices, body(): summed = lax.psum_scatter(partial, 'tok', scatter_dimension=0, tiled=True)  77.9 us
    all_gather x1, waiting for transfers between devices, body(): res_all = lax.all_gather(residual[0], 'tok', axis=0, tiled=True)  53.1 us
    dot_general x1, matrix products, body(): jnp.einsum('lbxe,lbed->lbxd', gathered, decoder_weight[0].reshape(layers,...  26.1 us
    dot_general x1, matrix products, body(): jnp.einsum('lgtbx,lbgxd->gtd', combine, terms.reshape(layers, per_owner,...  15.1 us
    all_gather x1, blocking collectives, body(): codes_all = lax.all_gather(codes_own, 'tok', axis=1, tiled=True)  14.4 us
    ppermute x3, starting transfers between devices, body(): lax.ppermute(codes, 'layer', [(i, i + shift) for i in range(layers - shif...  8.22 us
    pallas_call x1, Pallas kernels, encode(): pl.pallas_call(encode_kernel, grid=(per_owner // group,), in_specs=[pl.Bl...  8.17 us
    dot_general x1, matrix products, body(): jnp.einsum('gtbx,gtd->gbxd', own_hits.reshape(halves, tokens // halves, p...  7.05 us
  transfers between devices with their start and end apart: 5, of which 5 were waited for; matrix products, arithmetic and copies ran while one was open for 4% of the time, Pallas kernels for 0%

profile of v8, /device:TPU:0, one launch (start us, length us, event | category | flops | bytes accessed | tf_op | source)
XLA Modules:
  0.0 243.6 jit_solution(6743206442600287113)
XLA Ops:
  7.2 0.7 all-gather.3.cloned.1.call-update
  7.9 0.8 copy.50
  8.8 0.1 copy.51
  8.9 0.4 convert_reduce_fusion
  9.3 0.1 copy.53
  9.5 0.1 copy.54
  9.5 0.7 fusion.21
  10.2 14.4 %all_gather.6 = s32[4,1024,2]{1,0,2:T(4,128)S(1)} all-gather(s32[4,128,2]{1,0,2:T(4,128)S(1)} %fusion.21), channel_id=1, replica_groups=mesh['layer'=4,'tok'=8] {'tok'}, dimensions={1}, use_global_device_ids=true | all-gather | bytes 36864 | tf_op jit(solution)/shard_map/all_gather | solution.py:64
  24.6 0.1 broadcast_bitcast_fusion
  24.7 0.1 add_select_fusion.1
  25.0 0.1 iota_compare_fusion
  25.1 1.5 and_reduce_fusion
  26.7 1.9 reduce_or.12
  28.6 0.5 reshape.121
  29.1 3.6 %broadcast_and_fusion = pred[4,2,512,16,16]{2,1,4,3,0:T(4,128)(4,1)} fusion(pred[4,2,512,16,16]{2,1,4,3,0:T(4,128)(4,1)S(1)} %reduce_or.12, pred[4]{0:T(512)(128)(4,1)S(1)} %get-tuple-element.9), kind=kLoop, calls=%fused_computation.7 | loop fusion | flops 1048576 | bytes 2097156 | tf_op jit(solution)/shard_map/and | solution.py:102
  32.7 53.1 %all-gather.3.cloned.1.call-done = bf16[1,1024,3584]{2,1,0:T(8,128)(2,1)} async-done(((bf16[1,128,3584]{2,1,0:T(8,128)(2,1)}), bf16[1,1024,3584]{2,1,0:T(8,128)(2,1)}) %all-gather.3.cloned.1.call-update) | async-done | bytes 7340048 | tf_op jit(solution)/shard_map/all_gather | solution.py:79
  85.8 7.1 %convolution_convert_fusion.1.rows_ref = bf16[2,16,16,3584]{3,2,1,0:T(8,128)(2,1)} fusion(bf16[2,512,3584,1]{2,1,3,0:T(8,128)(2,1)} %bitcast.44, pred[2,512,16,16]{1,0,3,2:T(4,128)(4,1)S(1)} %reshape.121), kind=kOutput, calls=%fused_computation.6 | convolution fusion | flops 1880883200 | bytes 11272192 | tf_op jit(solution)/shard_map/gtbx,gtd->gbxd/dot_general | solution.py:81
  92.9 8.2 %shard_map.86 = bf16[16,32,128]{2,1,0:T(8,128)(2,1)} custom-call(bf16[2,16,16,3584]{3,2,1,0:T(8,128)(2,1)} %convolution_convert_fusion.1.rows_ref, bf16[3584,2048]{1,0:T(8,128)(2,1)} %bitcast.42, f32[1,2048]{1,0:T(1,128)} %b_ref.1), custom_call_target="tpu_custom_call" | custom-call | tf_op jit(solution)/shard_map/pallas_call | solution.py:25
  101.0 4.3 %collective-permute-start.2 = (bf16[16,32,128]{2,1,0:T(8,128)(2,1)}, bf16[16,32,128]{2,1,0:T(8,128)(2,1)S(1)}, u32[]{:S(2)}, u32[]{:S(2)}) collective-permute-start(bf16[16,32,128]{2,1,0:T(8,128)(2,1)} %shard_map.86), channel_id=1, source_target_pairs={{0,24},{1,25},{2,26},{3,27},{4,28},{5,29},{6,30},{7,31}} | collective-permute-start | bytes 393224 | tf_op jit(solution)/shard_map/ppermute | solution.py:89
  105.3 1.3 collective-permute-start
  106.6 2.6 %collective-permute-start.1 = (bf16[16,32,128]{2,1,0:T(8,128)(2,1)}, bf16[16,32,128]{2,1,0:T(8,128)(2,1)S(1)}, u32[]{:S(2)}, u32[]{:S(2)}) collective-permute-start(bf16[16,32,128]{2,1,0:T(8,128)(2,1)} %shard_map.86), channel_id=1, source_target_pairs={{0,16},{8,24},{1,17},{9,25},{2,18},{10,26},{3,19},{11,27},{4,20},{... | collective-permute-start | bytes 393224 | tf_op jit(solution)/shard_map/ppermute | solution.py:89
  109.3 0.2 collective-permute-done.2
  109.5 2.1 collective-permute-done
  111.6 0.7 collective-permute-done.1
  112.3 1.0 pad_maximum_fusion
  113.2 0.6 gather_fusion
  113.9 26.1 %convolution_convert_fusion = bf16[4,16,32,3584]{3,2,1,0:T(8,128)(2,1)} fusion(bf16[4,16,128,3584]{3,2,1,0:T(8,128)(2,1)} %bitcast.40, bf16[4,16,32,128]{3,2,1,0:T(8,128)(2,1)S(1)} %gather_fusion, pred[4]{0:T(512)(128)(4,1)S(1)} %get-tuple-element.8), kind=kOutput, calls=%fused_computation.4 | convolution fusion | flops 1886650368 | bytes 73924608 | tf_op jit(solution)/shard_map/lbxe,lbed->lbxd/dot_general | solution.py:96
  140.0 15.1 %bitcast_convert_fusion = bf16[2,512,3584]{2,1,0:T(8,128)(2,1)} fusion(bf16[4,16,2,16,3584]{4,3,2,1,0:T(8,128)(2,1)} %bitcast.41, pred[4,2,512,16,16]{2,1,4,3,0:T(4,128)(4,1)S(1)} %copy-done), kind=kOutput, calls=%fused_computation.1 | convolution fusion | flops 7519862784 | bytes 23068672 | tf_op jit(solution)/shard_map/lgtbx,lbgxd->gtd/dot_general | solution.py:104
  155.1 0.7 copy-done.2
  155.8 77.9 %reduce-scatter.2.cloned.1.call-done = bf16[128,3584]{1,0:T(8,128)(2,1)} async-done(((bf16[1024,3584]{1,0:T(8,128)(2,1)}), bf16[128,3584]{1,0:T(8,128)(2,1)}) %reduce-scatter.2.cloned.1.call-update) | async-done | bytes 917520 | tf_op jit(solution)/shard_map/reduce_scatter | solution.py:110
  233.8 2.5 %fusion.6 = (f32[128]{0:T(128)S(1)}, bf16[1,128,3584]{2,1,0:T(8,128)(2,1)}) fusion(bf16[128,3584]{1,0:T(8,128)(2,1)} %reduce-scatter.2.cloned.1.call-done, bf16[1,128,3584]{2,1,0:T(8,128)(2,1)S(1)} %copy-done.1, f32[3584]{0:T(1024)S(1)} %reduce), kind=kLoop, calls=%fused_computation.11 | loop fusion | flops 3211136 | bytes 2767360 | tf_op jit(solution)/shard_map/reduce_sum | solution.py:113
  236.3 0.5 multiply_bitcast_fusion
  (20 shorter events, 0.4 us)
Async XLA Ops:
  7.2 78.6 %all-gather.3.cloned.1.call-start = ((), (), s32[]{:S(2)}) async-start(), calls=%async_computation.2 | async-start | bytes 8257536 | tf_op jit(solution)/shard_map/all_gather | solution.py:79
  7.9 225.9 %reduce-scatter.2.cloned.1.call-start = ((), (), s32[]{:S(2)}) async-start(), calls=%async_computation.1 | async-start | bytes 8257536 | tf_op jit(solution)/shard_map/reduce_scatter | solution.py:110
  101.0 8.4 %collective-permute-start.2 = (bf16[16,32,128]{2,1,0:T(8,128)(2,1)}, bf16[16,32,128]{2,1,0:T(8,128)(2,1)S(1)}, u32[]{:S(2)}, u32[]{:S(2)}) collective-permute-start(bf16[16,32,128]{2,1,0:T(8,128)(2,1)} %shard_map.86), channel_id=1, source_target_pairs={{0,24},{1,25},{2,26},{3,27},{4,28},{5,29},{6,30},{7,31}} | collective-permute-start | bytes 393224 | tf_op jit(solution)/shard_map/ppermute | solution.py:89
  105.3 6.3 %collective-permute-start = (bf16[16,32,128]{2,1,0:T(8,128)(2,1)}, bf16[16,32,128]{2,1,0:T(8,128)(2,1)S(1)}, u32[]{:S(2)}, u32[]{:S(2)}) collective-permute-start(bf16[16,32,128]{2,1,0:T(8,128)(2,1)} %shard_map.86), channel_id=1, source_target_pairs={{0,8},{8,16},{16,24},{1,9},{9,17},{17,25},{2,10},{10,18},{18,26},{... | collective-permute-start | bytes 393224 | tf_op jit(solution)/shard_map/ppermute | solution.py:89
  106.6 5.6 %collective-permute-start.1 = (bf16[16,32,128]{2,1,0:T(8,128)(2,1)}, bf16[16,32,128]{2,1,0:T(8,128)(2,1)S(1)}, u32[]{:S(2)}, u32[]{:S(2)}) collective-permute-start(bf16[16,32,128]{2,1,0:T(8,128)(2,1)} %shard_map.86), channel_id=1, source_target_pairs={{0,16},{8,24},{1,17},{9,25},{2,18},{10,26},{3,19},{11,27},{4,20},{... | collective-permute-start | bytes 393224 | tf_op jit(solution)/shard_map/ppermute | solution.py:89
  113.9 26.1 %copy-start = (pred[4,2,512,16,16]{2,1,4,3,0:T(4,128)(4,1)S(1)}, pred[4,2,512,16,16]{2,1,4,3,0:T(4,128)(4,1)}, u32[]{:S(2)}) copy-start(pred[4,2,512,16,16]{2,1,4,3,0:T(4,128)(4,1)} %broadcast_and_fusion) | copy-start | bytes 3145732
  155.1 0.7 copy-start.2
  155.1 78.7 %copy-start.1 = (bf16[1,128,3584]{2,1,0:T(8,128)(2,1)S(1)}, bf16[1,128,3584]{2,1,0:T(8,128)(2,1)}, u32[]{:S(2)}) copy-start(bf16[1,128,3584]{2,1,0:T(8,128)(2,1)} %param.8) | copy-start | bytes 2752516
Sparse Core Ops, SparseCore 0:
  9.6 76.1 all-gather.2
  155.2 78.4 reduce-scatter.1

commit v9 on v8

--- a/solution.py
+++ b/solution.py
@@ -93,21 +93,27 @@
     gathered = jnp.take(jnp.stack(received), shifts, axis=0)
 
     valid = jnp.arange(layers, dtype=jnp.int32) <= layer_index
-    terms = jnp.einsum(
-        "lbxe,lbed->lbxd",
-        gathered,
-        decoder_weight[0].reshape(layers, per_owner, BLOCK, width),
-        preferred_element_type=jnp.float32,
-    ).astype(jnp.bfloat16)
     combine = (hits & valid[:, None, None, None]).astype(jnp.bfloat16)
     combine = combine.reshape(layers, halves, tokens // halves, per_owner, rows_half)
-    partial = jnp.einsum(
-        "lgtbx,lbgxd->gtd",
-        combine,
-        terms.reshape(layers, per_owner, halves, rows_half, width),
-        preferred_element_type=jnp.float32,
-    ).reshape(tokens, width).astype(jnp.bfloat16)
-    summed = lax.psum_scatter(partial, "tok", scatter_dimension=0, tiled=True)
+    weights = decoder_weight[0].reshape(layers, per_owner, BLOCK, width)
+    chunks = 2 if width % (2 * BLOCK) == 0 else 1
+    step = width // chunks
+    pieces = []
+    for c in range(chunks):
+        terms = jnp.einsum(
+            "lbxe,lbed->lbxd",
+            gathered,
+            weights[..., c * step:(c + 1) * step],
+            preferred_element_type=jnp.float32,
+        ).astype(jnp.bfloat16)
+        partial = jnp.einsum(
+            "lgtbx,lbgxd->gtd",
+            combine,
+            terms.reshape(layers, per_owner, halves, rows_half, step),
+            preferred_element_type=jnp.float32,
+        ).reshape(tokens, step).astype(jnp.bfloat16)
+        pieces.append(lax.psum_scatter(partial, "tok", scatter_dimension=0, tiled=True))
+    summed = jnp.concatenate(pieces, axis=1)
     recon32 = decoder_bias[0][None, :] + summed.astype(jnp.float32)
     difference = recon32 - targets[0].astype(jnp.float32)
     error = jnp.mean(difference * difference, axis=1)

time: 244 us -> 238 us (0.975)
  waiting for transfers between devices: 135 us -> 122 us
  matrix products: 48.2 us -> 54.3 us
    reduce_scatter x1 -> x2, waiting for transfers between devices: 77.9 us -> 65.2 us  [body(): lax.psum_scatter(partial, 'tok', scatter_dimension=0, tiled=True)]
    dot_general x1 -> x2, matrix products: 26.1 us -> 29.8 us  [body(): jnp.einsum('lbxe,lbed->lbxd', gathered, weights[..., c * step:(c + 1) * s...]
    dot_general x1 -> x2, matrix products: 15.1 us -> 17.5 us  [body(): jnp.einsum('lgtbx,lbgxd->gtd', combine, terms.reshape(layers, per_owner,...]
  transfers between devices with their start and end apart: 5 -> 6, of which waited for: 5 -> 6; matrix products, arithmetic and copies ran while one was open for 4% -> 14% of each run, Pallas kernels for 0% -> 0%
where the time goes in v9:
time: 238 us
  waiting for transfers between devices  122 us (51%)
  matrix products  54.3 us (23%)
  blocking collectives  14.4 us (6%)
  between operations  13.9 us (6%)
  other arithmetic  12 us (5%)
  starting transfers between devices  8.34 us (4%)
  Pallas kernels  8.17 us (3%)
  local copies, waits for them, and re-layouts  5.02 us (2%)
    reduce_scatter x2, waiting for transfers between devices, body(): lax.psum_scatter(partial, 'tok', scatter_dimension=0, tiled=True)  65.2 us
    all_gather x1, waiting for transfers between devices, body(): res_all = lax.all_gather(residual[0], 'tok', axis=0, tiled=True)  53.1 us
    dot_general x2, matrix products, body(): jnp.einsum('lbxe,lbed->lbxd', gathered, weights[..., c * step:(c + 1) * s...  29.8 us
    dot_general x2, matrix products, body(): jnp.einsum('lgtbx,lbgxd->gtd', combine, terms.reshape(layers, per_owner,...  17.5 us
    all_gather x1, blocking collectives, body(): codes_all = lax.all_gather(codes_own, 'tok', axis=1, tiled=True)  14.4 us
    ppermute x3, starting transfers between devices, body(): lax.ppermute(codes, 'layer', [(i, i + shift) for i in range(layers - shif...  8.22 us
    pallas_call x1, Pallas kernels, encode(): pl.pallas_call(encode_kernel, grid=(per_owner // group,), in_specs=[pl.Bl...  8.17 us
    dot_general x1, matrix products, body(): jnp.einsum('gtbx,gtd->gbxd', own_hits.reshape(halves, tokens // halves, p...  7.06 us
  transfers between devices with their start and end apart: 6, of which 6 were waited for; matrix products, arithmetic and copies ran while one was open for 14% of the time, Pallas kernels for 0%

profile of v9, /device:TPU:0, one launch (start us, length us, event | category | flops | bytes accessed | tf_op | source)
XLA Modules:
  0.0 238.0 jit_solution(10857710431024841961)
XLA Ops:
  7.2 0.7 all-gather.3.cloned.1.call-update
  7.9 0.8 copy.57
  8.9 0.4 convert_reduce_fusion
  9.3 0.1 copy.60
  9.5 0.7 fusion.31
  10.2 14.4 %all_gather.6 = s32[4,1024,2]{1,0,2:T(4,128)S(1)} all-gather(s32[4,128,2]{1,0,2:T(4,128)S(1)} %fusion.31), channel_id=1, replica_groups=mesh['layer'=4,'tok'=8] {'tok'}, dimensions={1}, use_global_device_ids=true | all-gather | bytes 36864 | tf_op jit(solution)/shard_map/all_gather | solution.py:64
  25.0 0.1 iota_compare_fusion
  25.1 1.5 and_reduce_fusion
  26.7 1.9 reduce_or.12
  28.6 0.5 reshape.185
  29.1 3.6 %broadcast_and_fusion = pred[4,2,512,16,16]{2,1,4,3,0:T(4,128)(4,1)} fusion(pred[4,2,512,16,16]{2,1,4,3,0:T(4,128)(4,1)S(1)} %reduce_or.12, pred[4]{0:T(512)(128)(4,1)S(1)} %get-tuple-element.7), kind=kLoop, calls=%fused_computation.15 | loop fusion | flops 1048576 | bytes 2097156 | tf_op jit(solution)/shard_map/and | solution.py:96
  32.7 53.1 %all-gather.3.cloned.1.call-done = bf16[1,1024,3584]{2,1,0:T(8,128)(2,1)} async-done(((bf16[1,128,3584]{2,1,0:T(8,128)(2,1)}), bf16[1,1024,3584]{2,1,0:T(8,128)(2,1)}) %all-gather.3.cloned.1.call-update) | async-done | bytes 7340048 | tf_op jit(solution)/shard_map/all_gather | solution.py:79
  85.8 7.1 %convolution_convert_fusion.rows_ref = bf16[2,16,16,3584]{3,2,1,0:T(8,128)(2,1)} fusion(bf16[2,512,3584,1]{2,1,3,0:T(8,128)(2,1)} %bitcast.50, pred[2,512,16,16]{1,0,3,2:T(4,128)(4,1)S(1)} %reshape.185), kind=kOutput, calls=%fused_computation.12 | convolution fusion | flops 1880883200 | bytes 11272192 | tf_op jit(solution)/shard_map/gtbx,gtd->gbxd/dot_general | solution.py:81
  92.9 8.2 %shard_map.86 = bf16[16,32,128]{2,1,0:T(8,128)(2,1)} custom-call(bf16[2,16,16,3584]{3,2,1,0:T(8,128)(2,1)} %convolution_convert_fusion.rows_ref, bf16[3584,2048]{1,0:T(8,128)(2,1)} %bitcast.47, f32[1,2048]{1,0:T(1,128)} %b_ref.1), custom_call_target="tpu_custom_call" | custom-call | tf_op jit(solution)/shard_map/pallas_call | solution.py:25
  101.0 4.3 %collective-permute-start.2 = (bf16[16,32,128]{2,1,0:T(8,128)(2,1)}, bf16[16,32,128]{2,1,0:T(8,128)(2,1)S(1)}, u32[]{:S(2)}, u32[]{:S(2)}) collective-permute-start(bf16[16,32,128]{2,1,0:T(8,128)(2,1)} %shard_map.86), channel_id=1, source_target_pairs={{0,24},{1,25},{2,26},{3,27},{4,28},{5,29},{6,30},{7,31}} | collective-permute-start | bytes 393224 | tf_op jit(solution)/shard_map/ppermute | solution.py:89
  105.3 1.3 collective-permute-start
  106.6 2.6 %collective-permute-start.1 = (bf16[16,32,128]{2,1,0:T(8,128)(2,1)}, bf16[16,32,128]{2,1,0:T(8,128)(2,1)S(1)}, u32[]{:S(2)}, u32[]{:S(2)}) collective-permute-start(bf16[16,32,128]{2,1,0:T(8,128)(2,1)} %shard_map.86), channel_id=1, source_target_pairs={{0,16},{8,24},{1,17},{9,25},{2,18},{10,26},{3,19},{11,27},{4,20},{... | collective-permute-start | bytes 393224 | tf_op jit(solution)/shard_map/ppermute | solution.py:89
  109.3 0.2 collective-permute-done.2
  109.5 2.1 collective-permute-done
  111.6 0.7 collective-permute-done.1
  112.3 1.0 pad_maximum_fusion
  113.2 0.6 gather_fusion
  113.9 14.8 %fusion.8 = bf16[4,16,32,1792]{3,2,1,0:T(8,128)(2,1)} fusion(bf16[4,16,128,3584]{3,2,1,0:T(8,128)(2,1)} %bitcast.45, bf16[4,16,32,128]{3,2,1,0:T(8,128)(2,1)S(1)} %gather_fusion, pred[4]{0:T(512)(128)(4,1)S(1)} %get-tuple-element.6), kind=kOutput, calls=%fused_computation.13 | convolution fusion | flops 943456256 | bytes 37224452 | tf_op jit(solution)/shard_map/lbxe,lbed->lbxd/dot_general | solution.py:103
  128.7 8.7 %bitcast_convert_fusion.1 = bf16[2,512,1792]{2,1,0:T(8,128)(2,1)} fusion(bf16[4,16,2,16,1792]{4,3,2,1,0:T(8,128)(2,1)} %bitcast.49, pred[4,2,512,16,16]{2,1,4,3,0:T(4,128)(4,1)S(1)} %copy-done), kind=kOutput, calls=%fused_computation.7 | convolution fusion | flops 3759931392 | bytes 12058624 | tf_op jit(solution)/shard_map/lgtbx,lbgxd->gtd/dot_general | solution.py:109
  137.5 15.0 %fusion.11 = bf16[4,16,32,1792]{3,2,1,0:T(8,128)(2,1)} fusion(bf16[4,16,128,3584]{3,2,1,0:T(8,128)(2,1)} %bitcast.46, bf16[4,16,32,128]{3,2,1,0:T(8,128)(2,1)S(1)} %gather_fusion, pred[4]{0:T(512)(128)(4,1)S(1)} %get-tuple-element.6), kind=kOutput, calls=%fused_computation.14 | convolution fusion | flops 943456256 | bytes 37224452 | tf_op jit(solution)/shard_map/lbxe,lbed->lbxd/dot_general | solution.py:103
  152.5 8.8 %bitcast_convert_fusion = bf16[2,512,1792]{2,1,0:T(8,128)(2,1)} fusion(bf16[4,16,2,16,1792]{4,3,2,1,0:T(8,128)(2,1)} %bitcast.48, pred[4,2,512,16,16]{2,1,4,3,0:T(4,128)(4,1)S(1)} %copy-done), kind=kOutput, calls=%fused_computation.6 | convolution fusion | flops 3759931392 | bytes 12058624 | tf_op jit(solution)/shard_map/lgtbx,lbgxd->gtd/dot_general | solution.py:109
  161.3 0.7 copy-done.2
  162.0 19.4 %reduce-scatter.3.cloned.1.call-done = bf16[128,1792]{1,0:T(8,128)(2,1)} async-done(((bf16[1024,1792]{1,0:T(8,128)(2,1)}), bf16[128,1792]{1,0:T(8,128)(2,1)}) %reduce-scatter.3.cloned.1.call-update) | async-done | bytes 458768 | tf_op jit(solution)/shard_map/reduce_scatter | solution.py:115
  181.4 45.8 %reduce-scatter.5.cloned.1.call-done = bf16[128,1792]{1,0:T(8,128)(2,1)} async-done(((bf16[1024,1792]{1,0:T(8,128)(2,1)}), bf16[128,1792]{1,0:T(8,128)(2,1)}) %reduce-scatter.5.cloned.1.call-update) | async-done | bytes 458768 | tf_op jit(solution)/shard_map/reduce_scatter | solution.py:115
  227.2 1.6 fusion.19
  228.8 0.5 multiply_bitcast_fusion
  229.3 2.2 add_convert_fusion
  (26 shorter events, 0.8 us)
Async XLA Ops:
  7.2 78.6 %all-gather.3.cloned.1.call-start = ((), (), s32[]{:S(2)}) async-start(), calls=%async_computation.4 | async-start | bytes 8257536 | tf_op jit(solution)/shard_map/all_gather | solution.py:79
  7.9 173.5 %reduce-scatter.3.cloned.1.call-start = ((), (), s32[]{:S(2)}) async-start(), calls=%async_computation.2 | async-start | bytes 4128768 | tf_op jit(solution)/shard_map/reduce_scatter | solution.py:115
  101.0 8.4 %collective-permute-start.2 = (bf16[16,32,128]{2,1,0:T(8,128)(2,1)}, bf16[16,32,128]{2,1,0:T(8,128)(2,1)S(1)}, u32[]{:S(2)}, u32[]{:S(2)}) collective-permute-start(bf16[16,32,128]{2,1,0:T(8,128)(2,1)} %shard_map.86), channel_id=1, source_target_pairs={{0,24},{1,25},{2,26},{3,27},{4,28},{5,29},{6,30},{7,31}} | collective-permute-start | bytes 393224 | tf_op jit(solution)/shard_map/ppermute | solution.py:89
  105.3 6.3 %collective-permute-start = (bf16[16,32,128]{2,1,0:T(8,128)(2,1)}, bf16[16,32,128]{2,1,0:T(8,128)(2,1)S(1)}, u32[]{:S(2)}, u32[]{:S(2)}) collective-permute-start(bf16[16,32,128]{2,1,0:T(8,128)(2,1)} %shard_map.86), channel_id=1, source_target_pairs={{0,8},{8,16},{16,24},{1,9},{9,17},{17,25},{2,10},{10,18},{18,26},{... | collective-permute-start | bytes 393224 | tf_op jit(solution)/shard_map/ppermute | solution.py:89
  106.6 5.6 %collective-permute-start.1 = (bf16[16,32,128]{2,1,0:T(8,128)(2,1)}, bf16[16,32,128]{2,1,0:T(8,128)(2,1)S(1)}, u32[]{:S(2)}, u32[]{:S(2)}) collective-permute-start(bf16[16,32,128]{2,1,0:T(8,128)(2,1)} %shard_map.86), channel_id=1, source_target_pairs={{0,16},{8,24},{1,17},{9,25},{2,18},{10,26},{3,19},{11,27},{4,20},{... | collective-permute-start | bytes 393224 | tf_op jit(solution)/shard_map/ppermute | solution.py:89
  113.9 14.8 %copy-start = (pred[4,2,512,16,16]{2,1,4,3,0:T(4,128)(4,1)S(1)}, pred[4,2,512,16,16]{2,1,4,3,0:T(4,128)(4,1)}, u32[]{:S(2)}) copy-start(pred[4,2,512,16,16]{2,1,4,3,0:T(4,128)(4,1)} %broadcast_and_fusion) | copy-start | bytes 3145732
  137.4 89.7 %reduce-scatter.5.cloned.1.call-start = ((), (), s32[]{:S(2)}) async-start(), calls=%async_computation.3 | async-start | bytes 4128768 | tf_op jit(solution)/shard_map/reduce_scatter | solution.py:115
  161.2 0.7 copy-start.2
  161.2 65.9 %copy-start.1 = (bf16[1,128,3584]{2,1,0:T(8,128)(2,1)S(1)}, bf16[1,128,3584]{2,1,0:T(8,128)(2,1)}, u32[]{:S(2)}) copy-start(bf16[1,128,3584]{2,1,0:T(8,128)(2,1)} %param.8) | copy-start | bytes 2752516
Sparse Core Ops, SparseCore 0:
  9.6 76.1 all-gather.2
  137.5 43.8 reduce-scatter.2
  183.7 43.4 reduce-scatter.4

commit v10 on v9

--- a/solution.py
+++ b/solution.py
@@ -96,22 +96,24 @@
     combine = (hits & valid[:, None, None, None]).astype(jnp.bfloat16)
     combine = combine.reshape(layers, halves, tokens // halves, per_owner, rows_half)
     weights = decoder_weight[0].reshape(layers, per_owner, BLOCK, width)
-    chunks = 2 if width % (2 * BLOCK) == 0 else 1
-    step = width // chunks
+    cut = (width // BLOCK) * 2 // 7 * BLOCK if width % BLOCK == 0 else 0
+    bounds = [0, cut, width] if 0 < cut < width else [0, width]
     pieces = []
-    for c in range(chunks):
+    chunk_codes = gathered
+    for lo, hi in zip(bounds[:-1], bounds[1:]):
         terms = jnp.einsum(
             "lbxe,lbed->lbxd",
-            gathered,
-            weights[..., c * step:(c + 1) * step],
+            chunk_codes,
+            weights[..., lo:hi],
             preferred_element_type=jnp.float32,
         ).astype(jnp.bfloat16)
         partial = jnp.einsum(
             "lgtbx,lbgxd->gtd",
             combine,
-            terms.reshape(layers, per_owner, halves, rows_half, step),
+            terms.reshape(layers, per_owner, halves, rows_half, hi - lo),
             preferred_element_type=jnp.float32,
-        ).reshape(tokens, step).astype(jnp.bfloat16)
+        ).reshape(tokens, hi - lo).astype(jnp.bfloat16)
+        chunk_codes, partial = lax.optimization_barrier((chunk_codes, partial))
         pieces.append(lax.psum_scatter(partial, "tok", scatter_dimension=0, tiled=True))
     summed = jnp.concatenate(pieces, axis=1)
     recon32 = decoder_bias[0][None, :] + summed.astype(jnp.float32)

time: 238 us -> 233 us (0.979)
  matrix products: 54.3 us -> 49.8 us
  transfers between devices with their start and end apart: 6 -> 6, of which waited for: 6 -> 4; matrix products, arithmetic and copies ran while one was open for 14% -> 18% of each run, Pallas kernels for 0% -> 0%
where the time goes in v10:
time: 233 us
  waiting for transfers between devices  121 us (52%)
  matrix products  49.8 us (21%)
  blocking collectives  14.4 us (6%)
  between operations  13.9 us (6%)
  other arithmetic  12.1 us (5%)
  starting transfers between devices  8.34 us (4%)
  Pallas kernels  8.17 us (4%)
  local copies, waits for them, and re-layouts  5.02 us (2%)
    reduce_scatter x2, waiting for transfers between devices, body(): lax.psum_scatter(partial, 'tok', scatter_dimension=0, tiled=True)  63.9 us
    all_gather x1, waiting for transfers between devices, body(): res_all = lax.all_gather(residual[0], 'tok', axis=0, tiled=True)  53.1 us
    dot_general x2, matrix products, body(): jnp.einsum('lbxe,lbed->lbxd', chunk_codes, weights[..., lo:hi], preferred...  27.6 us
    dot_general x2, matrix products, body(): jnp.einsum('lgtbx,lbgxd->gtd', combine, terms.reshape(layers, per_owner,...  15.2 us
    all_gather x1, blocking collectives, body(): codes_all = lax.all_gather(codes_own, 'tok', axis=1, tiled=True)  14.4 us
    ppermute x3, starting transfers between devices, body(): lax.ppermute(codes, 'layer', [(i, i + shift) for i in range(layers - shif...  8.22 us
    pallas_call x1, Pallas kernels, encode(): pl.pallas_call(encode_kernel, grid=(per_owner // group,), in_specs=[pl.Bl...  8.17 us
    dot_general x1, matrix products, body(): jnp.einsum('gtbx,gtd->gbxd', own_hits.reshape(halves, tokens // halves, p...  7.06 us
  transfers between devices with their start and end apart: 6, of which 4 were waited for; matrix products, arithmetic and copies ran while one was open for 18% of the time, Pallas kernels for 0%

profile of v10, /device:TPU:0, one launch (start us, length us, event | category | flops | bytes accessed | tf_op | source)
XLA Modules:
  0.0 233.0 jit_solution(6004629058621323939)
XLA Ops:
  7.2 0.7 all-gather.3.cloned.1.call-update
  7.9 0.8 copy.57
  8.9 0.4 convert_reduce_fusion
  9.3 0.1 copy.60
  9.5 0.7 fusion.31
  10.2 14.4 %all_gather.6 = s32[4,1024,2]{1,0,2:T(4,128)S(1)} all-gather(s32[4,128,2]{1,0,2:T(4,128)S(1)} %fusion.31), channel_id=1, replica_groups=mesh['layer'=4,'tok'=8] {'tok'}, dimensions={1}, use_global_device_ids=true | all-gather | bytes 36864 | tf_op jit(solution)/shard_map/all_gather | solution.py:64
  24.7 0.1 add_select_fusion.1
  25.0 0.1 iota_compare_fusion
  25.1 1.5 and_reduce_fusion
  26.7 1.9 reduce_or.12
  28.6 0.5 reshape.185
  29.1 3.6 %broadcast_and_fusion = pred[4,2,512,16,16]{2,1,4,3,0:T(4,128)(4,1)} fusion(pred[4,2,512,16,16]{2,1,4,3,0:T(4,128)(4,1)S(1)} %reduce_or.12, pred[4]{0:T(512)(128)(4,1)S(1)} %get-tuple-element.13), kind=kLoop, calls=%fused_computation.14 | loop fusion | flops 1048576 | bytes 2097156 | tf_op jit(solution)/shard_map/and | solution.py:96
  32.7 53.1 %all-gather.3.cloned.1.call-done = bf16[1,1024,3584]{2,1,0:T(8,128)(2,1)} async-done(((bf16[1,128,3584]{2,1,0:T(8,128)(2,1)}), bf16[1,1024,3584]{2,1,0:T(8,128)(2,1)}) %all-gather.3.cloned.1.call-update) | async-done | bytes 7340048 | tf_op jit(solution)/shard_map/all_gather | solution.py:79
  85.8 7.1 %convolution_convert_fusion.rows_ref = bf16[2,16,16,3584]{3,2,1,0:T(8,128)(2,1)} fusion(bf16[2,512,3584,1]{2,1,3,0:T(8,128)(2,1)} %bitcast.51, pred[2,512,16,16]{1,0,3,2:T(4,128)(4,1)S(1)} %reshape.185), kind=kOutput, calls=%fused_computation.10 | convolution fusion | flops 1880883200 | bytes 11272192 | tf_op jit(solution)/shard_map/gtbx,gtd->gbxd/dot_general | solution.py:81
  92.9 8.2 %shard_map.86 = bf16[16,32,128]{2,1,0:T(8,128)(2,1)} custom-call(bf16[2,16,16,3584]{3,2,1,0:T(8,128)(2,1)} %convolution_convert_fusion.rows_ref, bf16[3584,2048]{1,0:T(8,128)(2,1)} %bitcast.50, f32[1,2048]{1,0:T(1,128)} %b_ref.1), custom_call_target="tpu_custom_call" | custom-call | tf_op jit(solution)/shard_map/pallas_call | solution.py:25
  101.0 4.3 %collective-permute-start.2 = (bf16[16,32,128]{2,1,0:T(8,128)(2,1)}, bf16[16,32,128]{2,1,0:T(8,128)(2,1)S(1)}, u32[]{:S(2)}, u32[]{:S(2)}) collective-permute-start(bf16[16,32,128]{2,1,0:T(8,128)(2,1)} %shard_map.86), channel_id=1, source_target_pairs={{0,24},{1,25},{2,26},{3,27},{4,28},{5,29},{6,30},{7,31}} | collective-permute-start | bytes 393224 | tf_op jit(solution)/shard_map/ppermute | solution.py:89
  105.3 1.3 collective-permute-start.1
  106.6 2.7 %collective-permute-start = (bf16[16,32,128]{2,1,0:T(8,128)(2,1)}, bf16[16,32,128]{2,1,0:T(8,128)(2,1)S(1)}, u32[]{:S(2)}, u32[]{:S(2)}) collective-permute-start(bf16[16,32,128]{2,1,0:T(8,128)(2,1)} %shard_map.86), channel_id=1, source_target_pairs={{0,8},{8,16},{16,24},{1,9},{9,17},{17,25},{2,10},{10,18},{18,26},{... | collective-permute-start | bytes 393224 | tf_op jit(solution)/shard_map/ppermute | solution.py:89
  109.3 3.6 %collective-permute-done.1 = bf16[16,32,128]{2,1,0:T(8,128)(2,1)S(1)} collective-permute-done((bf16[16,32,128]{2,1,0:T(8,128)(2,1)}, bf16[16,32,128]{2,1,0:T(8,128)(2,1)S(1)}, u32[]{:S(2)}, u32[]{:S(2)}) %collective-permute-start.1) | collective-permute-done | bytes 131104 | tf_op jit(solution)/shard_map/ppermute | solution.py:89
  112.9 1.0 pad_maximum_fusion
  113.9 0.6 gather_fusion
  114.5 0.1 broadcast_select_fusion
  114.6 8.2 %fusion.13 = bf16[4,16,32,1024]{3,2,1,0:T(8,128)(2,1)S(1)} fusion(bf16[4,16,32,128]{3,2,1,0:T(8,128)(2,1)S(1)} %broadcast_select_fusion, bf16[4,16,128,3584]{3,2,1,0:T(8,128)(2,1)} %bitcast.47), kind=kOutput, calls=%fused_computation.15 | convolution fusion | flops 538968064 | bytes 21495808 | tf_op jit(solution)/shard_map/lbxe,lbed->lbxd/dot_general | solution.py:104
  122.9 3.7 %bitcast_convert_fusion.1 = bf16[2,512,1024]{2,1,0:T(8,128)(2,1)} fusion(bf16[4,16,2,16,1024]{4,3,2,1,0:T(8,128)(2,1)S(1)} %bitcast.53, pred[4,2,512,16,16]{2,1,4,3,0:T(4,128)(4,1)S(1)} %copy-done), kind=kOutput, calls=%fused_computation.11 | convolution fusion | flops 2148532224 | bytes 7340032 | tf_op jit(solution)/shard_map/lgtbx,lbgxd->gtd/dot_general | solution.py:110
  126.7 19.3 %fusion.6 = bf16[4,16,32,2560]{3,2,1,0:T(8,128)(2,1)} fusion(bf16[4,16,32,128]{3,2,1,0:T(8,128)(2,1)S(1)} %broadcast_select_fusion, bf16[4,16,128,3584]{3,2,1,0:T(8,128)(2,1)} %bitcast.48), kind=kOutput, calls=%fused_computation.9 | convolution fusion | flops 1347420160 | bytes 52953088 | tf_op jit(solution)/shard_map/lbxe,lbed->lbxd/dot_general | solution.py:104
  146.0 11.5 %bitcast_convert_fusion = bf16[2,512,2560]{2,1,0:T(8,128)(2,1)} fusion(bf16[4,16,2,16,2560]{4,3,2,1,0:T(8,128)(2,1)} %bitcast.49, pred[4,2,512,16,16]{2,1,4,3,0:T(4,128)(4,1)S(1)} %copy-done), kind=kOutput, calls=%fused_computation.5 | convolution fusion | flops 5371330560 | bytes 16777216 | tf_op jit(solution)/shard_map/lgtbx,lbgxd->gtd/dot_general | solution.py:110
  157.5 0.7 copy-done.2
  158.2 2.9 %reduce-scatter.3.cloned.1.call-done = bf16[128,1024]{1,0:T(8,128)(2,1)} async-done(((bf16[1024,1024]{1,0:T(8,128)(2,1)}), bf16[128,1024]{1,0:T(8,128)(2,1)}) %reduce-scatter.3.cloned.1.call-update) | async-done | bytes 262160 | tf_op jit(solution)/shard_map/reduce_scatter | solution.py:117
  161.1 61.0 %reduce-scatter.5.cloned.1.call-done = bf16[128,2560]{1,0:T(8,128)(2,1)} async-done(((bf16[1024,2560]{1,0:T(8,128)(2,1)}), bf16[128,2560]{1,0:T(8,128)(2,1)}) %reduce-scatter.5.cloned.1.call-update) | async-done | bytes 655376 | tf_op jit(solution)/shard_map/reduce_scatter | solution.py:117
  222.1 1.6 fusion.19
  223.7 0.5 multiply_bitcast_fusion
  224.2 2.2 add_convert_fusion
  (27 shorter events, 0.6 us)
Async XLA Ops:
  7.2 78.6 %all-gather.3.cloned.1.call-start = ((), (), s32[]{:S(2)}) async-start(), calls=%async_computation.4 | async-start | bytes 8257536 | tf_op jit(solution)/shard_map/all_gather | solution.py:79
  7.9 153.2 %reduce-scatter.3.cloned.1.call-start = ((), (), s32[]{:S(2)}) async-start(), calls=%async_computation.2 | async-start | bytes 2359296 | tf_op jit(solution)/shard_map/reduce_scatter | solution.py:117
  101.0 8.3 %collective-permute-start.2 = (bf16[16,32,128]{2,1,0:T(8,128)(2,1)}, bf16[16,32,128]{2,1,0:T(8,128)(2,1)S(1)}, u32[]{:S(2)}, u32[]{:S(2)}) collective-permute-start(bf16[16,32,128]{2,1,0:T(8,128)(2,1)} %shard_map.86), channel_id=1, source_target_pairs={{0,24},{1,25},{2,26},{3,27},{4,28},{5,29},{6,30},{7,31}} | collective-permute-start | bytes 393224 | tf_op jit(solution)/shard_map/ppermute | solution.py:89
  105.3 7.6 %collective-permute-start.1 = (bf16[16,32,128]{2,1,0:T(8,128)(2,1)}, bf16[16,32,128]{2,1,0:T(8,128)(2,1)S(1)}, u32[]{:S(2)}, u32[]{:S(2)}) collective-permute-start(bf16[16,32,128]{2,1,0:T(8,128)(2,1)} %shard_map.86), channel_id=1, source_target_pairs={{0,16},{8,24},{1,17},{9,25},{2,18},{10,26},{3,19},{11,27},{4,20},{... | collective-permute-start | bytes 393224 | tf_op jit(solution)/shard_map/ppermute | solution.py:89
  106.6 6.3 %collective-permute-start = (bf16[16,32,128]{2,1,0:T(8,128)(2,1)}, bf16[16,32,128]{2,1,0:T(8,128)(2,1)S(1)}, u32[]{:S(2)}, u32[]{:S(2)}) collective-permute-start(bf16[16,32,128]{2,1,0:T(8,128)(2,1)} %shard_map.86), channel_id=1, source_target_pairs={{0,8},{8,16},{16,24},{1,9},{9,17},{17,25},{2,10},{10,18},{18,26},{... | collective-permute-start | bytes 393224 | tf_op jit(solution)/shard_map/ppermute | solution.py:89
  114.6 8.3 %copy-start = (pred[4,2,512,16,16]{2,1,4,3,0:T(4,128)(4,1)S(1)}, pred[4,2,512,16,16]{2,1,4,3,0:T(4,128)(4,1)}, u32[]{:S(2)}) copy-start(pred[4,2,512,16,16]{2,1,4,3,0:T(4,128)(4,1)} %broadcast_and_fusion) | copy-start | bytes 3145732
  126.6 95.5 %reduce-scatter.5.cloned.1.call-start = ((), (), s32[]{:S(2)}) async-start(), calls=%async_computation.3 | async-start | bytes 5898240 | tf_op jit(solution)/shard_map/reduce_scatter | solution.py:117
  157.5 0.7 copy-start.2
  157.5 64.6 %copy-start.1 = (bf16[1,128,3584]{2,1,0:T(8,128)(2,1)S(1)}, bf16[1,128,3584]{2,1,0:T(8,128)(2,1)}, u32[]{:S(2)}) copy-start(bf16[1,128,3584]{2,1,0:T(8,128)(2,1)} %param.8) | copy-start | bytes 2752516
Sparse Core Ops, SparseCore 0:
  9.6 76.1 all-gather.2
  126.8 34.3 reduce-scatter.2
  163.5 58.5 reduce-scatter.4

commit v11 on v10

--- a/solution.py
+++ b/solution.py
@@ -14,8 +14,10 @@
     for i in range(group):
         cols = slice(i * BLOCK, (i + 1) * BLOCK)
         rows = rows_ref[:, i].reshape(halves * rows_half, width)
-        acc = jnp.dot(rows, w_ref[:, cols], preferred_element_type=jnp.float32)
-        acc = acc + b_ref[:, cols]
+        acc_t = lax.dot_general(
+            w_ref[:, cols], rows, (((0,), (1,)), ((), ())), preferred_element_type=jnp.float32
+        )
+        acc = acc_t.T + b_ref[:, cols]
         o_ref[i] = jnp.maximum(acc, 0.0).astype(o_ref.dtype)
 
 

time: 233 us -> 234 us (level)
  no operation moved by 1% of the time
where the time goes in v11:
time: 234 us
  waiting for transfers between devices  121 us (52%)
  matrix products  49.8 us (21%)
  blocking collectives  14.4 us (6%)
  between operations  13.9 us (6%)
  other arithmetic  12.1 us (5%)
  Pallas kernels  9.35 us (4%)
  starting transfers between devices  8.34 us (4%)
  local copies, waits for them, and re-layouts  5.02 us (2%)
    reduce_scatter x2, waiting for transfers between devices, body(): lax.psum_scatter(partial, 'tok', scatter_dimension=0, tiled=True)  63.7 us
    all_gather x1, waiting for transfers between devices, body(): res_all = lax.all_gather(residual[0], 'tok', axis=0, tiled=True)  53.1 us
    dot_general x2, matrix products, body(): jnp.einsum('lbxe,lbed->lbxd', chunk_codes, weights[..., lo:hi], preferred...  27.6 us
    dot_general x2, matrix products, body(): jnp.einsum('lgtbx,lbgxd->gtd', combine, terms.reshape(layers, per_owner,...  15.2 us
    all_gather x1, blocking collectives, body(): codes_all = lax.all_gather(codes_own, 'tok', axis=1, tiled=True)  14.4 us
    pallas_call x1, Pallas kernels, encode(): pl.pallas_call(encode_kernel, grid=(per_owner // group,), in_specs=[pl.Bl...  9.35 us
    ppermute x3, starting transfers between devices, body(): lax.ppermute(codes, 'layer', [(i, i + shift) for i in range(layers - shif...  8.22 us
    dot_general x1, matrix products, body(): jnp.einsum('gtbx,gtd->gbxd', own_hits.reshape(halves, tokens // halves, p...  7.06 us
  transfers between devices with their start and end apart: 6, of which 4 were waited for; matrix products, arithmetic and copies ran while one was open for 18% of the time, Pallas kernels for 0%

profile of v11, /device:TPU:0, one launch (start us, length us, event | category | flops | bytes accessed | tf_op | source)
XLA Modules:
  0.0 233.9 jit_solution(5879310282921964775)
XLA Ops:
  7.2 0.7 all-gather.3.cloned.1.call-update
  7.9 0.8 copy.57
  8.9 0.4 convert_reduce_fusion
  9.3 0.1 copy.60
  9.5 0.7 fusion.31
  10.2 14.4 %all_gather.6 = s32[4,1024,2]{1,0,2:T(4,128)S(1)} all-gather(s32[4,128,2]{1,0,2:T(4,128)S(1)} %fusion.31), channel_id=1, replica_groups=mesh['layer'=4,'tok'=8] {'tok'}, dimensions={1}, use_global_device_ids=true | all-gather | bytes 36864 | tf_op jit(solution)/shard_map/all_gather | solution.py:66
  24.7 0.1 add_select_fusion.1
  25.0 0.1 iota_compare_fusion
  25.1 1.5 and_reduce_fusion
  26.7 1.9 reduce_or.12
  28.6 0.5 reshape.185
  29.1 3.6 %broadcast_and_fusion = pred[4,2,512,16,16]{2,1,4,3,0:T(4,128)(4,1)} fusion(pred[4,2,512,16,16]{2,1,4,3,0:T(4,128)(4,1)S(1)} %reduce_or.12, pred[4]{0:T(512)(128)(4,1)S(1)} %get-tuple-element.13), kind=kLoop, calls=%fused_computation.14 | loop fusion | flops 1048576 | bytes 2097156 | tf_op jit(solution)/shard_map/and | solution.py:98
  32.7 53.1 %all-gather.3.cloned.1.call-done = bf16[1,1024,3584]{2,1,0:T(8,128)(2,1)} async-done(((bf16[1,128,3584]{2,1,0:T(8,128)(2,1)}), bf16[1,1024,3584]{2,1,0:T(8,128)(2,1)}) %all-gather.3.cloned.1.call-update) | async-done | bytes 7340048 | tf_op jit(solution)/shard_map/all_gather | solution.py:81
  85.8 7.1 %convolution_convert_fusion.rows_ref = bf16[2,16,16,3584]{3,2,1,0:T(8,128)(2,1)} fusion(bf16[2,512,3584,1]{2,1,3,0:T(8,128)(2,1)} %bitcast.51, pred[2,512,16,16]{1,0,3,2:T(4,128)(4,1)S(1)} %reshape.185), kind=kOutput, calls=%fused_computation.10 | convolution fusion | flops 1880883200 | bytes 11272192 | tf_op jit(solution)/shard_map/gtbx,gtd->gbxd/dot_general | solution.py:83
  92.9 9.4 %shard_map.86 = bf16[16,32,128]{2,1,0:T(8,128)(2,1)} custom-call(bf16[2,16,16,3584]{3,2,1,0:T(8,128)(2,1)} %convolution_convert_fusion.rows_ref, bf16[3584,2048]{1,0:T(8,128)(2,1)} %bitcast.50, f32[1,2048]{1,0:T(1,128)} %b_ref.1), custom_call_target="tpu_custom_call" | custom-call | tf_op jit(solution)/shard_map/pallas_call | solution.py:27
  102.2 4.3 %collective-permute-start.2 = (bf16[16,32,128]{2,1,0:T(8,128)(2,1)}, bf16[16,32,128]{2,1,0:T(8,128)(2,1)S(1)}, u32[]{:S(2)}, u32[]{:S(2)}) collective-permute-start(bf16[16,32,128]{2,1,0:T(8,128)(2,1)} %shard_map.86), channel_id=1, source_target_pairs={{0,24},{1,25},{2,26},{3,27},{4,28},{5,29},{6,30},{7,31}} | collective-permute-start | bytes 393224 | tf_op jit(solution)/shard_map/ppermute | solution.py:91
  106.5 1.3 collective-permute-start.1
  107.8 2.7 %collective-permute-start = (bf16[16,32,128]{2,1,0:T(8,128)(2,1)}, bf16[16,32,128]{2,1,0:T(8,128)(2,1)S(1)}, u32[]{:S(2)}, u32[]{:S(2)}) collective-permute-start(bf16[16,32,128]{2,1,0:T(8,128)(2,1)} %shard_map.86), channel_id=1, source_target_pairs={{0,8},{8,16},{16,24},{1,9},{9,17},{17,25},{2,10},{10,18},{18,26},{... | collective-permute-start | bytes 393224 | tf_op jit(solution)/shard_map/ppermute | solution.py:91
  110.5 3.6 %collective-permute-done.1 = bf16[16,32,128]{2,1,0:T(8,128)(2,1)S(1)} collective-permute-done((bf16[16,32,128]{2,1,0:T(8,128)(2,1)}, bf16[16,32,128]{2,1,0:T(8,128)(2,1)S(1)}, u32[]{:S(2)}, u32[]{:S(2)}) %collective-permute-start.1) | collective-permute-done | bytes 131104 | tf_op jit(solution)/shard_map/ppermute | solution.py:91
  114.1 1.0 pad_maximum_fusion
  115.0 0.6 gather_fusion
  115.7 0.1 broadcast_select_fusion
  115.8 8.2 %fusion.13 = bf16[4,16,32,1024]{3,2,1,0:T(8,128)(2,1)S(1)} fusion(bf16[4,16,32,128]{3,2,1,0:T(8,128)(2,1)S(1)} %broadcast_select_fusion, bf16[4,16,128,3584]{3,2,1,0:T(8,128)(2,1)} %bitcast.47), kind=kOutput, calls=%fused_computation.15 | convolution fusion | flops 538968064 | bytes 21495808 | tf_op jit(solution)/shard_map/lbxe,lbed->lbxd/dot_general | solution.py:106
  124.1 3.7 %bitcast_convert_fusion.1 = bf16[2,512,1024]{2,1,0:T(8,128)(2,1)} fusion(bf16[4,16,2,16,1024]{4,3,2,1,0:T(8,128)(2,1)S(1)} %bitcast.53, pred[4,2,512,16,16]{2,1,4,3,0:T(4,128)(4,1)S(1)} %copy-done), kind=kOutput, calls=%fused_computation.11 | convolution fusion | flops 2148532224 | bytes 7340032 | tf_op jit(solution)/shard_map/lgtbx,lbgxd->gtd/dot_general | solution.py:112
  127.9 19.3 %fusion.6 = bf16[4,16,32,2560]{3,2,1,0:T(8,128)(2,1)} fusion(bf16[4,16,32,128]{3,2,1,0:T(8,128)(2,1)S(1)} %broadcast_select_fusion, bf16[4,16,128,3584]{3,2,1,0:T(8,128)(2,1)} %bitcast.48), kind=kOutput, calls=%fused_computation.9 | convolution fusion | flops 1347420160 | bytes 52953088 | tf_op jit(solution)/shard_map/lbxe,lbed->lbxd/dot_general | solution.py:106
  147.2 11.5 %bitcast_convert_fusion = bf16[2,512,2560]{2,1,0:T(8,128)(2,1)} fusion(bf16[4,16,2,16,2560]{4,3,2,1,0:T(8,128)(2,1)} %bitcast.49, pred[4,2,512,16,16]{2,1,4,3,0:T(4,128)(4,1)S(1)} %copy-done), kind=kOutput, calls=%fused_computation.5 | convolution fusion | flops 5371330560 | bytes 16777216 | tf_op jit(solution)/shard_map/lgtbx,lbgxd->gtd/dot_general | solution.py:112
  158.7 0.7 copy-done.2
  159.4 2.9 %reduce-scatter.3.cloned.1.call-done = bf16[128,1024]{1,0:T(8,128)(2,1)} async-done(((bf16[1024,1024]{1,0:T(8,128)(2,1)}), bf16[128,1024]{1,0:T(8,128)(2,1)}) %reduce-scatter.3.cloned.1.call-update) | async-done | bytes 262160 | tf_op jit(solution)/shard_map/reduce_scatter | solution.py:119
  162.3 60.8 %reduce-scatter.5.cloned.1.call-done = bf16[128,2560]{1,0:T(8,128)(2,1)} async-done(((bf16[1024,2560]{1,0:T(8,128)(2,1)}), bf16[128,2560]{1,0:T(8,128)(2,1)}) %reduce-scatter.5.cloned.1.call-update) | async-done | bytes 655376 | tf_op jit(solution)/shard_map/reduce_scatter | solution.py:119
  223.1 1.6 fusion.19
  224.7 0.5 multiply_bitcast_fusion
  225.2 2.2 add_convert_fusion
  (27 shorter events, 0.6 us)
Async XLA Ops:
  7.2 78.6 %all-gather.3.cloned.1.call-start = ((), (), s32[]{:S(2)}) async-start(), calls=%async_computation.4 | async-start | bytes 8257536 | tf_op jit(solution)/shard_map/all_gather | solution.py:81
  7.9 154.4 %reduce-scatter.3.cloned.1.call-start = ((), (), s32[]{:S(2)}) async-start(), calls=%async_computation.2 | async-start | bytes 2359296 | tf_op jit(solution)/shard_map/reduce_scatter | solution.py:119
  102.2 8.3 %collective-permute-start.2 = (bf16[16,32,128]{2,1,0:T(8,128)(2,1)}, bf16[16,32,128]{2,1,0:T(8,128)(2,1)S(1)}, u32[]{:S(2)}, u32[]{:S(2)}) collective-permute-start(bf16[16,32,128]{2,1,0:T(8,128)(2,1)} %shard_map.86), channel_id=1, source_target_pairs={{0,24},{1,25},{2,26},{3,27},{4,28},{5,29},{6,30},{7,31}} | collective-permute-start | bytes 393224 | tf_op jit(solution)/shard_map/ppermute | solution.py:91
  106.5 7.6 %collective-permute-start.1 = (bf16[16,32,128]{2,1,0:T(8,128)(2,1)}, bf16[16,32,128]{2,1,0:T(8,128)(2,1)S(1)}, u32[]{:S(2)}, u32[]{:S(2)}) collective-permute-start(bf16[16,32,128]{2,1,0:T(8,128)(2,1)} %shard_map.86), channel_id=1, source_target_pairs={{0,16},{8,24},{1,17},{9,25},{2,18},{10,26},{3,19},{11,27},{4,20},{... | collective-permute-start | bytes 393224 | tf_op jit(solution)/shard_map/ppermute | solution.py:91
  107.8 6.3 %collective-permute-start = (bf16[16,32,128]{2,1,0:T(8,128)(2,1)}, bf16[16,32,128]{2,1,0:T(8,128)(2,1)S(1)}, u32[]{:S(2)}, u32[]{:S(2)}) collective-permute-start(bf16[16,32,128]{2,1,0:T(8,128)(2,1)} %shard_map.86), channel_id=1, source_target_pairs={{0,8},{8,16},{16,24},{1,9},{9,17},{17,25},{2,10},{10,18},{18,26},{... | collective-permute-start | bytes 393224 | tf_op jit(solution)/shard_map/ppermute | solution.py:91
  115.8 8.3 %copy-start = (pred[4,2,512,16,16]{2,1,4,3,0:T(4,128)(4,1)S(1)}, pred[4,2,512,16,16]{2,1,4,3,0:T(4,128)(4,1)}, u32[]{:S(2)}) copy-start(pred[4,2,512,16,16]{2,1,4,3,0:T(4,128)(4,1)} %broadcast_and_fusion) | copy-start | bytes 3145732
  127.8 95.3 %reduce-scatter.5.cloned.1.call-start = ((), (), s32[]{:S(2)}) async-start(), calls=%async_computation.3 | async-start | bytes 5898240 | tf_op jit(solution)/shard_map/reduce_scatter | solution.py:119
  158.7 0.7 copy-start.2
  158.7 64.4 %copy-start.1 = (bf16[1,128,3584]{2,1,0:T(8,128)(2,1)S(1)}, bf16[1,128,3584]{2,1,0:T(8,128)(2,1)}, u32[]{:S(2)}) copy-start(bf16[1,128,3584]{2,1,0:T(8,128)(2,1)} %param.8) | copy-start | bytes 2752516
Sparse Core Ops, SparseCore 0:
  9.6 76.1 all-gather.2
  127.9 34.3 reduce-scatter.2
  164.6 58.4 reduce-scatter.4

commit v12 on v10

--- a/solution.py
+++ b/solution.py
@@ -21,7 +21,7 @@
 
 def encode(rows, weight, bias):
     halves, per_owner, rows_half, width = rows.shape
-    group = math.gcd(per_owner, 4)
+    group = math.gcd(per_owner, 8)
     return pl.pallas_call(
         encode_kernel,
         grid=(per_owner // group,),

time: 233 us -> 234 us (level)
  no operation moved by 1% of the time
where the time goes in v12:
time: 234 us
  waiting for transfers between devices  121 us (52%)
  matrix products  49.8 us (21%)
  blocking collectives  14.4 us (6%)
  between operations  13.9 us (6%)
  other arithmetic  12.1 us (5%)
  Pallas kernels  9.11 us (4%)
  starting transfers between devices  8.34 us (4%)
  local copies, waits for them, and re-layouts  5.02 us (2%)
    reduce_scatter x2, waiting for transfers between devices, body(): lax.psum_scatter(partial, 'tok', scatter_dimension=0, tiled=True)  63.6 us
    all_gather x1, waiting for transfers between devices, body(): res_all = lax.all_gather(residual[0], 'tok', axis=0, tiled=True)  53.1 us
    dot_general x2, matrix products, body(): jnp.einsum('lbxe,lbed->lbxd', chunk_codes, weights[..., lo:hi], preferred...  27.6 us
    dot_general x2, matrix products, body(): jnp.einsum('lgtbx,lbgxd->gtd', combine, terms.reshape(layers, per_owner,...  15.2 us
    all_gather x1, blocking collectives, body(): codes_all = lax.all_gather(codes_own, 'tok', axis=1, tiled=True)  14.4 us
    pallas_call x1, Pallas kernels, encode(): pl.pallas_call(encode_kernel, grid=(per_owner // group,), in_specs=[pl.Bl...  9.11 us
    ppermute x3, starting transfers between devices, body(): lax.ppermute(codes, 'layer', [(i, i + shift) for i in range(layers - shif...  8.22 us
    dot_general x1, matrix products, body(): jnp.einsum('gtbx,gtd->gbxd', own_hits.reshape(halves, tokens // halves, p...  7.06 us
  transfers between devices with their start and end apart: 6, of which 4 were waited for; matrix products, arithmetic and copies ran while one was open for 18% of the time, Pallas kernels for 0%

profile of v12, /device:TPU:0, one launch (start us, length us, event | category | flops | bytes accessed | tf_op | source)
XLA Modules:
  0.0 233.7 jit_solution(10474877264098945426)
XLA Ops:
  7.2 0.7 all-gather.3.cloned.1.call-update
  7.9 0.8 copy.57
  8.9 0.4 convert_reduce_fusion
  9.3 0.1 copy.60
  9.5 0.7 fusion.31
  10.2 14.4 %all_gather.6 = s32[4,1024,2]{1,0,2:T(4,128)S(1)} all-gather(s32[4,128,2]{1,0,2:T(4,128)S(1)} %fusion.31), channel_id=1, replica_groups=mesh['layer'=4,'tok'=8] {'tok'}, dimensions={1}, use_global_device_ids=true | all-gather | bytes 36864 | tf_op jit(solution)/shard_map/all_gather | solution.py:64
  24.7 0.1 add_select_fusion.1
  25.0 0.1 iota_compare_fusion
  25.1 1.5 and_reduce_fusion
  26.7 1.9 reduce_or.12
  28.6 0.5 reshape.185
  29.1 3.6 %broadcast_and_fusion = pred[4,2,512,16,16]{2,1,4,3,0:T(4,128)(4,1)} fusion(pred[4,2,512,16,16]{2,1,4,3,0:T(4,128)(4,1)S(1)} %reduce_or.12, pred[4]{0:T(512)(128)(4,1)S(1)} %get-tuple-element.13), kind=kLoop, calls=%fused_computation.14 | loop fusion | flops 1048576 | bytes 2097156 | tf_op jit(solution)/shard_map/and | solution.py:96
  32.7 53.1 %all-gather.3.cloned.1.call-done = bf16[1,1024,3584]{2,1,0:T(8,128)(2,1)} async-done(((bf16[1,128,3584]{2,1,0:T(8,128)(2,1)}), bf16[1,1024,3584]{2,1,0:T(8,128)(2,1)}) %all-gather.3.cloned.1.call-update) | async-done | bytes 7340048 | tf_op jit(solution)/shard_map/all_gather | solution.py:79
  85.8 7.1 %convolution_convert_fusion.rows_ref = bf16[2,16,16,3584]{3,2,1,0:T(8,128)(2,1)} fusion(bf16[2,512,3584,1]{2,1,3,0:T(8,128)(2,1)} %bitcast.51, pred[2,512,16,16]{1,0,3,2:T(4,128)(4,1)S(1)} %reshape.185), kind=kOutput, calls=%fused_computation.10 | convolution fusion | flops 1880883200 | bytes 11272192 | tf_op jit(solution)/shard_map/gtbx,gtd->gbxd/dot_general | solution.py:81
  92.9 9.1 %shard_map.86 = bf16[16,32,128]{2,1,0:T(8,128)(2,1)} custom-call(bf16[2,16,16,3584]{3,2,1,0:T(8,128)(2,1)} %convolution_convert_fusion.rows_ref, bf16[3584,2048]{1,0:T(8,128)(2,1)} %bitcast.50, f32[1,2048]{1,0:T(1,128)} %b_ref.1), custom_call_target="tpu_custom_call" | custom-call | tf_op jit(solution)/shard_map/pallas_call | solution.py:25
  102.0 4.3 %collective-permute-start.2 = (bf16[16,32,128]{2,1,0:T(8,128)(2,1)}, bf16[16,32,128]{2,1,0:T(8,128)(2,1)S(1)}, u32[]{:S(2)}, u32[]{:S(2)}) collective-permute-start(bf16[16,32,128]{2,1,0:T(8,128)(2,1)} %shard_map.86), channel_id=1, source_target_pairs={{0,24},{1,25},{2,26},{3,27},{4,28},{5,29},{6,30},{7,31}} | collective-permute-start | bytes 393224 | tf_op jit(solution)/shard_map/ppermute | solution.py:89
  106.3 1.3 collective-permute-start.1
  107.6 2.7 %collective-permute-start = (bf16[16,32,128]{2,1,0:T(8,128)(2,1)}, bf16[16,32,128]{2,1,0:T(8,128)(2,1)S(1)}, u32[]{:S(2)}, u32[]{:S(2)}) collective-permute-start(bf16[16,32,128]{2,1,0:T(8,128)(2,1)} %shard_map.86), channel_id=1, source_target_pairs={{0,8},{8,16},{16,24},{1,9},{9,17},{17,25},{2,10},{10,18},{18,26},{... | collective-permute-start | bytes 393224 | tf_op jit(solution)/shard_map/ppermute | solution.py:89
  110.3 3.6 %collective-permute-done.1 = bf16[16,32,128]{2,1,0:T(8,128)(2,1)S(1)} collective-permute-done((bf16[16,32,128]{2,1,0:T(8,128)(2,1)}, bf16[16,32,128]{2,1,0:T(8,128)(2,1)S(1)}, u32[]{:S(2)}, u32[]{:S(2)}) %collective-permute-start.1) | collective-permute-done | bytes 131104 | tf_op jit(solution)/shard_map/ppermute | solution.py:89
  113.8 1.0 pad_maximum_fusion
  114.8 0.6 gather_fusion
  115.5 0.1 broadcast_select_fusion
  115.6 8.2 %fusion.13 = bf16[4,16,32,1024]{3,2,1,0:T(8,128)(2,1)S(1)} fusion(bf16[4,16,32,128]{3,2,1,0:T(8,128)(2,1)S(1)} %broadcast_select_fusion, bf16[4,16,128,3584]{3,2,1,0:T(8,128)(2,1)} %bitcast.47), kind=kOutput, calls=%fused_computation.15 | convolution fusion | flops 538968064 | bytes 21495808 | tf_op jit(solution)/shard_map/lbxe,lbed->lbxd/dot_general | solution.py:104
  123.8 3.7 %bitcast_convert_fusion.1 = bf16[2,512,1024]{2,1,0:T(8,128)(2,1)} fusion(bf16[4,16,2,16,1024]{4,3,2,1,0:T(8,128)(2,1)S(1)} %bitcast.53, pred[4,2,512,16,16]{2,1,4,3,0:T(4,128)(4,1)S(1)} %copy-done), kind=kOutput, calls=%fused_computation.11 | convolution fusion | flops 2148532224 | bytes 7340032 | tf_op jit(solution)/shard_map/lgtbx,lbgxd->gtd/dot_general | solution.py:110
  127.6 19.3 %fusion.6 = bf16[4,16,32,2560]{3,2,1,0:T(8,128)(2,1)} fusion(bf16[4,16,32,128]{3,2,1,0:T(8,128)(2,1)S(1)} %broadcast_select_fusion, bf16[4,16,128,3584]{3,2,1,0:T(8,128)(2,1)} %bitcast.48), kind=kOutput, calls=%fused_computation.9 | convolution fusion | flops 1347420160 | bytes 52953088 | tf_op jit(solution)/shard_map/lbxe,lbed->lbxd/dot_general | solution.py:104
  147.0 11.5 %bitcast_convert_fusion = bf16[2,512,2560]{2,1,0:T(8,128)(2,1)} fusion(bf16[4,16,2,16,2560]{4,3,2,1,0:T(8,128)(2,1)} %bitcast.49, pred[4,2,512,16,16]{2,1,4,3,0:T(4,128)(4,1)S(1)} %copy-done), kind=kOutput, calls=%fused_computation.5 | convolution fusion | flops 5371330560 | bytes 16777216 | tf_op jit(solution)/shard_map/lgtbx,lbgxd->gtd/dot_general | solution.py:110
  158.5 0.7 copy-done.2
  159.2 3.0 %reduce-scatter.3.cloned.1.call-done = bf16[128,1024]{1,0:T(8,128)(2,1)} async-done(((bf16[1024,1024]{1,0:T(8,128)(2,1)}), bf16[128,1024]{1,0:T(8,128)(2,1)}) %reduce-scatter.3.cloned.1.call-update) | async-done | bytes 262160 | tf_op jit(solution)/shard_map/reduce_scatter | solution.py:117
  162.2 60.6 %reduce-scatter.5.cloned.1.call-done = bf16[128,2560]{1,0:T(8,128)(2,1)} async-done(((bf16[1024,2560]{1,0:T(8,128)(2,1)}), bf16[128,2560]{1,0:T(8,128)(2,1)}) %reduce-scatter.5.cloned.1.call-update) | async-done | bytes 655376 | tf_op jit(solution)/shard_map/reduce_scatter | solution.py:117
  222.8 1.6 fusion.19
  224.4 0.5 multiply_bitcast_fusion
  224.9 2.2 add_convert_fusion
  (27 shorter events, 0.6 us)
Async XLA Ops:
  7.2 78.6 %all-gather.3.cloned.1.call-start = ((), (), s32[]{:S(2)}) async-start(), calls=%async_computation.4 | async-start | bytes 8257536 | tf_op jit(solution)/shard_map/all_gather | solution.py:79
  7.9 154.3 %reduce-scatter.3.cloned.1.call-start = ((), (), s32[]{:S(2)}) async-start(), calls=%async_computation.2 | async-start | bytes 2359296 | tf_op jit(solution)/shard_map/reduce_scatter | solution.py:117
  102.0 8.3 %collective-permute-start.2 = (bf16[16,32,128]{2,1,0:T(8,128)(2,1)}, bf16[16,32,128]{2,1,0:T(8,128)(2,1)S(1)}, u32[]{:S(2)}, u32[]{:S(2)}) collective-permute-start(bf16[16,32,128]{2,1,0:T(8,128)(2,1)} %shard_map.86), channel_id=1, source_target_pairs={{0,24},{1,25},{2,26},{3,27},{4,28},{5,29},{6,30},{7,31}} | collective-permute-start | bytes 393224 | tf_op jit(solution)/shard_map/ppermute | solution.py:89
  106.3 7.6 %collective-permute-start.1 = (bf16[16,32,128]{2,1,0:T(8,128)(2,1)}, bf16[16,32,128]{2,1,0:T(8,128)(2,1)S(1)}, u32[]{:S(2)}, u32[]{:S(2)}) collective-permute-start(bf16[16,32,128]{2,1,0:T(8,128)(2,1)} %shard_map.86), channel_id=1, source_target_pairs={{0,16},{8,24},{1,17},{9,25},{2,18},{10,26},{3,19},{11,27},{4,20},{... | collective-permute-start | bytes 393224 | tf_op jit(solution)/shard_map/ppermute | solution.py:89
  107.6 6.3 %collective-permute-start = (bf16[16,32,128]{2,1,0:T(8,128)(2,1)}, bf16[16,32,128]{2,1,0:T(8,128)(2,1)S(1)}, u32[]{:S(2)}, u32[]{:S(2)}) collective-permute-start(bf16[16,32,128]{2,1,0:T(8,128)(2,1)} %shard_map.86), channel_id=1, source_target_pairs={{0,8},{8,16},{16,24},{1,9},{9,17},{17,25},{2,10},{10,18},{18,26},{... | collective-permute-start | bytes 393224 | tf_op jit(solution)/shard_map/ppermute | solution.py:89
  115.6 8.3 %copy-start = (pred[4,2,512,16,16]{2,1,4,3,0:T(4,128)(4,1)S(1)}, pred[4,2,512,16,16]{2,1,4,3,0:T(4,128)(4,1)}, u32[]{:S(2)}) copy-start(pred[4,2,512,16,16]{2,1,4,3,0:T(4,128)(4,1)} %broadcast_and_fusion) | copy-start | bytes 3145732
  127.6 95.2 %reduce-scatter.5.cloned.1.call-start = ((), (), s32[]{:S(2)}) async-start(), calls=%async_computation.3 | async-start | bytes 5898240 | tf_op jit(solution)/shard_map/reduce_scatter | solution.py:117
  158.4 0.7 copy-start.2
  158.4 64.4 %copy-start.1 = (bf16[1,128,3584]{2,1,0:T(8,128)(2,1)S(1)}, bf16[1,128,3584]{2,1,0:T(8,128)(2,1)}, u32[]{:S(2)}) copy-start(bf16[1,128,3584]{2,1,0:T(8,128)(2,1)} %param.8) | copy-start | bytes 2752516
Sparse Core Ops, SparseCore 0:
  9.6 76.1 all-gather.2
  127.7 34.4 reduce-scatter.2
  164.5 58.2 reduce-scatter.4

commit v13 on v10

--- a/solution.py
+++ b/solution.py
@@ -78,9 +78,11 @@
 
     res_all = lax.all_gather(residual[0], "tok", axis=0, tiled=True)
     own_hits = lax.dynamic_index_in_dim(hits, layer_index, 0, keepdims=False).astype(jnp.bfloat16)
+    own_hits = own_hits.reshape(halves, tokens // halves, per_owner, rows_half).transpose(0, 2, 3, 1)
+    own_hits = lax.optimization_barrier(own_hits)
     rows = jnp.einsum(
-        "gtbx,gtd->gbxd",
-        own_hits.reshape(halves, tokens // halves, per_owner, rows_half),
+        "gbxt,gtd->gbxd",
+        own_hits,
         res_all.reshape(halves, tokens // halves, width),
         preferred_element_type=jnp.float32,
     ).astype(jnp.bfloat16)

time: 233 us -> 233 us (level)
  no operation moved by 1% of the time
where the time goes in v13:
time: 233 us
  waiting for transfers between devices  119 us (51%)
  matrix products  49.8 us (21%)
  blocking collectives  14.4 us (6%)
  between operations  13.9 us (6%)
  other arithmetic  12.9 us (6%)
  starting transfers between devices  8.34 us (4%)
  Pallas kernels  8.17 us (4%)
  local copies, waits for them, and re-layouts  5.93 us (3%)
    reduce_scatter x2, waiting for transfers between devices, body(): lax.psum_scatter(partial, 'tok', scatter_dimension=0, tiled=True)  63.8 us
    all_gather x1, waiting for transfers between devices, body(): res_all = lax.all_gather(residual[0], 'tok', axis=0, tiled=True)  51.3 us
    dot_general x2, matrix products, body(): jnp.einsum('lbxe,lbed->lbxd', chunk_codes, weights[..., lo:hi], preferred...  27.6 us
    dot_general x2, matrix products, body(): jnp.einsum('lgtbx,lbgxd->gtd', combine, terms.reshape(layers, per_owner,...  15.2 us
    all_gather x1, blocking collectives, body(): codes_all = lax.all_gather(codes_own, 'tok', axis=1, tiled=True)  14.4 us
    ppermute x3, starting transfers between devices, body(): lax.ppermute(codes, 'layer', [(i, i + shift) for i in range(layers - shif...  8.22 us
    pallas_call x1, Pallas kernels, encode(): pl.pallas_call(encode_kernel, grid=(per_owner // group,), in_specs=[pl.Bl...  8.17 us
    dot_general x1, matrix products, body(): jnp.einsum('gbxt,gtd->gbxd', own_hits, res_all.reshape(halves, tokens //...  7.06 us
  transfers between devices with their start and end apart: 6, of which 4 were waited for; matrix products, arithmetic and copies ran while one was open for 18% of the time, Pallas kernels for 0%

profile of v13, /device:TPU:0, one launch (start us, length us, event | category | flops | bytes accessed | tf_op | source)
XLA Modules:
  0.0 232.9 jit_solution(17151579292772959695)
XLA Ops:
  7.2 0.7 all-gather.3.cloned.1.call-update
  7.9 0.8 copy.57
  8.9 0.4 convert_reduce_fusion
  9.3 0.1 copy.60
  9.5 0.7 fusion.31
  10.2 14.4 %all_gather.6 = s32[4,1024,2]{1,0,2:T(4,128)S(1)} all-gather(s32[4,128,2]{1,0,2:T(4,128)S(1)} %fusion.31), channel_id=1, replica_groups=mesh['layer'=4,'tok'=8] {'tok'}, dimensions={1}, use_global_device_ids=true | all-gather | bytes 36864 | tf_op jit(solution)/shard_map/all_gather | solution.py:64
  24.7 0.1 add_select_fusion.1
  25.0 0.1 iota_compare_fusion
  25.1 1.5 and_reduce_fusion
  26.7 1.9 reduce_or.12
  28.5 0.9 dynamic-slice_convert_fusion
  29.4 1.4 reshape.189
  30.9 3.6 %broadcast_and_fusion = pred[4,2,512,16,16]{2,1,4,3,0:T(4,128)(4,1)} fusion(pred[4,2,512,16,16]{2,1,4,3,0:T(4,128)(4,1)S(1)} %reduce_or.12, pred[4]{0:T(512)(128)(4,1)S(1)} %get-tuple-element.13), kind=kLoop, calls=%fused_computation.14 | loop fusion | flops 1048576 | bytes 2097156 | tf_op jit(solution)/shard_map/and | solution.py:98
  34.5 51.3 %all-gather.3.cloned.1.call-done = bf16[1,1024,3584]{2,1,0:T(8,128)(2,1)} async-done(((bf16[1,128,3584]{2,1,0:T(8,128)(2,1)}), bf16[1,1024,3584]{2,1,0:T(8,128)(2,1)}) %all-gather.3.cloned.1.call-update) | async-done | bytes 7340048 | tf_op jit(solution)/shard_map/all_gather | solution.py:79
  85.8 7.1 %convolution_convert_fusion.rows_ref = bf16[2,16,16,3584]{3,2,1,0:T(8,128)(2,1)} fusion(bf16[2,512,3584,1]{2,1,3,0:T(8,128)(2,1)} %bitcast.64, bf16[2,16,16,512]{3,0,2,1:T(2,128)(2,1)S(1)} %bitcast.58), kind=kOutput, calls=%fused_computation.10 | convolution fusion | flops 1880883200 | bytes 11534336 | tf_op jit(solution)/shard_map/gbxt,gtd->gbxd/dot_general | solution.py:83
  92.9 8.2 %shard_map.86 = bf16[16,32,128]{2,1,0:T(8,128)(2,1)} custom-call(bf16[2,16,16,3584]{3,2,1,0:T(8,128)(2,1)} %convolution_convert_fusion.rows_ref, bf16[3584,2048]{1,0:T(8,128)(2,1)} %bitcast.51, f32[1,2048]{1,0:T(1,128)} %b_ref.1), custom_call_target="tpu_custom_call" | custom-call | tf_op jit(solution)/shard_map/pallas_call | solution.py:25
  101.0 4.3 %collective-permute-start.2 = (bf16[16,32,128]{2,1,0:T(8,128)(2,1)}, bf16[16,32,128]{2,1,0:T(8,128)(2,1)S(1)}, u32[]{:S(2)}, u32[]{:S(2)}) collective-permute-start(bf16[16,32,128]{2,1,0:T(8,128)(2,1)} %shard_map.86), channel_id=1, source_target_pairs={{0,24},{1,25},{2,26},{3,27},{4,28},{5,29},{6,30},{7,31}} | collective-permute-start | bytes 393224 | tf_op jit(solution)/shard_map/ppermute | solution.py:91
  105.3 1.3 collective-permute-start.1
  106.6 2.7 %collective-permute-start = (bf16[16,32,128]{2,1,0:T(8,128)(2,1)}, bf16[16,32,128]{2,1,0:T(8,128)(2,1)S(1)}, u32[]{:S(2)}, u32[]{:S(2)}) collective-permute-start(bf16[16,32,128]{2,1,0:T(8,128)(2,1)} %shard_map.86), channel_id=1, source_target_pairs={{0,8},{8,16},{16,24},{1,9},{9,17},{17,25},{2,10},{10,18},{18,26},{... | collective-permute-start | bytes 393224 | tf_op jit(solution)/shard_map/ppermute | solution.py:91
  109.3 3.6 %collective-permute-done.1 = bf16[16,32,128]{2,1,0:T(8,128)(2,1)S(1)} collective-permute-done((bf16[16,32,128]{2,1,0:T(8,128)(2,1)}, bf16[16,32,128]{2,1,0:T(8,128)(2,1)S(1)}, u32[]{:S(2)}, u32[]{:S(2)}) %collective-permute-start.1) | collective-permute-done | bytes 131104 | tf_op jit(solution)/shard_map/ppermute | solution.py:91
  112.9 1.0 pad_maximum_fusion
  113.9 0.6 gather_fusion
  114.7 8.2 %fusion.13 = bf16[4,16,32,1024]{3,2,1,0:T(8,128)(2,1)S(1)} fusion(bf16[4,16,32,128]{3,2,1,0:T(8,128)(2,1)S(1)} %broadcast_select_fusion, bf16[4,16,128,3584]{3,2,1,0:T(8,128)(2,1)} %bitcast.48), kind=kOutput, calls=%fused_computation.15 | convolution fusion | flops 538968064 | bytes 21495808 | tf_op jit(solution)/shard_map/lbxe,lbed->lbxd/dot_general | solution.py:106
  122.9 3.7 %bitcast_convert_fusion.1 = bf16[2,512,1024]{2,1,0:T(8,128)(2,1)} fusion(bf16[4,16,2,16,1024]{4,3,2,1,0:T(8,128)(2,1)S(1)} %bitcast.53, pred[4,2,512,16,16]{2,1,4,3,0:T(4,128)(4,1)S(1)} %copy-done), kind=kOutput, calls=%fused_computation.11 | convolution fusion | flops 2148532224 | bytes 7340032 | tf_op jit(solution)/shard_map/lgtbx,lbgxd->gtd/dot_general | solution.py:112
  126.7 19.3 %fusion.6 = bf16[4,16,32,2560]{3,2,1,0:T(8,128)(2,1)} fusion(bf16[4,16,32,128]{3,2,1,0:T(8,128)(2,1)S(1)} %broadcast_select_fusion, bf16[4,16,128,3584]{3,2,1,0:T(8,128)(2,1)} %bitcast.49), kind=kOutput, calls=%fused_computation.9 | convolution fusion | flops 1347420160 | bytes 52953088 | tf_op jit(solution)/shard_map/lbxe,lbed->lbxd/dot_general | solution.py:106
  146.0 11.5 %bitcast_convert_fusion = bf16[2,512,2560]{2,1,0:T(8,128)(2,1)} fusion(bf16[4,16,2,16,2560]{4,3,2,1,0:T(8,128)(2,1)} %bitcast.50, pred[4,2,512,16,16]{2,1,4,3,0:T(4,128)(4,1)S(1)} %copy-done), kind=kOutput, calls=%fused_computation.5 | convolution fusion | flops 5371330560 | bytes 16777216 | tf_op jit(solution)/shard_map/lgtbx,lbgxd->gtd/dot_general | solution.py:112
  157.5 0.7 copy-done.2
  158.3 2.9 %reduce-scatter.3.cloned.1.call-done = bf16[128,1024]{1,0:T(8,128)(2,1)} async-done(((bf16[1024,1024]{1,0:T(8,128)(2,1)}), bf16[128,1024]{1,0:T(8,128)(2,1)}) %reduce-scatter.3.cloned.1.call-update) | async-done | bytes 262160 | tf_op jit(solution)/shard_map/reduce_scatter | solution.py:119
  161.2 60.9 %reduce-scatter.5.cloned.1.call-done = bf16[128,2560]{1,0:T(8,128)(2,1)} async-done(((bf16[1024,2560]{1,0:T(8,128)(2,1)}), bf16[128,2560]{1,0:T(8,128)(2,1)}) %reduce-scatter.5.cloned.1.call-update) | async-done | bytes 655376 | tf_op jit(solution)/shard_map/reduce_scatter | solution.py:119
  222.1 1.6 fusion.19
  223.7 0.5 multiply_bitcast_fusion
  224.2 2.2 add_convert_fusion
  (27 shorter events, 0.7 us)
Async XLA Ops:
  7.2 78.6 %all-gather.3.cloned.1.call-start = ((), (), s32[]{:S(2)}) async-start(), calls=%async_computation.4 | async-start | bytes 8257536 | tf_op jit(solution)/shard_map/all_gather | solution.py:79
  7.9 153.3 %reduce-scatter.3.cloned.1.call-start = ((), (), s32[]{:S(2)}) async-start(), calls=%async_computation.2 | async-start | bytes 2359296 | tf_op jit(solution)/shard_map/reduce_scatter | solution.py:119
  101.0 8.3 %collective-permute-start.2 = (bf16[16,32,128]{2,1,0:T(8,128)(2,1)}, bf16[16,32,128]{2,1,0:T(8,128)(2,1)S(1)}, u32[]{:S(2)}, u32[]{:S(2)}) collective-permute-start(bf16[16,32,128]{2,1,0:T(8,128)(2,1)} %shard_map.86), channel_id=1, source_target_pairs={{0,24},{1,25},{2,26},{3,27},{4,28},{5,29},{6,30},{7,31}} | collective-permute-start | bytes 393224 | tf_op jit(solution)/shard_map/ppermute | solution.py:91
  105.3 7.6 %collective-permute-start.1 = (bf16[16,32,128]{2,1,0:T(8,128)(2,1)}, bf16[16,32,128]{2,1,0:T(8,128)(2,1)S(1)}, u32[]{:S(2)}, u32[]{:S(2)}) collective-permute-start(bf16[16,32,128]{2,1,0:T(8,128)(2,1)} %shard_map.86), channel_id=1, source_target_pairs={{0,16},{8,24},{1,17},{9,25},{2,18},{10,26},{3,19},{11,27},{4,20},{... | collective-permute-start | bytes 393224 | tf_op jit(solution)/shard_map/ppermute | solution.py:91
  106.6 6.3 %collective-permute-start = (bf16[16,32,128]{2,1,0:T(8,128)(2,1)}, bf16[16,32,128]{2,1,0:T(8,128)(2,1)S(1)}, u32[]{:S(2)}, u32[]{:S(2)}) collective-permute-start(bf16[16,32,128]{2,1,0:T(8,128)(2,1)} %shard_map.86), channel_id=1, source_target_pairs={{0,8},{8,16},{16,24},{1,9},{9,17},{17,25},{2,10},{10,18},{18,26},{... | collective-permute-start | bytes 393224 | tf_op jit(solution)/shard_map/ppermute | solution.py:91
  114.6 8.3 %copy-start = (pred[4,2,512,16,16]{2,1,4,3,0:T(4,128)(4,1)S(1)}, pred[4,2,512,16,16]{2,1,4,3,0:T(4,128)(4,1)}, u32[]{:S(2)}) copy-start(pred[4,2,512,16,16]{2,1,4,3,0:T(4,128)(4,1)} %broadcast_and_fusion) | copy-start | bytes 3145732
  126.7 95.4 %reduce-scatter.5.cloned.1.call-start = ((), (), s32[]{:S(2)}) async-start(), calls=%async_computation.3 | async-start | bytes 5898240 | tf_op jit(solution)/shard_map/reduce_scatter | solution.py:119
  157.5 0.7 copy-start.2
  157.5 64.6 %copy-start.1 = (bf16[1,128,3584]{2,1,0:T(8,128)(2,1)S(1)}, bf16[1,128,3584]{2,1,0:T(8,128)(2,1)}, u32[]{:S(2)}) copy-start(bf16[1,128,3584]{2,1,0:T(8,128)(2,1)} %param.8) | copy-start | bytes 2752516
Sparse Core Ops, SparseCore 0:
  9.6 76.1 all-gather.2
  126.8 34.3 reduce-scatter.2
  163.5 58.5 reduce-scatter.4

commit v14 on v13

--- a/solution.py
+++ b/solution.py
@@ -98,7 +98,7 @@
     combine = (hits & valid[:, None, None, None]).astype(jnp.bfloat16)
     combine = combine.reshape(layers, halves, tokens // halves, per_owner, rows_half)
     weights = decoder_weight[0].reshape(layers, per_owner, BLOCK, width)
-    cut = (width // BLOCK) * 2 // 7 * BLOCK if width % BLOCK == 0 else 0
+    cut = (width // BLOCK) // 4 * BLOCK if width % BLOCK == 0 else 0
     bounds = [0, cut, width] if 0 < cut < width else [0, width]
     pieces = []
     chunk_codes = gathered

time: 233 us -> 234 us (level)
  transfers between devices with their start and end apart: 6 -> 6, of which waited for: 4 -> 3; matrix products, arithmetic and copies ran while one was open for 18% -> 19% of each run, Pallas kernels for 0% -> 0%
where the time goes in v14:
time: 234 us
  waiting for transfers between devices  118 us (50%)
  matrix products  51.5 us (22%)
  blocking collectives  14.4 us (6%)
  between operations  13.9 us (6%)
  other arithmetic  12.9 us (6%)
  starting transfers between devices  8.34 us (4%)
  Pallas kernels  8.17 us (3%)
  local copies, waits for them, and re-layouts  5.93 us (3%)
    reduce_scatter x2, waiting for transfers between devices, body(): lax.psum_scatter(partial, 'tok', scatter_dimension=0, tiled=True)  62.7 us
    all_gather x1, waiting for transfers between devices, body(): res_all = lax.all_gather(residual[0], 'tok', axis=0, tiled=True)  51.3 us
    dot_general x2, matrix products, body(): jnp.einsum('lbxe,lbed->lbxd', chunk_codes, weights[..., lo:hi], preferred...  28.7 us
    dot_general x2, matrix products, body(): jnp.einsum('lgtbx,lbgxd->gtd', combine, terms.reshape(layers, per_owner,...  15.8 us
    all_gather x1, blocking collectives, body(): codes_all = lax.all_gather(codes_own, 'tok', axis=1, tiled=True)  14.4 us
    ppermute x3, starting transfers between devices, body(): lax.ppermute(codes, 'layer', [(i, i + shift) for i in range(layers - shif...  8.22 us
    pallas_call x1, Pallas kernels, encode(): pl.pallas_call(encode_kernel, grid=(per_owner // group,), in_specs=[pl.Bl...  8.17 us
    dot_general x1, matrix products, body(): jnp.einsum('gbxt,gtd->gbxd', own_hits, res_all.reshape(halves, tokens //...  7.06 us
  transfers between devices with their start and end apart: 6, of which 3 were waited for; matrix products, arithmetic and copies ran while one was open for 19% of the time, Pallas kernels for 0%

profile of v14, /device:TPU:0, one launch (start us, length us, event | category | flops | bytes accessed | tf_op | source)
XLA Modules:
  0.0 233.6 jit_solution(2343974740762697245)
XLA Ops:
  7.2 0.7 all-gather.3.cloned.1.call-update
  7.9 0.8 copy.57
  8.9 0.4 convert_reduce_fusion
  9.3 0.1 copy.60
  9.5 0.7 fusion.31
  10.2 14.4 %all_gather.6 = s32[4,1024,2]{1,0,2:T(4,128)S(1)} all-gather(s32[4,128,2]{1,0,2:T(4,128)S(1)} %fusion.31), channel_id=1, replica_groups=mesh['layer'=4,'tok'=8] {'tok'}, dimensions={1}, use_global_device_ids=true | all-gather | bytes 36864 | tf_op jit(solution)/shard_map/all_gather | solution.py:64
  24.7 0.1 add_select_fusion.1
  25.0 0.1 iota_compare_fusion
  25.1 1.5 and_reduce_fusion
  26.7 1.9 reduce_or.12
  28.5 0.9 dynamic-slice_convert_fusion
  29.4 1.4 reshape.189
  30.9 3.6 %broadcast_and_fusion = pred[4,2,512,16,16]{2,1,4,3,0:T(4,128)(4,1)} fusion(pred[4,2,512,16,16]{2,1,4,3,0:T(4,128)(4,1)S(1)} %reduce_or.12, pred[4]{0:T(512)(128)(4,1)S(1)} %get-tuple-element.13), kind=kLoop, calls=%fused_computation.11 | loop fusion | flops 1048576 | bytes 2097156 | tf_op jit(solution)/shard_map/and | solution.py:98
  34.5 51.3 %all-gather.3.cloned.1.call-done = bf16[1,1024,3584]{2,1,0:T(8,128)(2,1)} async-done(((bf16[1,128,3584]{2,1,0:T(8,128)(2,1)}), bf16[1,1024,3584]{2,1,0:T(8,128)(2,1)}) %all-gather.3.cloned.1.call-update) | async-done | bytes 7340048 | tf_op jit(solution)/shard_map/all_gather | solution.py:79
  85.8 7.1 %convolution_convert_fusion.rows_ref = bf16[2,16,16,3584]{3,2,1,0:T(8,128)(2,1)} fusion(bf16[2,512,3584,1]{2,1,3,0:T(8,128)(2,1)} %bitcast.64, bf16[2,16,16,512]{3,0,2,1:T(2,128)(2,1)S(1)} %bitcast.58), kind=kOutput, calls=%fused_computation.10 | convolution fusion | flops 1880883200 | bytes 11534336 | tf_op jit(solution)/shard_map/gbxt,gtd->gbxd/dot_general | solution.py:83
  92.9 8.2 %shard_map.86 = bf16[16,32,128]{2,1,0:T(8,128)(2,1)} custom-call(bf16[2,16,16,3584]{3,2,1,0:T(8,128)(2,1)} %convolution_convert_fusion.rows_ref, bf16[3584,2048]{1,0:T(8,128)(2,1)} %bitcast.51, f32[1,2048]{1,0:T(1,128)} %b_ref.1), custom_call_target="tpu_custom_call" | custom-call | tf_op jit(solution)/shard_map/pallas_call | solution.py:25
  101.0 4.3 %collective-permute-start.2 = (bf16[16,32,128]{2,1,0:T(8,128)(2,1)}, bf16[16,32,128]{2,1,0:T(8,128)(2,1)S(1)}, u32[]{:S(2)}, u32[]{:S(2)}) collective-permute-start(bf16[16,32,128]{2,1,0:T(8,128)(2,1)} %shard_map.86), channel_id=1, source_target_pairs={{0,24},{1,25},{2,26},{3,27},{4,28},{5,29},{6,30},{7,31}} | collective-permute-start | bytes 393224 | tf_op jit(solution)/shard_map/ppermute | solution.py:91
  105.3 1.3 collective-permute-start.1
  106.6 2.7 %collective-permute-start = (bf16[16,32,128]{2,1,0:T(8,128)(2,1)}, bf16[16,32,128]{2,1,0:T(8,128)(2,1)S(1)}, u32[]{:S(2)}, u32[]{:S(2)}) collective-permute-start(bf16[16,32,128]{2,1,0:T(8,128)(2,1)} %shard_map.86), channel_id=1, source_target_pairs={{0,8},{8,16},{16,24},{1,9},{9,17},{17,25},{2,10},{10,18},{18,26},{... | collective-permute-start | bytes 393224 | tf_op jit(solution)/shard_map/ppermute | solution.py:91
  109.3 3.6 %collective-permute-done.1 = bf16[16,32,128]{2,1,0:T(8,128)(2,1)S(1)} collective-permute-done((bf16[16,32,128]{2,1,0:T(8,128)(2,1)}, bf16[16,32,128]{2,1,0:T(8,128)(2,1)S(1)}, u32[]{:S(2)}, u32[]{:S(2)}) %collective-permute-start.1) | collective-permute-done | bytes 131104 | tf_op jit(solution)/shard_map/ppermute | solution.py:91
  112.9 1.0 pad_maximum_fusion
  113.9 0.6 gather_fusion
  114.5 0.1 broadcast_select_fusion
  114.7 7.6 %fusion.13 = bf16[4,16,32,896]{3,2,1,0:T(8,128)(2,1)S(1)} fusion(bf16[4,16,32,128]{3,2,1,0:T(8,128)(2,1)S(1)} %broadcast_select_fusion, bf16[4,16,128,3584]{3,2,1,0:T(8,128)(2,1)} %bitcast.48), kind=kOutput, calls=%fused_computation.15 | convolution fusion | flops 471597056 | bytes 18874368 | tf_op jit(solution)/shard_map/lbxe,lbed->lbxd/dot_general | solution.py:106
  122.3 3.6 %bitcast_convert_fusion.1 = bf16[2,512,896]{2,1,0:T(8,128)(2,1)} fusion(bf16[4,16,2,16,896]{4,3,2,1,0:T(8,128)(2,1)S(1)} %bitcast.53, pred[4,2,512,16,16]{2,1,4,3,0:T(4,128)(4,1)S(1)} %copy-done), kind=kOutput, calls=%fused_computation.12 | convolution fusion | flops 1879965696 | bytes 6553600 | tf_op jit(solution)/shard_map/lgtbx,lbgxd->gtd/dot_general | solution.py:112
  126.0 21.1 %fusion.6 = bf16[4,16,32,2688]{3,2,1,0:T(8,128)(2,1)} fusion(bf16[4,16,32,128]{3,2,1,0:T(8,128)(2,1)S(1)} %broadcast_select_fusion, bf16[4,16,128,3584]{3,2,1,0:T(8,128)(2,1)} %bitcast.49), kind=kOutput, calls=%fused_computation.9 | convolution fusion | flops 1414791168 | bytes 55574528 | tf_op jit(solution)/shard_map/lbxe,lbed->lbxd/dot_general | solution.py:106
  147.1 12.1 %bitcast_convert_fusion = bf16[2,512,2688]{2,1,0:T(8,128)(2,1)} fusion(bf16[4,16,2,16,2688]{4,3,2,1,0:T(8,128)(2,1)} %bitcast.50, pred[4,2,512,16,16]{2,1,4,3,0:T(4,128)(4,1)S(1)} %copy-done), kind=kOutput, calls=%fused_computation.5 | convolution fusion | flops 5639897088 | bytes 17563648 | tf_op jit(solution)/shard_map/lgtbx,lbgxd->gtd/dot_general | solution.py:112
  159.3 0.7 copy-done.2
  160.0 62.7 %reduce-scatter.5.cloned.1.call-done = bf16[128,2688]{1,0:T(8,128)(2,1)} async-done(((bf16[1024,2688]{1,0:T(8,128)(2,1)}), bf16[128,2688]{1,0:T(8,128)(2,1)}) %reduce-scatter.5.cloned.1.call-update) | async-done | bytes 688144 | tf_op jit(solution)/shard_map/reduce_scatter | solution.py:119
  222.7 1.6 fusion.17
  224.3 0.5 multiply_bitcast_fusion
  224.8 2.2 add_convert_fusion
  (27 shorter events, 0.6 us)
Async XLA Ops:
  7.2 78.6 %all-gather.3.cloned.1.call-start = ((), (), s32[]{:S(2)}) async-start(), calls=%async_computation.4 | async-start | bytes 8257536 | tf_op jit(solution)/shard_map/all_gather | solution.py:79
  7.9 152.1 %reduce-scatter.3.cloned.1.call-start = ((), (), s32[]{:S(2)}) async-start(), calls=%async_computation.2 | async-start | bytes 2064384 | tf_op jit(solution)/shard_map/reduce_scatter | solution.py:119
  101.0 8.3 %collective-permute-start.2 = (bf16[16,32,128]{2,1,0:T(8,128)(2,1)}, bf16[16,32,128]{2,1,0:T(8,128)(2,1)S(1)}, u32[]{:S(2)}, u32[]{:S(2)}) collective-permute-start(bf16[16,32,128]{2,1,0:T(8,128)(2,1)} %shard_map.86), channel_id=1, source_target_pairs={{0,24},{1,25},{2,26},{3,27},{4,28},{5,29},{6,30},{7,31}} | collective-permute-start | bytes 393224 | tf_op jit(solution)/shard_map/ppermute | solution.py:91
  105.3 7.6 %collective-permute-start.1 = (bf16[16,32,128]{2,1,0:T(8,128)(2,1)}, bf16[16,32,128]{2,1,0:T(8,128)(2,1)S(1)}, u32[]{:S(2)}, u32[]{:S(2)}) collective-permute-start(bf16[16,32,128]{2,1,0:T(8,128)(2,1)} %shard_map.86), channel_id=1, source_target_pairs={{0,16},{8,24},{1,17},{9,25},{2,18},{10,26},{3,19},{11,27},{4,20},{... | collective-permute-start | bytes 393224 | tf_op jit(solution)/shard_map/ppermute | solution.py:91
  106.6 6.3 %collective-permute-start = (bf16[16,32,128]{2,1,0:T(8,128)(2,1)}, bf16[16,32,128]{2,1,0:T(8,128)(2,1)S(1)}, u32[]{:S(2)}, u32[]{:S(2)}) collective-permute-start(bf16[16,32,128]{2,1,0:T(8,128)(2,1)} %shard_map.86), channel_id=1, source_target_pairs={{0,8},{8,16},{16,24},{1,9},{9,17},{17,25},{2,10},{10,18},{18,26},{... | collective-permute-start | bytes 393224 | tf_op jit(solution)/shard_map/ppermute | solution.py:91
  114.6 7.6 %copy-start = (pred[4,2,512,16,16]{2,1,4,3,0:T(4,128)(4,1)S(1)}, pred[4,2,512,16,16]{2,1,4,3,0:T(4,128)(4,1)}, u32[]{:S(2)}) copy-start(pred[4,2,512,16,16]{2,1,4,3,0:T(4,128)(4,1)} %broadcast_and_fusion) | copy-start | bytes 3145732
  126.0 96.8 %reduce-scatter.5.cloned.1.call-start = ((), (), s32[]{:S(2)}) async-start(), calls=%async_computation.3 | async-start | bytes 6193152 | tf_op jit(solution)/shard_map/reduce_scatter | solution.py:119
  159.2 0.7 copy-start.2
  159.2 63.5 %copy-start.1 = (bf16[1,128,3584]{2,1,0:T(8,128)(2,1)S(1)}, bf16[1,128,3584]{2,1,0:T(8,128)(2,1)}, u32[]{:S(2)}) copy-start(bf16[1,128,3584]{2,1,0:T(8,128)(2,1)} %param.8) | copy-start | bytes 2752516
Sparse Core Ops, SparseCore 0:
  9.6 76.1 all-gather.2
  126.1 33.6 reduce-scatter.2
  162.1 60.5 reduce-scatter.4

commit v15 on v13

--- a/solution.py
+++ b/solution.py
@@ -87,12 +87,7 @@
         preferred_element_type=jnp.float32,
     ).astype(jnp.bfloat16)
     codes = encode(rows, encoder_weight[0], encoder_bias[0].reshape(1, -1))
-    received = [codes] + [
-        lax.ppermute(codes, "layer", [(i, i + shift) for i in range(layers - shift)])
-        for shift in range(1, layers)
-    ]
-    shifts = (layer_index - jnp.arange(layers, dtype=jnp.int32)) % layers
-    gathered = jnp.take(jnp.stack(received), shifts, axis=0)
+    gathered = lax.all_gather(codes, "layer", axis=0, tiled=False)
 
     valid = jnp.arange(layers, dtype=jnp.int32) <= layer_index
     combine = (hits & valid[:, None, None, None]).astype(jnp.bfloat16)

time: 233 us -> 230 us (0.987)
  blocking collectives: 14.4 us -> 25.6 us
  starting transfers between devices: 8.34 us -> 0.12 us
  waiting for transfers between devices: 119 us -> 115 us
    all_gather x0 -> x1, blocking collectives: none -> 11.2 us  [body(): gathered = lax.all_gather(codes, 'layer', axis=0, tiled=False)]
    ppermute x3 -> x0, starting transfers between devices: 8.22 us -> none  [body(): lax.ppermute(codes, 'layer', [(i, i + shift) for i in range(layers - shif...]
    ppermute x3 -> x0, waiting for transfers between devices: 3.57 us -> none  [body(): lax.ppermute(codes, 'layer', [(i, i + shift) for i in range(layers - shif...]
  transfers between devices with their start and end apart: 6 -> 3, of which waited for: 4 -> 3; matrix products, arithmetic and copies ran while one was open for 18% -> 19% of each run, Pallas kernels for 0% -> 0%
where the time goes in v15:
time: 230 us; the launch traced here: 229 us
  waiting for transfers between devices  115 us (50%)
  matrix products  49.8 us (22%)
  blocking collectives  25.6 us (11%)
  between operations  13.9 us (6%)
  other arithmetic  11.8 us (5%)
  Pallas kernels  8.17 us (4%)
  local copies, waits for them, and re-layouts  5.28 us (2%)
    reduce_scatter x2, waiting for transfers between devices, body(): lax.psum_scatter(partial, 'tok', scatter_dimension=0, tiled=True)  62.7 us
    all_gather x1, waiting for transfers between devices, body(): res_all = lax.all_gather(residual[0], 'tok', axis=0, tiled=True)  51.3 us
    dot_general x2, matrix products, body(): jnp.einsum('lbxe,lbed->lbxd', chunk_codes, weights[..., lo:hi], preferred...  27.6 us
    dot_general x2, matrix products, body(): jnp.einsum('lgtbx,lbgxd->gtd', combine, terms.reshape(layers, per_owner,...  15.2 us
    all_gather x1, blocking collectives, body(): codes_all = lax.all_gather(codes_own, 'tok', axis=1, tiled=True)  14.4 us
    all_gather x1, blocking collectives, body(): gathered = lax.all_gather(codes, 'layer', axis=0, tiled=False)  11.2 us
    pallas_call x1, Pallas kernels, encode(): pl.pallas_call(encode_kernel, grid=(per_owner // group,), in_specs=[pl.Bl...  8.17 us
    dot_general x1, matrix products, body(): jnp.einsum('gbxt,gtd->gbxd', own_hits, res_all.reshape(halves, tokens //...  7.06 us
  transfers between devices with their start and end apart: 3, of which 3 were waited for; matrix products, arithmetic and copies ran while one was open for 19% of the time, Pallas kernels for 0%

profile of v15, /device:TPU:0, one launch (start us, length us, event | category | flops | bytes accessed | tf_op | source)
XLA Modules:
  0.0 229.5 jit_solution(15539327259343554923)
XLA Ops:
  7.2 0.7 all-gather.4.cloned.1.call-update
  7.9 0.0 reduce-scatter.3.cloned.1.call-start
  7.9 0.8 copy.57
  8.8 0.1 copy.58
  8.9 0.4 convert_reduce_fusion
  9.3 0.1 copy.60
  9.5 0.1 copy.61
  9.5 0.7 fusion.31
  10.2 14.4 %all_gather.12 = s32[4,1024,2]{1,0,2:T(4,128)S(1)} all-gather(s32[4,128,2]{1,0,2:T(4,128)S(1)} %fusion.31), channel_id=1, replica_groups=mesh['layer'=4,'tok'=8] {'tok'}, dimensions={1}, use_global_device_ids=true | all-gather | bytes 36864 | tf_op jit(solution)/shard_map/all_gather | solution.py:64
  24.6 0.1 broadcast_bitcast_fusion
  24.7 0.1 add_select_fusion.1
  25.0 0.1 iota_compare_fusion
  25.1 1.5 and_reduce_fusion
  26.7 1.9 reduce_or.12
  28.5 0.9 dynamic-slice_convert_fusion
  29.4 1.4 reshape.135
  30.9 3.6 %broadcast_and_fusion = pred[4,2,512,16,16]{2,1,4,3,0:T(4,128)(4,1)} fusion(pred[4,2,512,16,16]{2,1,4,3,0:T(4,128)(4,1)S(1)} %reduce_or.12, pred[4]{0:T(512)(128)(4,1)S(1)} %iota_compare_fusion.3), kind=kLoop, calls=%fused_computation.13 | loop fusion | flops 1048576 | bytes 2097156 | tf_op jit(solution)/shard_map/and | solution.py:93
  34.5 51.3 %all-gather.4.cloned.1.call-done = bf16[1,1024,3584]{2,1,0:T(8,128)(2,1)} async-done(((bf16[1,128,3584]{2,1,0:T(8,128)(2,1)}), bf16[1,1024,3584]{2,1,0:T(8,128)(2,1)}) %all-gather.4.cloned.1.call-update) | async-done | bytes 7340048 | tf_op jit(solution)/shard_map/all_gather | solution.py:79
  85.8 7.1 %convolution_convert_fusion.rows_ref = bf16[2,16,16,3584]{3,2,1,0:T(8,128)(2,1)} fusion(bf16[2,512,3584,1]{2,1,3,0:T(8,128)(2,1)} %bitcast.57, bf16[2,16,16,512]{3,0,2,1:T(2,128)(2,1)S(1)} %bitcast.54), kind=kOutput, calls=%fused_computation.9 | convolution fusion | flops 1880883200 | bytes 11534336 | tf_op jit(solution)/shard_map/gbxt,gtd->gbxd/dot_general | solution.py:83
  92.9 8.2 %shard_map.86 = bf16[16,32,128]{2,1,0:T(8,128)(2,1)} custom-call(bf16[2,16,16,3584]{3,2,1,0:T(8,128)(2,1)} %convolution_convert_fusion.rows_ref, bf16[3584,2048]{1,0:T(8,128)(2,1)} %bitcast.46, f32[1,2048]{1,0:T(1,128)} %b_ref.1), custom_call_target="tpu_custom_call" | custom-call | tf_op jit(solution)/shard_map/pallas_call | solution.py:25
  101.0 11.2 %all-gather.1 = bf16[64,32,128]{2,1,0:T(8,128)(2,1)S(1)} all-gather(bf16[16,32,128]{2,1,0:T(8,128)(2,1)} %shard_map.86), channel_id=3, replica_groups=mesh['layer'=4,'tok'=8] {'layer'}, dimensions={0}, use_global_device_ids=true | all-gather | bytes 655360 | tf_op jit(solution)/shard_map/all_gather | solution.py:90
  112.3 8.2 %fusion.13 = bf16[4,16,32,1024]{3,2,1,0:T(8,128)(2,1)S(1)} fusion(bf16[4,16,32,128]{3,2,1,0:T(8,128)(2,1)S(1)} %bitcast.47, bf16[4,16,128,3584]{3,2,1,0:T(8,128)(2,1)} %bitcast.43), kind=kOutput, calls=%fused_computation.14 | convolution fusion | flops 538968064 | bytes 21495808 | tf_op jit(solution)/shard_map/lbxe,lbed->lbxd/dot_general | solution.py:101
  120.5 3.7 %bitcast_convert_fusion.1 = bf16[2,512,1024]{2,1,0:T(8,128)(2,1)} fusion(bf16[4,16,2,16,1024]{4,3,2,1,0:T(8,128)(2,1)S(1)} %bitcast.50, pred[4,2,512,16,16]{2,1,4,3,0:T(4,128)(4,1)S(1)} %copy-done), kind=kOutput, calls=%fused_computation.10 | convolution fusion | flops 2148532224 | bytes 7340032 | tf_op jit(solution)/shard_map/lgtbx,lbgxd->gtd/dot_general | solution.py:107
  124.3 0.0 reduce-scatter.5.cloned.1.call-start
  124.3 19.3 %fusion.6 = bf16[4,16,32,2560]{3,2,1,0:T(8,128)(2,1)} fusion(bf16[4,16,32,128]{3,2,1,0:T(8,128)(2,1)S(1)} %bitcast.48, bf16[4,16,128,3584]{3,2,1,0:T(8,128)(2,1)} %bitcast.44), kind=kOutput, calls=%fused_computation.8 | convolution fusion | flops 1347420160 | bytes 52953088 | tf_op jit(solution)/shard_map/lbxe,lbed->lbxd/dot_general | solution.py:101
  143.7 11.5 %bitcast_convert_fusion = bf16[2,512,2560]{2,1,0:T(8,128)(2,1)} fusion(bf16[4,16,2,16,2560]{4,3,2,1,0:T(8,128)(2,1)} %bitcast.45, pred[4,2,512,16,16]{2,1,4,3,0:T(4,128)(4,1)S(1)} %copy-done), kind=kOutput, calls=%fused_computation.4 | convolution fusion | flops 5371330560 | bytes 16777216 | tf_op jit(solution)/shard_map/lgtbx,lbgxd->gtd/dot_general | solution.py:107
  155.1 0.7 copy-done.2
  155.9 2.0 reduce-scatter.3.cloned.1.call-done
  157.8 60.8 %reduce-scatter.5.cloned.1.call-done = bf16[128,2560]{1,0:T(8,128)(2,1)} async-done(((bf16[1024,2560]{1,0:T(8,128)(2,1)}), bf16[128,2560]{1,0:T(8,128)(2,1)}) %reduce-scatter.5.cloned.1.call-update) | async-done | bytes 655376 | tf_op jit(solution)/shard_map/reduce_scatter | solution.py:114
  218.6 1.6 fusion.19
  220.2 0.5 multiply_bitcast_fusion
  220.7 2.2 add_convert_fusion
  (17 shorter events, 0.3 us)
Async XLA Ops:
  7.2 78.6 %all-gather.4.cloned.1.call-start = ((), (), s32[]{:S(2)}) async-start(), calls=%async_computation.4 | async-start | bytes 8257536 | tf_op jit(solution)/shard_map/all_gather | solution.py:79
  7.9 149.9 %reduce-scatter.3.cloned.1.call-start = ((), (), s32[]{:S(2)}) async-start(), calls=%async_computation.2 | async-start | bytes 2359296 | tf_op jit(solution)/shard_map/reduce_scatter | solution.py:114
  112.3 8.2 %copy-start = (pred[4,2,512,16,16]{2,1,4,3,0:T(4,128)(4,1)S(1)}, pred[4,2,512,16,16]{2,1,4,3,0:T(4,128)(4,1)}, u32[]{:S(2)}) copy-start(pred[4,2,512,16,16]{2,1,4,3,0:T(4,128)(4,1)} %broadcast_and_fusion) | copy-start | bytes 3145732
  124.3 94.3 %reduce-scatter.5.cloned.1.call-start = ((), (), s32[]{:S(2)}) async-start(), calls=%async_computation.3 | async-start | bytes 5898240 | tf_op jit(solution)/shard_map/reduce_scatter | solution.py:114
  155.1 0.7 copy-start.2
  155.1 63.5 %copy-start.1 = (bf16[1,128,3584]{2,1,0:T(8,128)(2,1)S(1)}, bf16[1,128,3584]{2,1,0:T(8,128)(2,1)}, u32[]{:S(2)}) copy-start(bf16[1,128,3584]{2,1,0:T(8,128)(2,1)} %param.8) | copy-start | bytes 2752516
Sparse Core Ops, SparseCore 0:
  9.6 76.1 all-gather.3
  124.4 33.4 reduce-scatter.2
  160.2 58.4 reduce-scatter.4
